TPU v7x, 128 devices: a whole 4x4x4 slice. The times are simulated.
128 devices in a mesh: dom: 32 (over y, x, core), band: 4 (over z).
Axes of the slice: x: 4, y: 4, z: 4, core: 2. Of those that a mesh axis runs over, the one named last changes fastest.
Arguments:
- states: bfloat16 [256, 393216], P('band', 'dom'), may hold values from -640 to 640
- cell_kinetic: bfloat16 [512, 512], replicated, may hold values from -0.3 to 0.3, as said below
- cell_scale: float32 [1024], P('dom'), may hold values from 0.5 to 2
- cell_potential: float32 [1024, 512], P('dom'), may hold values from -0.3 to 0.3
- connectivity: int32 [1024, 512], P('dom'), may hold values from 0 to 12287, as said below
- shared_nodes: int32 [32, 2, 1024], P('dom'), may hold values from 0 to 12287, as said below
- cell_counts: int32 [32], P('dom'), may hold values from 4 to 32, as said below
Outputs:
- rotated: bfloat16 [256, 393216], P('band', 'dom')
Inputs may be any that keep to these rules, and one draw needn't show every extreme that they name: cell_kinetic is symmetric. `connectivity`: row c of a domain (local cell number c) names each of the 512 nodes c * 3 * 128 to c * 3 * 128 + 511, counted round modulo 12288, exactly once. `shared_nodes`: the two rows of a domain name 2048 distinct nodes; position p of domain d's row 1 and of domain d+1's row 0 are the same physical node. `cell_counts`: in every draw some domain has all 32 cells live.
All inputs are finite; a program needn't handle non-finite values.
Results may differ from a plain program's by a relative error of at most 0.008.
Values may be sent and summed in bfloat16 or wider, within the bound.
No kernel may reach another device: no remote copies, remote signals or barrier semaphores. Data moves between devices by JAX's collectives and lax.ppermute only.
A program may use at most 128 MiB of HBM per device.

v0:
```python
import functools

import jax
import jax.numpy as jnp
from jax import lax
from jax.experimental import pallas as pl
from jax.experimental.pallas import tpu as pltpu
from jax.sharding import PartitionSpec as P

CHEB = 4
NS_ITERS = 5


VMEM_LIMIT = 60 * 1024 * 1024


def field_kernel(combine, older, apply, alpha, *refs):
    refs = list(refs)
    faces = refs.pop(0)
    if apply:
        scales = refs.pop(0)
    if combine:
        local_in = refs.pop(0)
        received = refs.pop(0)
        if older:
            older_ref = refs.pop(0)
    else:
        vector_in = refs.pop(0)
    if apply:
        ops_ref = refs.pop(0)
        pot_ref = refs.pop(0)
    if combine:
        vector_out = refs.pop(0)
    if apply:
        local_out = refs.pop(0)
        faces_out = refs.pop(0)
    if combine:
        work = refs.pop(0)
    vector = vector_out if combine else vector_in
    face_total = faces.shape[0]
    node_total = vector.shape[0]
    cell = pl.program_id(0) if apply else None

    def prologue():
        work[...] = local_in[...] if alpha == 1.0 else alpha * local_in[...]

        def fix(p, carry):
            n = faces[p]
            row = received[pl.ds(p, 1), :]
            work[pl.ds(n, 1), :] += row if alpha == 1.0 else alpha * row
            return carry

        lax.fori_loop(0, face_total, fix, 0, unroll=8)
        value = work[...]
        if older:
            value = value - older_ref[...].astype(jnp.float32)
        vector_out[...] = value.astype(vector_out.dtype)

    if combine:
        if apply:
            pl.when(cell == 0)(prologue)
        else:
            prologue()

    if apply:
        width = ops_ref.shape[1]
        quarter = width // 4
        body_rows = width - quarter

        @pl.when(cell == 0)
        def _():
            local_out[...] = jnp.zeros_like(local_out)

        start = pl.multiple_of(cell * body_rows, quarter)
        tail = pl.multiple_of(lax.rem((cell + 1) * body_rows, node_total), quarter)
        main_rows = vector[pl.ds(start, body_rows), :]
        tail_rows = vector[pl.ds(tail, quarter), :]
        ops = ops_ref[0]
        product = jnp.dot(ops[:, :body_rows], main_rows, preferred_element_type=jnp.float32)
        product = product + jnp.dot(ops[:, body_rows:], tail_rows, preferred_element_type=jnp.float32)
        scale = scales[cell]
        pot = pot_ref[0]
        top = product[:body_rows] * scale + pot[:body_rows] * main_rows.astype(jnp.float32)
        bottom = product[body_rows:] * scale + pot[body_rows:] * tail_rows.astype(jnp.float32)
        local_out[pl.ds(start, body_rows), :] += top
        local_out[pl.ds(tail, quarter), :] += bottom

        @pl.when(cell == pl.num_programs(0) - 1)
        def _():
            def pick(p, carry):
                n = faces[p]
                faces_out[pl.ds(p, 1), :] = local_out[pl.ds(n, 1), :]
                return carry

            lax.fori_loop(0, face_total, pick, 0, unroll=8)


def field_step(faces, scales, window_ops, window_pot, vector=None, local_in=None,
               received=None, older=None, alpha=1.0, apply=True):
    combine = local_in is not None
    has_older = older is not None
    node_total, cols = (local_in if combine else vector).shape
    face_total = faces.shape[0]
    cells, width, _ = window_ops.shape
    smem = pl.BlockSpec(memory_space=pltpu.SMEM)
    whole = pl.BlockSpec(memory_space=pltpu.VMEM)
    args, specs = [faces], [smem]
    if apply:
        args.append(scales); specs.append(smem)
    if combine:
        args += [local_in, received]; specs += [whole, whole]
        if has_older:
            args.append(older); specs.append(whole)
    else:
        args.append(vector); specs.append(whole)
    if apply:
        args += [window_ops, window_pot]
        specs += [pl.BlockSpec((1, width, width), lambda c: (c, 0, 0)),
                  pl.BlockSpec((1, width, cols), lambda c: (c, 0, 0))]
    out_shape, out_specs = [], []
    if combine:
        out_shape.append(jax.ShapeDtypeStruct((node_total, cols), jnp.bfloat16)); out_specs.append(whole)
    if apply:
        out_shape += [jax.ShapeDtypeStruct((node_total, cols), jnp.float32),
                      jax.ShapeDtypeStruct((face_total, cols), jnp.float32)]
        out_specs += [whole, whole]
    scratch = [pltpu.VMEM((node_total, cols), jnp.float32)] if combine else []
    flops = 2 * cells * width * width * cols if apply else 0
    result = pl.pallas_call(
        functools.partial(field_kernel, combine, has_older, apply, alpha),
        grid=(cells if apply else 1,),
        in_specs=specs,
        out_specs=out_specs,
        out_shape=out_shape,
        scratch_shapes=scratch,
        compiler_params=pltpu.CompilerParams(
            dimension_semantics=("arbitrary",), vmem_limit_bytes=VMEM_LIMIT),
        cost_estimate=pl.CostEstimate(
            flops=flops, transcendentals=0,
            bytes_accessed=(cells * width * width * 2 if apply else 0) + node_total * cols * 12),
    )(*args)
    return result


def operator_kernel(slot_ref, pot_ref, kinetic_ref, ops_ref, pot_out_ref):
    width = kinetic_ref.shape[0]
    cols = pot_out_ref.shape[2]
    slot_row = slot_ref[0]
    picks = (lax.broadcasted_iota(jnp.int32, (width, width), 0) == slot_row).astype(jnp.bfloat16)
    kinetic = kinetic_ref[...]
    columns = lax.dot_general(
        kinetic, picks, (((1,), (1,)), ((), ())), preferred_element_type=jnp.float32
    ).astype(jnp.bfloat16)
    ops_ref[0] = jnp.dot(picks, columns, preferred_element_type=jnp.float32).astype(ops_ref.dtype)
    pot_row = pot_ref[0]
    high = pot_row.astype(jnp.bfloat16)
    rest = pot_row - high.astype(jnp.float32)
    middle = rest.astype(jnp.bfloat16)
    low = (rest - middle.astype(jnp.float32)).astype(jnp.bfloat16)
    parts = jnp.concatenate(
        [high, middle, low, jnp.zeros((5, width), jnp.bfloat16)], axis=0
    )
    moved = lax.dot_general(
        parts, picks, (((1,), (1,)), ((), ())), preferred_element_type=jnp.float32
    )
    total = moved[0:1] + moved[1:2] + moved[2:3]
    column = jnp.transpose(jnp.broadcast_to(total, (8, width)))[:, 0:1]
    pot_out_ref[0] = jnp.broadcast_to(column, (width, cols))


def cell_operators(slots, potential, kinetic, cols):
    cells, width = slots.shape
    return pl.pallas_call(
        operator_kernel,
        grid=(cells,),
        in_specs=[
            pl.BlockSpec((1, 1, width), lambda c: (c, 0, 0)),
            pl.BlockSpec((1, 1, width), lambda c: (c, 0, 0)),
            pl.BlockSpec(memory_space=pltpu.VMEM),
        ],
        out_specs=[
            pl.BlockSpec((1, width, width), lambda c: (c, 0, 0)),
            pl.BlockSpec((1, width, cols), lambda c: (c, 0, 0)),
        ],
        out_shape=[
            jax.ShapeDtypeStruct((cells, width, width), jnp.bfloat16),
            jax.ShapeDtypeStruct((cells, width, cols), jnp.float32),
        ],
        compiler_params=pltpu.CompilerParams(dimension_semantics=("arbitrary",)),
        cost_estimate=pl.CostEstimate(
            flops=4 * cells * width * width * width, transcendentals=0,
            bytes_accessed=cells * width * (width * 2 + cols * 4 + 8)),
    )(slots.reshape(cells, 1, width), potential.reshape(cells, 1, width), kinetic)


def newton(gram_matrix):
    identity = jnp.eye(gram_matrix.shape[0], dtype=jnp.float32)
    frobenius = jnp.sqrt(jnp.sum(gram_matrix * gram_matrix))
    scaled = gram_matrix / frobenius
    inverse_root = identity
    for repeat in range(NS_ITERS):
        factor = 1.5 * identity - 0.5 * jnp.dot(
            inverse_root, scaled, precision=lax.Precision.HIGHEST
        )
        scaled = jnp.dot(scaled, factor, precision=lax.Precision.HIGHEST)
        inverse_root = jnp.dot(factor, inverse_root, precision=lax.Precision.HIGHEST)
    return inverse_root.astype(jnp.bfloat16)


def doubling_sum(value):
    band_size = lax.axis_size("band")
    count = lax.axis_size("dom") * band_size
    bits = list(range(count.bit_length() - 1))
    order = bits[2:3] + bits[0:2] + bits[3:]
    total = value
    for bit in order:
        mask = 1 << bit
        pairs = [(i, i ^ mask) for i in range(count)]
        total = total + lax.ppermute(total, ("dom", "band"), pairs)
    return total


def body(states, cell_kinetic, cell_scale, cell_potential, connectivity, shared_nodes, cell_counts):
    left_face = shared_nodes[0, 0]
    right_face = shared_nodes[0, 1]
    face_width = left_face.shape[0]
    faces = jnp.concatenate([left_face, right_face])
    live_count = cell_counts[0]
    domain = lax.axis_index("dom")
    domains = lax.axis_size("dom")
    node_total = states.shape[1]
    state_cols = states.shape[0]
    has_left = (domain > 0).astype(jnp.float32)
    has_right = (domain < domains - 1).astype(jnp.float32)
    multiplicity = (
        jnp.ones((node_total,), jnp.float32)
        .at[left_face]
        .add(has_left)
        .at[right_face]
        .add(has_right)
    )
    node_weight = (1.0 / multiplicity).astype(jnp.bfloat16)
    cells, width = connectivity.shape
    starts = jnp.arange(cells, dtype=jnp.int32) * (3 * (width // 4))
    slots = (connectivity - starts[:, None]) % node_total
    alive = (jnp.arange(cells) < live_count).astype(jnp.float32)
    scales = cell_scale * alive
    window_ops, window_pot = cell_operators(
        slots, cell_potential * alive[:, None], cell_kinetic, state_cols
    )
    up = [(i, i + 1) for i in range(domains - 1)]
    down = [(j, i) for i, j in up]

    def exchange(face_values):
        from_left = lax.ppermute(face_values[face_width:], "dom", up)
        from_right = lax.ppermute(face_values[:face_width], "dom", down)
        return jnp.concatenate([from_left, from_right], axis=0)

    step = functools.partial(field_step, faces, scales, window_ops, window_pot)
    first = states.T
    local_sum, face_values = step(vector=first)
    second, local_sum, face_values = step(local_in=local_sum, received=exchange(face_values))
    history = [first, second]
    for repeat in range(CHEB - 2):
        following, local_sum, face_values = step(
            local_in=local_sum, received=exchange(face_values), older=history[-2], alpha=2.0
        )
        history.append(following)
    (current,) = step(
        local_in=local_sum, received=exchange(face_values), older=history[-2], alpha=2.0,
        apply=False,
    )
    row_shard = lax.all_to_all(current, "band", split_axis=0, concat_axis=1, tiled=True)
    piece_nodes = row_shard.shape[0]
    weight_rows = lax.dynamic_slice_in_dim(
        node_weight, lax.axis_index("band") * piece_nodes, piece_nodes, 0
    )
    weighted = row_shard * weight_rows[:, None]
    partial_gram = lax.dot_general(
        weighted, row_shard, (((0,), (0,)), ((), ())), preferred_element_type=jnp.float32
    )
    gram_matrix = doubling_sum(partial_gram)
    mixing = newton(gram_matrix)
    rotated = lax.dot_general(
        row_shard, mixing, (((1,), (0,)), ((), ())), preferred_element_type=jnp.float32
    ).astype(jnp.bfloat16)
    back = lax.all_to_all(rotated, "band", split_axis=1, concat_axis=0, tiled=True)
    return back.T


def solution(mesh):
    in_specs = (
        P("band", "dom"),
        P(),
        P("dom"),
        P("dom", None),
        P("dom", None),
        P("dom", None, None),
        P("dom"),
    )
    out_specs = P("band", "dom")
    return jax.shard_map(body, mesh=mesh, in_specs=in_specs, out_specs=out_specs, check_vma=False)
```

profile of v0, /device:TPU:6, one launch (start us, length us, event | category | flops | bytes accessed | tf_op | source)
XLA Modules:
  0.0 388.7 jit_solution(12997843956166176654)
XLA Ops:
  4.7 4.1 %copy.10 = bf16[64,12288]{0,1:T(8,128)(2,1)} copy(bf16[64,12288]{1,0:T(8,128)(2,1)} %param.7) | data formatting | bytes 3145728 | tf_op args[0]
  9.9 39.2 %shard_map.73 = (bf16[32,512,512]{2,1,0:T(8,128)(2,1)}, f32[32,512,64]{2,1,0:T(8,128)}) custom-call(s32[32,1,512]{2,1,0:T(1,128)} %reshape.84.slot_ref, f32[32,1,512]{2,1,0:T(1,128)} %reshape.85.pot_ref, bf16[512,512]{1,0:T(8,128)(2,1)} %kinetic_ref.1), custom_call_target="tpu_custom_call" | custom-call | flops 17179869184 | bytes 21102592 | tf_op jit(solution)/shard_map/pallas_call | solution.py:173
  49.1 31.3 %shard_map.74 = (f32[12288,64]{1,0:T(8,128)}, f32[2048,64]{1,0:T(8,128)}) custom-call(s32[2048]{0:T(1024)} %pad_add_fusion.refs_0_, f32[32]{0:T(128)} %compare_select_fusion.2.refs_1_, bf16[12288,64]{1,0:T(8,128)(2,1)} %bitcast.52, bf16[32,512,512]{2,1,0:T(8,128)(2,1)} %get-tuple-element.17.refs_3_.refs_4_.refs_5_, ...), custom_call_target="tpu_custom_call" | custom-call | flops 1073741824 | bytes 26214400 | tf_op jit(solution)/shard_map/pallas_call | solution.py:129
  83.6 3.6 collective-permute-start.1
  87.3 4.9 %collective-permute-done = f32[1024,64]{1,0:T(8,128)S(1)} collective-permute-done((f32[1024,64]{1,0:T(8,128)S(1)}, f32[1024,64]{1,0:T(8,128)S(1)}, u32[]{:S(2)}, u32[]{:S(2)}) %collective-permute-start) | collective-permute-done | bytes 262176 | tf_op jit(solution)/shard_map/ppermute | solution.py:255
  95.0 39.9 %shard_map.75 = (bf16[12288,64]{1,0:T(8,128)(2,1)}, f32[12288,64]{1,0:T(8,128)}, f32[2048,64]{1,0:T(8,128)}) custom-call(s32[2048]{0:T(1024)} %pad_add_fusion.refs_0_, f32[32]{0:T(128)} %compare_select_fusion.2.refs_1_, f32[12288,64]{1,0:T(8,128)} %get-tuple-element.19.refs_2_, f32[2048,64]{1,0:T(8,128)} %pad_maximum_fusion.refs_3_, ...), custom_call_target="tpu_custom_call" | custom-call | flops 1073741824 | bytes 26214400 | tf_op jit(solution)/shard_map/pallas_call | solution.py:129
  136.2 5.8 %collective-permute-start.2 = (f32[1024,64]{1,0:T(8,128)S(1)}, f32[1024,64]{1,0:T(8,128)S(1)}, u32[]{:S(2)}, u32[]{:S(2)}) collective-permute-start(f32[1024,64]{1,0:T(8,128)S(1)} %get-tuple-element.35), channel_id=1, source_target_pairs={{0,4},{4,8},{8,12},{12,16},{16,20},{20,24},{24,28},{28,32},{32,36}... | collective-permute-start | bytes 786440 | tf_op jit(solution)/shard_map/ppermute | solution.py:255
  143.9 3.0 collective-permute-done.2
  146.9 3.7 collective-permute-done.3
  151.6 40.9 %shard_map.76 = (bf16[12288,64]{1,0:T(8,128)(2,1)}, f32[12288,64]{1,0:T(8,128)}, f32[2048,64]{1,0:T(8,128)}) custom-call(s32[2048]{0:T(1024)} %pad_add_fusion.refs_0_, f32[32]{0:T(128)} %compare_select_fusion.2.refs_1_, f32[12288,64]{1,0:T(8,128)} %get-tuple-element.21.refs_2_, f32[2048,64]{1,0:T(8,128)} %pad_maximum_fusion.1.refs_3_, ...), custom_call_target="tpu_custom_call" | custom-call | flops 1073741824 | bytes 26214400 | tf_op jit(solution)/shard_map/pallas_call | solution.py:129
  193.8 5.9 %collective-permute-start.4 = (f32[1024,64]{1,0:T(8,128)S(1)}, f32[1024,64]{1,0:T(8,128)S(1)}, u32[]{:S(2)}, u32[]{:S(2)}) collective-permute-start(f32[1024,64]{1,0:T(8,128)S(1)} %get-tuple-element.33), channel_id=1, source_target_pairs={{0,4},{4,8},{8,12},{12,16},{16,20},{20,24},{24,28},{28,32},{32,36}... | collective-permute-start | bytes 786440 | tf_op jit(solution)/shard_map/ppermute | solution.py:255
  201.7 2.8 collective-permute-done.4
  204.5 3.9 collective-permute-done.5
  209.4 40.8 %shard_map.77 = (bf16[12288,64]{1,0:T(8,128)(2,1)}, f32[12288,64]{1,0:T(8,128)}, f32[2048,64]{1,0:T(8,128)}) custom-call(s32[2048]{0:T(1024)} %pad_add_fusion.refs_0_, f32[32]{0:T(128)} %compare_select_fusion.2.refs_1_, f32[12288,64]{1,0:T(8,128)} %get-tuple-element.23.refs_2_, f32[2048,64]{1,0:T(8,128)} %pad_maximum_fusion.2.refs_3_, ...), custom_call_target="tpu_custom_call" | custom-call | flops 1073741824 | bytes 26214400 | tf_op jit(solution)/shard_map/pallas_call | solution.py:129
  251.4 5.9 %collective-permute-start.6 = (f32[1024,64]{1,0:T(8,128)S(1)}, f32[1024,64]{1,0:T(8,128)S(1)}, u32[]{:S(2)}, u32[]{:S(2)}) collective-permute-start(f32[1024,64]{1,0:T(8,128)S(1)} %get-tuple-element.31), channel_id=1, source_target_pairs={{0,4},{4,8},{8,12},{12,16},{16,20},{20,24},{24,28},{28,32},{32,36}... | collective-permute-start | bytes 786440 | tf_op jit(solution)/shard_map/ppermute | solution.py:255
  259.3 2.8 collective-permute-done.6
  262.1 3.9 collective-permute-done.7
  267.0 12.2 %shard_map.78 = bf16[12288,64]{1,0:T(8,128)(2,1)} custom-call(s32[2048]{0:T(1024)} %pad_add_fusion.refs_0_, f32[12288,64]{1,0:T(8,128)} %get-tuple-element.26.refs_1_, f32[2048,64]{1,0:T(8,128)} %pad_maximum_fusion.3.refs_2_, bf16[12288,64]{1,0:T(8,128)(2,1)} %get-tuple-element.28.refs_3_), custom_call_target="tpu_custom_call" | custom-call | bytes 9437184 | tf_op jit(solution)/shard_map/pallas_call | solution.py:129
  279.2 4.3 %copy.11 = bf16[4,3072,64]{1,2,0:T(8,128)(2,1)} copy(bf16[4,3072,64]{2,1,0:T(8,128)(2,1)} %bitcast.56) | data formatting | bytes 3145728 | tf_op jit(solution)/shard_map/all_to_all | solution.py:273
  283.5 5.4 %all-to-all-start = ((bf16[4,3072,64]{1,2,0:T(8,128)(2,1)}), bf16[4,3072,64]{1,2,0:T(8,128)(2,1)S(1)}, u32[]{:S(2)}, u32[]{:S(2)}) async-start(bf16[4,3072,64]{1,2,0:T(8,128)(2,1)} %copy.11), calls=%async_computation | async-start | bytes 3145728 | tf_op jit(solution)/shard_map/all_to_all | solution.py:273
  288.9 5.9 %scatter_custom_fusion = f32[12288]{0:T(1024)S(1)} fusion(s32[1024]{0:T(1024)S(1)} %bitcast.63, f32[1024]{0:T(1024)S(1)} %broadcast.71, f32[]{:T(128)} %constant.11.clone.1), kind=kCustom, calls=%fused_computation.27 | custom fusion | flops 1024 | bytes 49156 | tf_op jit(solution)/shard_map/scatter-add | solution.py:238
  294.9 6.2 %scatter_fusion = f32[12288]{0:T(1024)S(1)} fusion(f32[12288]{0:T(1024)S(1)} %scatter_custom_fusion, s32[1024]{0:T(1024)S(1)} %bitcast.60, f32[1024]{0:T(1024)S(1)} %broadcast.72), kind=kCustom, calls=%fused_computation.1 | custom fusion | flops 1024 | bytes 16384 | tf_op jit(solution)/shard_map/scatter-add | solution.py:240
  301.2 7.1 %all-to-all-done = bf16[4,3072,64]{1,2,0:T(8,128)(2,1)S(1)} async-done(((bf16[4,3072,64]{1,2,0:T(8,128)(2,1)}), bf16[4,3072,64]{1,2,0:T(8,128)(2,1)S(1)}, u32[]{:S(2)}, u32[]{:S(2)}) %all-to-all-start) | async-done | bytes 1572896 | tf_op jit(solution)/shard_map/all_to_all | solution.py:273
  309.0 2.7 collective-permute-start.8
  313.5 8.0 %collective-permute-done.9 = f32[256,256]{1,0:T(8,128)S(1)} collective-permute-done((f32[256,256]{1,0:T(8,128)S(1)}, f32[256,256]{1,0:T(8,128)S(1)}, u32[]{:S(2)}, u32[]{:S(2)}) %collective-permute-start.9) | collective-permute-done | bytes 262176 | tf_op jit(solution)/shard_map/ppermute | solution.py:219
  322.5 8.3 %collective-permute-done.10 = f32[256,256]{1,0:T(8,128)S(1)} collective-permute-done((f32[256,256]{1,0:T(8,128)S(1)}, f32[256,256]{1,0:T(8,128)S(1)}, u32[]{:S(2)}, u32[]{:S(2)}) %collective-permute-start.10) | collective-permute-done | bytes 262176 | tf_op jit(solution)/shard_map/ppermute | solution.py:219
  331.0 7.5 %collective-permute-done.11 = f32[256,256]{1,0:T(8,128)S(1)} collective-permute-done((f32[256,256]{1,0:T(8,128)S(1)}, f32[256,256]{1,0:T(8,128)S(1)}, u32[]{:S(2)}, u32[]{:S(2)}) %collective-permute-start.11) | collective-permute-done | bytes 262176 | tf_op jit(solution)/shard_map/ppermute | solution.py:219
  338.7 7.9 %collective-permute-done.12 = f32[256,256]{1,0:T(8,128)S(1)} collective-permute-done((f32[256,256]{1,0:T(8,128)S(1)}, f32[256,256]{1,0:T(8,128)S(1)}, u32[]{:S(2)}, u32[]{:S(2)}) %collective-permute-start.12) | collective-permute-done | bytes 262176 | tf_op jit(solution)/shard_map/ppermute | solution.py:219
  348.2 6.7 %collective-permute-done.13 = f32[256,256]{1,0:T(8,128)S(1)} collective-permute-done((f32[256,256]{1,0:T(8,128)S(1)}, f32[256,256]{1,0:T(8,128)S(1)}, u32[]{:S(2)}, u32[]{:S(2)}) %collective-permute-start.13) | collective-permute-done | bytes 262176 | tf_op jit(solution)/shard_map/ppermute | solution.py:219
  354.9 2.7 collective-permute-start.14
  357.7 5.2 %collective-permute-done.14 = f32[256,256]{1,0:T(8,128)S(1)} collective-permute-done((f32[256,256]{1,0:T(8,128)S(1)}, f32[256,256]{1,0:T(8,128)S(1)}, u32[]{:S(2)}, u32[]{:S(2)}) %collective-permute-start.14) | collective-permute-done | bytes 262176 | tf_op jit(solution)/shard_map/ppermute | solution.py:219
  370.2 17.2 %all_to_all.38 = bf16[3072,4,64]{0,2,1:T(8,128)(2,1)S(1)} all-to-all(bf16[3072,4,64]{0,2,1:T(8,128)(2,1)S(1)} %bitcast.57), channel_id=1, replica_groups=mesh['dom'=32,'band'=4] {'band'}, dimensions={1} | all-to-all | bytes 3145728 | tf_op jit(solution)/shard_map/all_to_all | solution.py:287
  (61 shorter events, 37.1 us)
Async XLA Ops:
  4.7 4.7 %copy-start.1 = (f32[32]{0:T(128)S(1)}, f32[32]{0:T(128)}, u32[]{:S(2)}) copy-start(f32[32]{0:T(128)} %param.9) | copy-start | bytes 388
  81.7 10.5 %collective-permute-start = (f32[1024,64]{1,0:T(8,128)S(1)}, f32[1024,64]{1,0:T(8,128)S(1)}, u32[]{:S(2)}, u32[]{:S(2)}) collective-permute-start(f32[1024,64]{1,0:T(8,128)S(1)} %get-tuple-element.37), channel_id=1, source_target_pairs={{0,4},{4,8},{8,12},{12,16},{16,20},{20,24},{24,28},{28,32},{32,36}... | collective-permute-start | bytes 786440 | tf_op jit(solution)/shard_map/ppermute | solution.py:255
  83.6 10.3 %collective-permute-start.1 = (f32[1024,64]{1,0:T(8,128)S(1)}, f32[1024,64]{1,0:T(8,128)S(1)}, u32[]{:S(2)}, u32[]{:S(2)}) collective-permute-start(f32[1024,64]{1,0:T(8,128)S(1)} %get-tuple-element.38), channel_id=1, source_target_pairs={{4,0},{8,4},{12,8},{16,12},{20,16},{24,20},{28,24},{32,28},{36,32}... | collective-permute-start | bytes 786440 | tf_op jit(solution)/shard_map/ppermute | solution.py:256
  136.2 10.7 %collective-permute-start.2 = (f32[1024,64]{1,0:T(8,128)S(1)}, f32[1024,64]{1,0:T(8,128)S(1)}, u32[]{:S(2)}, u32[]{:S(2)}) collective-permute-start(f32[1024,64]{1,0:T(8,128)S(1)} %get-tuple-element.35), channel_id=1, source_target_pairs={{0,4},{4,8},{8,12},{12,16},{16,20},{20,24},{24,28},{28,32},{32,36}... | collective-permute-start | bytes 786440 | tf_op jit(solution)/shard_map/ppermute | solution.py:255
  142.0 8.6 %collective-permute-start.3 = (f32[1024,64]{1,0:T(8,128)S(1)}, f32[1024,64]{1,0:T(8,128)S(1)}, u32[]{:S(2)}, u32[]{:S(2)}) collective-permute-start(f32[1024,64]{1,0:T(8,128)S(1)} %get-tuple-element.36), channel_id=1, source_target_pairs={{4,0},{8,4},{12,8},{16,12},{20,16},{24,20},{28,24},{32,28},{36,32}... | collective-permute-start | bytes 786440 | tf_op jit(solution)/shard_map/ppermute | solution.py:256
  193.8 10.7 %collective-permute-start.4 = (f32[1024,64]{1,0:T(8,128)S(1)}, f32[1024,64]{1,0:T(8,128)S(1)}, u32[]{:S(2)}, u32[]{:S(2)}) collective-permute-start(f32[1024,64]{1,0:T(8,128)S(1)} %get-tuple-element.33), channel_id=1, source_target_pairs={{0,4},{4,8},{8,12},{12,16},{16,20},{20,24},{24,28},{28,32},{32,36}... | collective-permute-start | bytes 786440 | tf_op jit(solution)/shard_map/ppermute | solution.py:255
  199.7 8.6 %collective-permute-start.5 = (f32[1024,64]{1,0:T(8,128)S(1)}, f32[1024,64]{1,0:T(8,128)S(1)}, u32[]{:S(2)}, u32[]{:S(2)}) collective-permute-start(f32[1024,64]{1,0:T(8,128)S(1)} %get-tuple-element.34), channel_id=1, source_target_pairs={{4,0},{8,4},{12,8},{16,12},{20,16},{24,20},{28,24},{32,28},{36,32}... | collective-permute-start | bytes 786440 | tf_op jit(solution)/shard_map/ppermute | solution.py:256
  251.4 10.7 %collective-permute-start.6 = (f32[1024,64]{1,0:T(8,128)S(1)}, f32[1024,64]{1,0:T(8,128)S(1)}, u32[]{:S(2)}, u32[]{:S(2)}) collective-permute-start(f32[1024,64]{1,0:T(8,128)S(1)} %get-tuple-element.31), channel_id=1, source_target_pairs={{0,4},{4,8},{8,12},{12,16},{16,20},{20,24},{24,28},{28,32},{32,36}... | collective-permute-start | bytes 786440 | tf_op jit(solution)/shard_map/ppermute | solution.py:255
  257.3 8.6 %collective-permute-start.7 = (f32[1024,64]{1,0:T(8,128)S(1)}, f32[1024,64]{1,0:T(8,128)S(1)}, u32[]{:S(2)}, u32[]{:S(2)}) collective-permute-start(f32[1024,64]{1,0:T(8,128)S(1)} %get-tuple-element.32), channel_id=1, source_target_pairs={{4,0},{8,4},{12,8},{16,12},{20,16},{24,20},{28,24},{32,28},{36,32}... | collective-permute-start | bytes 786440 | tf_op jit(solution)/shard_map/ppermute | solution.py:256
  283.5 5.4 %copy-start = (s32[1,2,1024]{2,1,0:T(2,128)S(1)}, s32[1,2,1024]{2,1,0:T(2,128)}, u32[]{:S(2)}) copy-start(s32[1,2,1024]{2,1,0:T(2,128)} %param.12) | copy-start | bytes 24580
  283.5 24.8 %all-to-all-start = ((bf16[4,3072,64]{1,2,0:T(8,128)(2,1)}), bf16[4,3072,64]{1,2,0:T(8,128)(2,1)S(1)}, u32[]{:S(2)}, u32[]{:S(2)}) async-start(bf16[4,3072,64]{1,2,0:T(8,128)(2,1)} %copy.11), calls=%async_computation | async-start | bytes 3145728 | tf_op jit(solution)/shard_map/all_to_all | solution.py:273
  309.0 3.8 collective-permute-start.8
  312.9 8.7 %collective-permute-start.9 = (f32[256,256]{1,0:T(8,128)S(1)}, f32[256,256]{1,0:T(8,128)S(1)}, u32[]{:S(2)}, u32[]{:S(2)}) collective-permute-start(f32[256,256]{1,0:T(8,128)S(1)} %add.58), channel_id=1, source_target_pairs={{0,1},{1,0},{2,3},{3,2},{4,5},{5,4},{6,7},{7,6},{8,9},{9,8},{10,11... | collective-permute-start | bytes 786440 | tf_op jit(solution)/shard_map/ppermute | solution.py:219
  321.6 9.3 %collective-permute-start.10 = (f32[256,256]{1,0:T(8,128)S(1)}, f32[256,256]{1,0:T(8,128)S(1)}, u32[]{:S(2)}, u32[]{:S(2)}) collective-permute-start(f32[256,256]{1,0:T(8,128)S(1)} %add.59), channel_id=1, source_target_pairs={{0,2},{1,3},{2,0},{3,1},{4,6},{5,7},{6,4},{7,5},{8,10},{9,11},{10,... | collective-permute-start | bytes 786440 | tf_op jit(solution)/shard_map/ppermute | solution.py:219
  330.9 7.6 %collective-permute-start.11 = (f32[256,256]{1,0:T(8,128)S(1)}, f32[256,256]{1,0:T(8,128)S(1)}, u32[]{:S(2)}, u32[]{:S(2)}) collective-permute-start(f32[256,256]{1,0:T(8,128)S(1)} %add.60), channel_id=1, source_target_pairs={{0,8},{1,9},{2,10},{3,11},{4,12},{5,13},{6,14},{7,15},{8,0},{9,1},... | collective-permute-start | bytes 786440 | tf_op jit(solution)/shard_map/ppermute | solution.py:219
  338.6 8.0 %collective-permute-start.12 = (f32[256,256]{1,0:T(8,128)S(1)}, f32[256,256]{1,0:T(8,128)S(1)}, u32[]{:S(2)}, u32[]{:S(2)}) collective-permute-start(f32[256,256]{1,0:T(8,128)S(1)} %add.61), channel_id=1, source_target_pairs={{0,16},{1,17},{2,18},{3,19},{4,20},{5,21},{6,22},{7,23},{8,24},{9,... | collective-permute-start | bytes 786440 | tf_op jit(solution)/shard_map/ppermute | solution.py:219
  346.6 8.3 %collective-permute-start.13 = (f32[256,256]{1,0:T(8,128)S(1)}, f32[256,256]{1,0:T(8,128)S(1)}, u32[]{:S(2)}, u32[]{:S(2)}) collective-permute-start(f32[256,256]{1,0:T(8,128)S(1)} %add.62), channel_id=1, source_target_pairs={{0,32},{1,33},{2,34},{3,35},{4,36},{5,37},{6,38},{7,39},{8,40},{9,... | collective-permute-start | bytes 786440 | tf_op jit(solution)/shard_map/ppermute | solution.py:219
  354.9 8.0 %collective-permute-start.14 = (f32[256,256]{1,0:T(8,128)S(1)}, f32[256,256]{1,0:T(8,128)S(1)}, u32[]{:S(2)}, u32[]{:S(2)}) collective-permute-start(f32[256,256]{1,0:T(8,128)S(1)} %add.63), channel_id=1, source_target_pairs={{0,64},{1,65},{2,66},{3,67},{4,68},{5,69},{6,70},{7,71},{8,72},{9,... | collective-permute-start | bytes 786440 | tf_op jit(solution)/shard_map/ppermute | solution.py:219
where the time goes:
time: 391 us; the launch traced here: 389 us
  Pallas kernels  204 us (52%)
  waiting for transfers between devices  78.6 us (20%)
  starting transfers between devices  43.2 us (11%)
  other arithmetic  20.3 us (5%)
  blocking collectives  17.2 us (4%)
  local copies, waits for them, and re-layouts  16.9 us (4%)
  matrix products  6.39 us (2%)
    pallas_call x5, Pallas kernels, field_step(): pl.pallas_call(functools.partial(field_kernel, combine, has_older, apply,...  165 us
    ppermute x7, waiting for transfers between devices, doubling_sum(): total = total + lax.ppermute(total, ('dom', 'band'), pairs)  44.8 us
    pallas_call x1, Pallas kernels, cell_operators(): pl.pallas_call(operator_kernel, grid=(cells,), in_specs=[pl.BlockSpec((1,...  39.2 us
    ppermute x4, starting transfers between devices, exchange(): from_left = lax.ppermute(face_values[face_width:], 'dom', up)  19.5 us
    all_to_all x1, blocking collectives, body(): lax.all_to_all(rotated, 'band', split_axis=1, concat_axis=0, tiled=True)  17.2 us
    ppermute x4, waiting for transfers between devices, exchange(): from_left = lax.ppermute(face_values[face_width:], 'dom', up)  13.5 us
    ppermute x4, waiting for transfers between devices, exchange(): from_right = lax.ppermute(face_values[:face_width], 'dom', down)  13.2 us
    scatter-add x2, other arithmetic, body(): multiplicity = jnp.ones((node_total,), jnp.float32).at[left_face].add(has...  12.2 us
  transfers between devices with their start and end apart: 16, of which 16 were waited for; matrix products, arithmetic and copies ran while one was open for 3% of the time, Pallas kernels for 0%

commit v1 on v0

--- a/solution.py
+++ b/solution.py
@@ -146,12 +146,11 @@
     width = kinetic_ref.shape[0]
     cols = pot_out_ref.shape[2]
     slot_row = slot_ref[0]
-    picks = (lax.broadcasted_iota(jnp.int32, (width, width), 0) == slot_row).astype(jnp.bfloat16)
-    kinetic = kinetic_ref[...]
-    columns = lax.dot_general(
-        kinetic, picks, (((1,), (1,)), ((), ())), preferred_element_type=jnp.float32
-    ).astype(jnp.bfloat16)
-    ops_ref[0] = jnp.dot(picks, columns, preferred_element_type=jnp.float32).astype(ops_ref.dtype)
+    slot_column = jnp.transpose(jnp.broadcast_to(slot_row, (8, width)))[:, 0:1]
+    picks = (lax.broadcasted_iota(jnp.int32, (width, width), 1) == slot_column).astype(jnp.bfloat16)
+    picks_t = (lax.broadcasted_iota(jnp.int32, (width, width), 0) == slot_row).astype(jnp.bfloat16)
+    columns = jnp.dot(kinetic_ref[...], picks, preferred_element_type=jnp.float32).astype(jnp.bfloat16)
+    ops_ref[0] = jnp.dot(picks_t, columns, preferred_element_type=jnp.float32).astype(ops_ref.dtype)
     pot_row = pot_ref[0]
     high = pot_row.astype(jnp.bfloat16)
     rest = pot_row - high.astype(jnp.float32)
@@ -160,9 +159,7 @@
     parts = jnp.concatenate(
         [high, middle, low, jnp.zeros((5, width), jnp.bfloat16)], axis=0
     )
-    moved = lax.dot_general(
-        parts, picks, (((1,), (1,)), ((), ())), preferred_element_type=jnp.float32
-    )
+    moved = jnp.dot(parts, picks, preferred_element_type=jnp.float32)
     total = moved[0:1] + moved[1:2] + moved[2:3]
     column = jnp.transpose(jnp.broadcast_to(total, (8, width)))[:, 0:1]
     pot_out_ref[0] = jnp.broadcast_to(column, (width, cols))
@@ -232,14 +229,15 @@
     state_cols = states.shape[0]
     has_left = (domain > 0).astype(jnp.float32)
     has_right = (domain < domains - 1).astype(jnp.float32)
-    multiplicity = (
+    face_counts = jnp.concatenate(
+        [jnp.full((face_width,), has_left), jnp.full((face_width,), has_right)]
+    )
+    node_weight = (
         jnp.ones((node_total,), jnp.float32)
-        .at[left_face]
-        .add(has_left)
-        .at[right_face]
-        .add(has_right)
-    )
-    node_weight = (1.0 / multiplicity).astype(jnp.bfloat16)
+        .at[faces]
+        .set(1.0 / (1.0 + face_counts), unique_indices=True)
+        .astype(jnp.bfloat16)
+    )
     cells, width = connectivity.shape
     starts = jnp.arange(cells, dtype=jnp.int32) * (3 * (width // 4))
     slots = (connectivity - starts[:, None]) % node_total

time: 391 us -> 397 us (1.015)
  other arithmetic: 20.3 us -> 8.13 us
  local copies, waits for them, and re-layouts: 16.9 us -> 25.1 us
  Pallas kernels: 204 us -> 210 us
    scatter-add x2 -> x0, other arithmetic: 12.2 us -> none  [body(): multiplicity = jnp.ones((node_total,), jnp.float32).at[left_face].add(has...]
    scatter x0 -> x1, local copies, waits for them, and re-layouts: none -> 8.25 us  [body(): node_weight = jnp.ones((node_total,), jnp.float32).at[faces].set(1.0 / (1...]
    pallas_call x1, Pallas kernels: 39.2 us -> 44.9 us  [cell_operators(): pl.pallas_call(operator_kernel, grid=(cells,), in_specs=[pl.BlockSpec((1,...]
  transfers between devices with their start and end apart: 16 -> 16, of which waited for: 16 -> 16; matrix products, arithmetic and copies ran while one was open for 3% -> 2% of each run, Pallas kernels for 0% -> 0%
where the time goes in v1:
time: 397 us; the launch traced here: 394 us
  Pallas kernels  210 us (53%)
  waiting for transfers between devices  82.5 us (21%)
  starting transfers between devices  43.1 us (11%)
  local copies, waits for them, and re-layouts  25.1 us (6%)
  blocking collectives  17.2 us (4%)
  other arithmetic  8.13 us (2%)
  matrix products  6.39 us (2%)
    pallas_call x5, Pallas kernels, field_step(): pl.pallas_call(functools.partial(field_kernel, combine, has_older, apply,...  165 us
    pallas_call x1, Pallas kernels, cell_operators(): pl.pallas_call(operator_kernel, grid=(cells,), in_specs=[pl.BlockSpec((1,...  44.9 us
    ppermute x7, waiting for transfers between devices, doubling_sum(): total = total + lax.ppermute(total, ('dom', 'band'), pairs)  44.8 us
    ppermute x4, starting transfers between devices, exchange(): from_left = lax.ppermute(face_values[face_width:], 'dom', up)  19.6 us
    all_to_all x1, blocking collectives, body(): lax.all_to_all(rotated, 'band', split_axis=1, concat_axis=0, tiled=True)  17.2 us
    ppermute x4, waiting for transfers between devices, exchange(): from_left = lax.ppermute(face_values[face_width:], 'dom', up)  13.5 us
    ppermute x4, waiting for transfers between devices, exchange(): from_right = lax.ppermute(face_values[:face_width], 'dom', down)  13.2 us
    all_to_all x1, waiting for transfers between devices, body(): lax.all_to_all(current, 'band', split_axis=0, concat_axis=1, tiled=True)  11.1 us
  transfers between devices with their start and end apart: 16, of which 16 were waited for; matrix products, arithmetic and copies ran while one was open for 2% of the time, Pallas kernels for 0%

profile of v1, /device:TPU:6, one launch (start us, length us, event | category | flops | bytes accessed | tf_op | source)
XLA Modules:
  0.0 394.2 jit_solution(16212859263993911265)
XLA Ops:
  4.7 4.1 %copy.10 = bf16[64,12288]{0,1:T(8,128)(2,1)} copy(bf16[64,12288]{1,0:T(8,128)(2,1)} %param.7) | data formatting | bytes 3145728 | tf_op args[0]
  9.9 44.9 %shard_map.73 = (bf16[32,512,512]{2,1,0:T(8,128)(2,1)}, f32[32,512,64]{2,1,0:T(8,128)}) custom-call(s32[32,1,512]{2,1,0:T(1,128)} %reshape.113.slot_ref, f32[32,1,512]{2,1,0:T(1,128)} %reshape.114.pot_ref, bf16[512,512]{1,0:T(8,128)(2,1)} %kinetic_ref.1), custom_call_target="tpu_custom_call" | custom-call | flops 17179869184 | bytes 21102592 | tf_op jit(solution)/shard_map/pallas_call | solution.py:170
  54.8 31.3 %shard_map.74 = (f32[12288,64]{1,0:T(8,128)}, f32[2048,64]{1,0:T(8,128)}) custom-call(s32[2048]{0:T(1024)} %pad_add_fusion.refs_0_, f32[32]{0:T(128)} %compare_select_fusion.1.refs_1_, bf16[12288,64]{1,0:T(8,128)(2,1)} %bitcast.52, bf16[32,512,512]{2,1,0:T(8,128)(2,1)} %get-tuple-element.17.refs_3_.refs_4_.refs_5_, ...), custom_call_target="tpu_custom_call" | custom-call | flops 1073741824 | bytes 26214400 | tf_op jit(solution)/shard_map/pallas_call | solution.py:129
  89.3 3.6 collective-permute-start.1
  93.0 4.9 %collective-permute-done = f32[1024,64]{1,0:T(8,128)S(1)} collective-permute-done((f32[1024,64]{1,0:T(8,128)S(1)}, f32[1024,64]{1,0:T(8,128)S(1)}, u32[]{:S(2)}, u32[]{:S(2)}) %collective-permute-start) | collective-permute-done | bytes 262176 | tf_op jit(solution)/shard_map/ppermute | solution.py:253
  100.7 39.9 %shard_map.75 = (bf16[12288,64]{1,0:T(8,128)(2,1)}, f32[12288,64]{1,0:T(8,128)}, f32[2048,64]{1,0:T(8,128)}) custom-call(s32[2048]{0:T(1024)} %pad_add_fusion.refs_0_, f32[32]{0:T(128)} %compare_select_fusion.1.refs_1_, f32[12288,64]{1,0:T(8,128)} %get-tuple-element.19.refs_2_, f32[2048,64]{1,0:T(8,128)} %pad_maximum_fusion.refs_3_, ...), custom_call_target="tpu_custom_call" | custom-call | flops 1073741824 | bytes 26214400 | tf_op jit(solution)/shard_map/pallas_call | solution.py:129
  141.9 5.8 %collective-permute-start.2 = (f32[1024,64]{1,0:T(8,128)S(1)}, f32[1024,64]{1,0:T(8,128)S(1)}, u32[]{:S(2)}, u32[]{:S(2)}) collective-permute-start(f32[1024,64]{1,0:T(8,128)S(1)} %get-tuple-element.35), channel_id=1, source_target_pairs={{0,4},{4,8},{8,12},{12,16},{16,20},{20,24},{24,28},{28,32},{32,36}... | collective-permute-start | bytes 786440 | tf_op jit(solution)/shard_map/ppermute | solution.py:253
  149.6 3.0 collective-permute-done.2
  152.5 3.7 collective-permute-done.3
  157.3 40.9 %shard_map.76 = (bf16[12288,64]{1,0:T(8,128)(2,1)}, f32[12288,64]{1,0:T(8,128)}, f32[2048,64]{1,0:T(8,128)}) custom-call(s32[2048]{0:T(1024)} %pad_add_fusion.refs_0_, f32[32]{0:T(128)} %compare_select_fusion.1.refs_1_, f32[12288,64]{1,0:T(8,128)} %get-tuple-element.21.refs_2_, f32[2048,64]{1,0:T(8,128)} %pad_maximum_fusion.1.refs_3_, ...), custom_call_target="tpu_custom_call" | custom-call | flops 1073741824 | bytes 26214400 | tf_op jit(solution)/shard_map/pallas_call | solution.py:129
  199.5 5.9 %collective-permute-start.4 = (f32[1024,64]{1,0:T(8,128)S(1)}, f32[1024,64]{1,0:T(8,128)S(1)}, u32[]{:S(2)}, u32[]{:S(2)}) collective-permute-start(f32[1024,64]{1,0:T(8,128)S(1)} %get-tuple-element.33), channel_id=1, source_target_pairs={{0,4},{4,8},{8,12},{12,16},{16,20},{20,24},{24,28},{28,32},{32,36}... | collective-permute-start | bytes 786440 | tf_op jit(solution)/shard_map/ppermute | solution.py:253
  205.4 1.9 collective-permute-start.5
  207.3 2.8 collective-permute-done.4
  210.2 3.9 collective-permute-done.5
  215.1 40.7 %shard_map.77 = (bf16[12288,64]{1,0:T(8,128)(2,1)}, f32[12288,64]{1,0:T(8,128)}, f32[2048,64]{1,0:T(8,128)}) custom-call(s32[2048]{0:T(1024)} %pad_add_fusion.refs_0_, f32[32]{0:T(128)} %compare_select_fusion.1.refs_1_, f32[12288,64]{1,0:T(8,128)} %get-tuple-element.23.refs_2_, f32[2048,64]{1,0:T(8,128)} %pad_maximum_fusion.2.refs_3_, ...), custom_call_target="tpu_custom_call" | custom-call | flops 1073741824 | bytes 26214400 | tf_op jit(solution)/shard_map/pallas_call | solution.py:129
  257.1 5.9 %collective-permute-start.6 = (f32[1024,64]{1,0:T(8,128)S(1)}, f32[1024,64]{1,0:T(8,128)S(1)}, u32[]{:S(2)}, u32[]{:S(2)}) collective-permute-start(f32[1024,64]{1,0:T(8,128)S(1)} %get-tuple-element.31), channel_id=1, source_target_pairs={{0,4},{4,8},{8,12},{12,16},{16,20},{20,24},{24,28},{28,32},{32,36}... | collective-permute-start | bytes 786440 | tf_op jit(solution)/shard_map/ppermute | solution.py:253
  264.9 2.8 collective-permute-done.6
  267.7 3.9 collective-permute-done.7
  272.6 12.2 %shard_map.78 = bf16[12288,64]{1,0:T(8,128)(2,1)} custom-call(s32[2048]{0:T(1024)} %pad_add_fusion.refs_0_, f32[12288,64]{1,0:T(8,128)} %get-tuple-element.26.refs_1_, f32[2048,64]{1,0:T(8,128)} %pad_maximum_fusion.3.refs_2_, bf16[12288,64]{1,0:T(8,128)(2,1)} %get-tuple-element.28.refs_3_), custom_call_target="tpu_custom_call" | custom-call | bytes 9437184 | tf_op jit(solution)/shard_map/pallas_call | solution.py:129
  284.8 4.3 %copy.11 = bf16[4,3072,64]{1,2,0:T(8,128)(2,1)} copy(bf16[4,3072,64]{2,1,0:T(8,128)(2,1)} %bitcast.56) | data formatting | bytes 3145728 | tf_op jit(solution)/shard_map/all_to_all | solution.py:271
  289.1 5.3 %all-to-all-start = ((bf16[4,3072,64]{1,2,0:T(8,128)(2,1)}), bf16[4,3072,64]{1,2,0:T(8,128)(2,1)S(1)}, u32[]{:S(2)}, u32[]{:S(2)}) async-start(bf16[4,3072,64]{1,2,0:T(8,128)(2,1)} %copy.11), calls=%async_computation | async-start | bytes 3145728 | tf_op jit(solution)/shard_map/all_to_all | solution.py:271
  294.4 8.2 %scatter_custom_fusion = f32[12288]{0:T(1024)S(1)} fusion(s32[2048]{0:T(1024)S(1)} %bitcast.62, f32[2048]{0:T(1024)S(1)} %add_divide_fusion, f32[]{:T(128)} %constant.17.clone.1), kind=kCustom, calls=%fused_computation.27 | custom fusion | bytes 49156 | tf_op jit(solution)/shard_map/scatter | solution.py:238
  302.7 11.1 %all-to-all-done = bf16[4,3072,64]{1,2,0:T(8,128)(2,1)S(1)} async-done(((bf16[4,3072,64]{1,2,0:T(8,128)(2,1)}), bf16[4,3072,64]{1,2,0:T(8,128)(2,1)S(1)}, u32[]{:S(2)}, u32[]{:S(2)}) %all-to-all-start) | async-done | bytes 1572896 | tf_op jit(solution)/shard_map/all_to_all | solution.py:271
  314.5 2.7 collective-permute-start.8
  319.0 8.0 %collective-permute-done.9 = f32[256,256]{1,0:T(8,128)S(1)} collective-permute-done((f32[256,256]{1,0:T(8,128)S(1)}, f32[256,256]{1,0:T(8,128)S(1)}, u32[]{:S(2)}, u32[]{:S(2)}) %collective-permute-start.9) | collective-permute-done | bytes 262176 | tf_op jit(solution)/shard_map/ppermute | solution.py:216
  328.1 8.3 %collective-permute-done.10 = f32[256,256]{1,0:T(8,128)S(1)} collective-permute-done((f32[256,256]{1,0:T(8,128)S(1)}, f32[256,256]{1,0:T(8,128)S(1)}, u32[]{:S(2)}, u32[]{:S(2)}) %collective-permute-start.10) | collective-permute-done | bytes 262176 | tf_op jit(solution)/shard_map/ppermute | solution.py:216
  336.5 7.5 %collective-permute-done.11 = f32[256,256]{1,0:T(8,128)S(1)} collective-permute-done((f32[256,256]{1,0:T(8,128)S(1)}, f32[256,256]{1,0:T(8,128)S(1)}, u32[]{:S(2)}, u32[]{:S(2)}) %collective-permute-start.11) | collective-permute-done | bytes 262176 | tf_op jit(solution)/shard_map/ppermute | solution.py:216
  344.2 7.9 %collective-permute-done.12 = f32[256,256]{1,0:T(8,128)S(1)} collective-permute-done((f32[256,256]{1,0:T(8,128)S(1)}, f32[256,256]{1,0:T(8,128)S(1)}, u32[]{:S(2)}, u32[]{:S(2)}) %collective-permute-start.12) | collective-permute-done | bytes 262176 | tf_op jit(solution)/shard_map/ppermute | solution.py:216
  353.7 6.7 %collective-permute-done.13 = f32[256,256]{1,0:T(8,128)S(1)} collective-permute-done((f32[256,256]{1,0:T(8,128)S(1)}, f32[256,256]{1,0:T(8,128)S(1)}, u32[]{:S(2)}, u32[]{:S(2)}) %collective-permute-start.13) | collective-permute-done | bytes 262176 | tf_op jit(solution)/shard_map/ppermute | solution.py:216
  360.4 2.8 collective-permute-start.14
  363.2 5.2 %collective-permute-done.14 = f32[256,256]{1,0:T(8,128)S(1)} collective-permute-done((f32[256,256]{1,0:T(8,128)S(1)}, f32[256,256]{1,0:T(8,128)S(1)}, u32[]{:S(2)}, u32[]{:S(2)}) %collective-permute-start.14) | collective-permute-done | bytes 262176 | tf_op jit(solution)/shard_map/ppermute | solution.py:216
  375.7 17.2 %all_to_all.38 = bf16[3072,4,64]{0,2,1:T(8,128)(2,1)S(1)} all-to-all(bf16[3072,4,64]{0,2,1:T(8,128)(2,1)S(1)} %bitcast.57), channel_id=1, replica_groups=mesh['dom'=32,'band'=4] {'band'}, dimensions={1} | all-to-all | bytes 3145728 | tf_op jit(solution)/shard_map/all_to_all | solution.py:285
  (58 shorter events, 35.1 us)
Async XLA Ops:
  4.7 4.1 %copy-start = (f32[32]{0:T(128)S(1)}, f32[32]{0:T(128)}, u32[]{:S(2)}) copy-start(f32[32]{0:T(128)} %param.9) | copy-start | bytes 388
  87.4 10.5 %collective-permute-start = (f32[1024,64]{1,0:T(8,128)S(1)}, f32[1024,64]{1,0:T(8,128)S(1)}, u32[]{:S(2)}, u32[]{:S(2)}) collective-permute-start(f32[1024,64]{1,0:T(8,128)S(1)} %get-tuple-element.37), channel_id=1, source_target_pairs={{0,4},{4,8},{8,12},{12,16},{16,20},{20,24},{24,28},{28,32},{32,36}... | collective-permute-start | bytes 786440 | tf_op jit(solution)/shard_map/ppermute | solution.py:253
  89.3 10.3 %collective-permute-start.1 = (f32[1024,64]{1,0:T(8,128)S(1)}, f32[1024,64]{1,0:T(8,128)S(1)}, u32[]{:S(2)}, u32[]{:S(2)}) collective-permute-start(f32[1024,64]{1,0:T(8,128)S(1)} %get-tuple-element.38), channel_id=1, source_target_pairs={{4,0},{8,4},{12,8},{16,12},{20,16},{24,20},{28,24},{32,28},{36,32}... | collective-permute-start | bytes 786440 | tf_op jit(solution)/shard_map/ppermute | solution.py:254
  141.9 10.7 %collective-permute-start.2 = (f32[1024,64]{1,0:T(8,128)S(1)}, f32[1024,64]{1,0:T(8,128)S(1)}, u32[]{:S(2)}, u32[]{:S(2)}) collective-permute-start(f32[1024,64]{1,0:T(8,128)S(1)} %get-tuple-element.35), channel_id=1, source_target_pairs={{0,4},{4,8},{8,12},{12,16},{16,20},{20,24},{24,28},{28,32},{32,36}... | collective-permute-start | bytes 786440 | tf_op jit(solution)/shard_map/ppermute | solution.py:253
  147.7 8.6 %collective-permute-start.3 = (f32[1024,64]{1,0:T(8,128)S(1)}, f32[1024,64]{1,0:T(8,128)S(1)}, u32[]{:S(2)}, u32[]{:S(2)}) collective-permute-start(f32[1024,64]{1,0:T(8,128)S(1)} %get-tuple-element.36), channel_id=1, source_target_pairs={{4,0},{8,4},{12,8},{16,12},{20,16},{24,20},{28,24},{32,28},{36,32}... | collective-permute-start | bytes 786440 | tf_op jit(solution)/shard_map/ppermute | solution.py:254
  199.5 10.7 %collective-permute-start.4 = (f32[1024,64]{1,0:T(8,128)S(1)}, f32[1024,64]{1,0:T(8,128)S(1)}, u32[]{:S(2)}, u32[]{:S(2)}) collective-permute-start(f32[1024,64]{1,0:T(8,128)S(1)} %get-tuple-element.33), channel_id=1, source_target_pairs={{0,4},{4,8},{8,12},{12,16},{16,20},{20,24},{24,28},{28,32},{32,36}... | collective-permute-start | bytes 786440 | tf_op jit(solution)/shard_map/ppermute | solution.py:253
  205.4 8.6 %collective-permute-start.5 = (f32[1024,64]{1,0:T(8,128)S(1)}, f32[1024,64]{1,0:T(8,128)S(1)}, u32[]{:S(2)}, u32[]{:S(2)}) collective-permute-start(f32[1024,64]{1,0:T(8,128)S(1)} %get-tuple-element.34), channel_id=1, source_target_pairs={{4,0},{8,4},{12,8},{16,12},{20,16},{24,20},{28,24},{32,28},{36,32}... | collective-permute-start | bytes 786440 | tf_op jit(solution)/shard_map/ppermute | solution.py:254
  257.1 10.7 %collective-permute-start.6 = (f32[1024,64]{1,0:T(8,128)S(1)}, f32[1024,64]{1,0:T(8,128)S(1)}, u32[]{:S(2)}, u32[]{:S(2)}) collective-permute-start(f32[1024,64]{1,0:T(8,128)S(1)} %get-tuple-element.31), channel_id=1, source_target_pairs={{0,4},{4,8},{8,12},{12,16},{16,20},{20,24},{24,28},{28,32},{32,36}... | collective-permute-start | bytes 786440 | tf_op jit(solution)/shard_map/ppermute | solution.py:253
  263.0 8.6 %collective-permute-start.7 = (f32[1024,64]{1,0:T(8,128)S(1)}, f32[1024,64]{1,0:T(8,128)S(1)}, u32[]{:S(2)}, u32[]{:S(2)}) collective-permute-start(f32[1024,64]{1,0:T(8,128)S(1)} %get-tuple-element.32), channel_id=1, source_target_pairs={{4,0},{8,4},{12,8},{16,12},{20,16},{24,20},{28,24},{32,28},{36,32}... | collective-permute-start | bytes 786440 | tf_op jit(solution)/shard_map/ppermute | solution.py:254
  289.1 24.7 %all-to-all-start = ((bf16[4,3072,64]{1,2,0:T(8,128)(2,1)}), bf16[4,3072,64]{1,2,0:T(8,128)(2,1)S(1)}, u32[]{:S(2)}, u32[]{:S(2)}) async-start(bf16[4,3072,64]{1,2,0:T(8,128)(2,1)} %copy.11), calls=%async_computation | async-start | bytes 3145728 | tf_op jit(solution)/shard_map/all_to_all | solution.py:271
  314.5 3.8 collective-permute-start.8
  318.4 8.7 %collective-permute-start.9 = (f32[256,256]{1,0:T(8,128)S(1)}, f32[256,256]{1,0:T(8,128)S(1)}, u32[]{:S(2)}, u32[]{:S(2)}) collective-permute-start(f32[256,256]{1,0:T(8,128)S(1)} %add.53), channel_id=1, source_target_pairs={{0,1},{1,0},{2,3},{3,2},{4,5},{5,4},{6,7},{7,6},{8,9},{9,8},{10,11... | collective-permute-start | bytes 786440 | tf_op jit(solution)/shard_map/ppermute | solution.py:216
  327.1 9.3 %collective-permute-start.10 = (f32[256,256]{1,0:T(8,128)S(1)}, f32[256,256]{1,0:T(8,128)S(1)}, u32[]{:S(2)}, u32[]{:S(2)}) collective-permute-start(f32[256,256]{1,0:T(8,128)S(1)} %add.54), channel_id=1, source_target_pairs={{0,2},{1,3},{2,0},{3,1},{4,6},{5,7},{6,4},{7,5},{8,10},{9,11},{10,... | collective-permute-start | bytes 786440 | tf_op jit(solution)/shard_map/ppermute | solution.py:216
  336.4 7.6 %collective-permute-start.11 = (f32[256,256]{1,0:T(8,128)S(1)}, f32[256,256]{1,0:T(8,128)S(1)}, u32[]{:S(2)}, u32[]{:S(2)}) collective-permute-start(f32[256,256]{1,0:T(8,128)S(1)} %add.55), channel_id=1, source_target_pairs={{0,8},{1,9},{2,10},{3,11},{4,12},{5,13},{6,14},{7,15},{8,0},{9,1},... | collective-permute-start | bytes 786440 | tf_op jit(solution)/shard_map/ppermute | solution.py:216
  344.1 8.0 %collective-permute-start.12 = (f32[256,256]{1,0:T(8,128)S(1)}, f32[256,256]{1,0:T(8,128)S(1)}, u32[]{:S(2)}, u32[]{:S(2)}) collective-permute-start(f32[256,256]{1,0:T(8,128)S(1)} %add.56), channel_id=1, source_target_pairs={{0,16},{1,17},{2,18},{3,19},{4,20},{5,21},{6,22},{7,23},{8,24},{9,... | collective-permute-start | bytes 786440 | tf_op jit(solution)/shard_map/ppermute | solution.py:216
  352.1 8.3 %collective-permute-start.13 = (f32[256,256]{1,0:T(8,128)S(1)}, f32[256,256]{1,0:T(8,128)S(1)}, u32[]{:S(2)}, u32[]{:S(2)}) collective-permute-start(f32[256,256]{1,0:T(8,128)S(1)} %add.57), channel_id=1, source_target_pairs={{0,32},{1,33},{2,34},{3,35},{4,36},{5,37},{6,38},{7,39},{8,40},{9,... | collective-permute-start | bytes 786440 | tf_op jit(solution)/shard_map/ppermute | solution.py:216
  360.4 8.0 %collective-permute-start.14 = (f32[256,256]{1,0:T(8,128)S(1)}, f32[256,256]{1,0:T(8,128)S(1)}, u32[]{:S(2)}, u32[]{:S(2)}) collective-permute-start(f32[256,256]{1,0:T(8,128)S(1)} %add.58), channel_id=1, source_target_pairs={{0,64},{1,65},{2,66},{3,67},{4,68},{5,69},{6,70},{7,71},{8,72},{9,... | collective-permute-start | bytes 786440 | tf_op jit(solution)/shard_map/ppermute | solution.py:216

commit v2 on v0

--- a/solution.py
+++ b/solution.py
@@ -79,7 +79,7 @@
         product = jnp.dot(ops[:, :body_rows], main_rows, preferred_element_type=jnp.float32)
         product = product + jnp.dot(ops[:, body_rows:], tail_rows, preferred_element_type=jnp.float32)
         scale = scales[cell]
-        pot = pot_ref[0]
+        pot = jnp.transpose(jnp.broadcast_to(pot_ref[0], (8, width)))[:, 0:1]
         top = product[:body_rows] * scale + pot[:body_rows] * main_rows.astype(jnp.float32)
         bottom = product[body_rows:] * scale + pot[body_rows:] * tail_rows.astype(jnp.float32)
         local_out[pl.ds(start, body_rows), :] += top
@@ -116,7 +116,7 @@
     if apply:
         args += [window_ops, window_pot]
         specs += [pl.BlockSpec((1, width, width), lambda c: (c, 0, 0)),
-                  pl.BlockSpec((1, width, cols), lambda c: (c, 0, 0))]
+                  pl.BlockSpec((1, 1, width), lambda c: (c, 0, 0))]
     out_shape, out_specs = [], []
     if combine:
         out_shape.append(jax.ShapeDtypeStruct((node_total, cols), jnp.bfloat16)); out_specs.append(whole)
@@ -144,7 +144,6 @@
 
 def operator_kernel(slot_ref, pot_ref, kinetic_ref, ops_ref, pot_out_ref):
     width = kinetic_ref.shape[0]
-    cols = pot_out_ref.shape[2]
     slot_row = slot_ref[0]
     picks = (lax.broadcasted_iota(jnp.int32, (width, width), 0) == slot_row).astype(jnp.bfloat16)
     kinetic = kinetic_ref[...]
@@ -163,9 +162,7 @@
     moved = lax.dot_general(
         parts, picks, (((1,), (1,)), ((), ())), preferred_element_type=jnp.float32
     )
-    total = moved[0:1] + moved[1:2] + moved[2:3]
-    column = jnp.transpose(jnp.broadcast_to(total, (8, width)))[:, 0:1]
-    pot_out_ref[0] = jnp.broadcast_to(column, (width, cols))
+    pot_out_ref[0] = moved[0:1] + moved[1:2] + moved[2:3]
 
 
 def cell_operators(slots, potential, kinetic, cols):
@@ -180,16 +177,16 @@
         ],
         out_specs=[
             pl.BlockSpec((1, width, width), lambda c: (c, 0, 0)),
-            pl.BlockSpec((1, width, cols), lambda c: (c, 0, 0)),
+            pl.BlockSpec((1, 1, width), lambda c: (c, 0, 0)),
         ],
         out_shape=[
             jax.ShapeDtypeStruct((cells, width, width), jnp.bfloat16),
-            jax.ShapeDtypeStruct((cells, width, cols), jnp.float32),
+            jax.ShapeDtypeStruct((cells, 1, width), jnp.float32),
         ],
         compiler_params=pltpu.CompilerParams(dimension_semantics=("arbitrary",)),
         cost_estimate=pl.CostEstimate(
             flops=4 * cells * width * width * width, transcendentals=0,
-            bytes_accessed=cells * width * (width * 2 + cols * 4 + 8)),
+            bytes_accessed=cells * width * (width * 2 + 12)),
     )(slots.reshape(cells, 1, width), potential.reshape(cells, 1, width), kinetic)
 
 
@@ -232,14 +229,15 @@
     state_cols = states.shape[0]
     has_left = (domain > 0).astype(jnp.float32)
     has_right = (domain < domains - 1).astype(jnp.float32)
-    multiplicity = (
+    face_counts = jnp.concatenate(
+        [jnp.full((face_width,), has_left), jnp.full((face_width,), has_right)]
+    )
+    node_weight = (
         jnp.ones((node_total,), jnp.float32)
-        .at[left_face]
-        .add(has_left)
-        .at[right_face]
-        .add(has_right)
-    )
-    node_weight = (1.0 / multiplicity).astype(jnp.bfloat16)
+        .at[faces]
+        .set(1.0 / (1.0 + face_counts), unique_indices=True)
+        .astype(jnp.bfloat16)
+    )
     cells, width = connectivity.shape
     starts = jnp.arange(cells, dtype=jnp.int32) * (3 * (width // 4))
     slots = (connectivity - starts[:, None]) % node_total

time: 391 us -> 381 us (0.974)
  other arithmetic: 20.3 us -> 8.12 us
  Pallas kernels: 204 us -> 194 us
  local copies, waits for them, and re-layouts: 16.9 us -> 25.1 us
    scatter-add x2 -> x0, other arithmetic: 12.2 us -> none  [body(): multiplicity = jnp.ones((node_total,), jnp.float32).at[left_face].add(has...]
    scatter x0 -> x1, local copies, waits for them, and re-layouts: none -> 8.25 us  [body(): node_weight = jnp.ones((node_total,), jnp.float32).at[faces].set(1.0 / (1...]
    pallas_call x1, Pallas kernels: 39.2 us -> 31.4 us  [cell_operators(): pl.pallas_call(operator_kernel, grid=(cells,), in_specs=[pl.BlockSpec((1,...]
    all_to_all x1, waiting for transfers between devices: 7.11 us -> 11.1 us  [body(): lax.all_to_all(current, 'band', split_axis=0, concat_axis=1, tiled=True)]
  transfers between devices with their start and end apart: 16 -> 16, of which waited for: 16 -> 16; matrix products, arithmetic and copies ran while one was open for 3% -> 2% of each run, Pallas kernels for 0% -> 0%
where the time goes in v2:
time: 381 us; the launch traced here: 378 us
  Pallas kernels  194 us (51%)
  waiting for transfers between devices  82.4 us (22%)
  starting transfers between devices  43.2 us (11%)
  local copies, waits for them, and re-layouts  25.1 us (7%)
  blocking collectives  17.3 us (5%)
  other arithmetic  8.12 us (2%)
  matrix products  6.39 us (2%)
    pallas_call x5, Pallas kernels, field_step(): pl.pallas_call(functools.partial(field_kernel, combine, has_older, apply,...  163 us
    ppermute x7, waiting for transfers between devices, doubling_sum(): total = total + lax.ppermute(total, ('dom', 'band'), pairs)  44.6 us
    pallas_call x1, Pallas kernels, cell_operators(): pl.pallas_call(operator_kernel, grid=(cells,), in_specs=[pl.BlockSpec((1,...  31.4 us
    ppermute x4, starting transfers between devices, exchange(): from_left = lax.ppermute(face_values[face_width:], 'dom', up)  19.6 us
    all_to_all x1, blocking collectives, body(): lax.all_to_all(rotated, 'band', split_axis=1, concat_axis=0, tiled=True)  17.3 us
    ppermute x4, waiting for transfers between devices, exchange(): from_left = lax.ppermute(face_values[face_width:], 'dom', up)  13.5 us
    ppermute x4, waiting for transfers between devices, exchange(): from_right = lax.ppermute(face_values[:face_width], 'dom', down)  13.2 us
    all_to_all x1, waiting for transfers between devices, body(): lax.all_to_all(current, 'band', split_axis=0, concat_axis=1, tiled=True)  11.1 us
  transfers between devices with their start and end apart: 16, of which 16 were waited for; matrix products, arithmetic and copies ran while one was open for 2% of the time, Pallas kernels for 0%

profile of v2, /device:TPU:6, one launch (start us, length us, event | category | flops | bytes accessed | tf_op | source)
XLA Modules:
  0.0 378.4 jit_solution(9503435059079902214)
XLA Ops:
  4.7 4.1 %copy.10 = bf16[64,12288]{0,1:T(8,128)(2,1)} copy(bf16[64,12288]{1,0:T(8,128)(2,1)} %param.7) | data formatting | bytes 3145728 | tf_op args[0]
  9.9 31.4 %shard_map.73 = (bf16[32,512,512]{2,1,0:T(8,128)(2,1)}, f32[32,1,512]{2,1,0:T(1,128)}) custom-call(s32[32,1,512]{2,1,0:T(1,128)} %reshape.113.slot_ref, f32[32,1,512]{2,1,0:T(1,128)} %reshape.114.pot_ref, bf16[512,512]{1,0:T(8,128)(2,1)} %kinetic_ref.1), custom_call_target="tpu_custom_call" | custom-call | flops 17179869184 | bytes 16973824 | tf_op jit(solution)/shard_map/pallas_call | solution.py:170
  41.3 30.8 %shard_map.74 = (f32[12288,64]{1,0:T(8,128)}, f32[2048,64]{1,0:T(8,128)}) custom-call(s32[2048]{0:T(1024)} %pad_add_fusion.refs_0_, f32[32]{0:T(128)} %compare_select_fusion.1.refs_1_, bf16[12288,64]{1,0:T(8,128)(2,1)} %bitcast.52, bf16[32,512,512]{2,1,0:T(8,128)(2,1)} %get-tuple-element.17.refs_3_.refs_4_.refs_5_, ...), custom_call_target="tpu_custom_call" | custom-call | flops 1073741824 | bytes 26214400 | tf_op jit(solution)/shard_map/pallas_call | solution.py:129
  75.3 3.6 collective-permute-start.1
  78.9 4.9 %collective-permute-done = f32[1024,64]{1,0:T(8,128)S(1)} collective-permute-done((f32[1024,64]{1,0:T(8,128)S(1)}, f32[1024,64]{1,0:T(8,128)S(1)}, u32[]{:S(2)}, u32[]{:S(2)}) %collective-permute-start) | collective-permute-done | bytes 262176 | tf_op jit(solution)/shard_map/ppermute | solution.py:253
  86.7 39.4 %shard_map.75 = (bf16[12288,64]{1,0:T(8,128)(2,1)}, f32[12288,64]{1,0:T(8,128)}, f32[2048,64]{1,0:T(8,128)}) custom-call(s32[2048]{0:T(1024)} %pad_add_fusion.refs_0_, f32[32]{0:T(128)} %compare_select_fusion.1.refs_1_, f32[12288,64]{1,0:T(8,128)} %get-tuple-element.19.refs_2_, f32[2048,64]{1,0:T(8,128)} %pad_maximum_fusion.refs_3_, ...), custom_call_target="tpu_custom_call" | custom-call | flops 1073741824 | bytes 26214400 | tf_op jit(solution)/shard_map/pallas_call | solution.py:129
  127.3 5.8 %collective-permute-start.2 = (f32[1024,64]{1,0:T(8,128)S(1)}, f32[1024,64]{1,0:T(8,128)S(1)}, u32[]{:S(2)}, u32[]{:S(2)}) collective-permute-start(f32[1024,64]{1,0:T(8,128)S(1)} %get-tuple-element.35), channel_id=1, source_target_pairs={{0,4},{4,8},{8,12},{12,16},{16,20},{20,24},{24,28},{28,32},{32,36}... | collective-permute-start | bytes 786440 | tf_op jit(solution)/shard_map/ppermute | solution.py:253
  133.1 1.9 collective-permute-start.3
  135.0 2.9 collective-permute-done.2
  138.0 3.7 collective-permute-done.3
  142.8 40.2 %shard_map.76 = (bf16[12288,64]{1,0:T(8,128)(2,1)}, f32[12288,64]{1,0:T(8,128)}, f32[2048,64]{1,0:T(8,128)}) custom-call(s32[2048]{0:T(1024)} %pad_add_fusion.refs_0_, f32[32]{0:T(128)} %compare_select_fusion.1.refs_1_, f32[12288,64]{1,0:T(8,128)} %get-tuple-element.21.refs_2_, f32[2048,64]{1,0:T(8,128)} %pad_maximum_fusion.1.refs_3_, ...), custom_call_target="tpu_custom_call" | custom-call | flops 1073741824 | bytes 26214400 | tf_op jit(solution)/shard_map/pallas_call | solution.py:129
  184.2 5.9 %collective-permute-start.4 = (f32[1024,64]{1,0:T(8,128)S(1)}, f32[1024,64]{1,0:T(8,128)S(1)}, u32[]{:S(2)}, u32[]{:S(2)}) collective-permute-start(f32[1024,64]{1,0:T(8,128)S(1)} %get-tuple-element.33), channel_id=1, source_target_pairs={{0,4},{4,8},{8,12},{12,16},{16,20},{20,24},{24,28},{28,32},{32,36}... | collective-permute-start | bytes 786440 | tf_op jit(solution)/shard_map/ppermute | solution.py:253
  192.1 2.8 collective-permute-done.4
  194.9 3.9 %collective-permute-done.5 = f32[1024,64]{1,0:T(8,128)S(1)} collective-permute-done((f32[1024,64]{1,0:T(8,128)S(1)}, f32[1024,64]{1,0:T(8,128)S(1)}, u32[]{:S(2)}, u32[]{:S(2)}) %collective-permute-start.5) | collective-permute-done | bytes 262176 | tf_op jit(solution)/shard_map/ppermute | solution.py:254
  199.8 40.3 %shard_map.77 = (bf16[12288,64]{1,0:T(8,128)(2,1)}, f32[12288,64]{1,0:T(8,128)}, f32[2048,64]{1,0:T(8,128)}) custom-call(s32[2048]{0:T(1024)} %pad_add_fusion.refs_0_, f32[32]{0:T(128)} %compare_select_fusion.1.refs_1_, f32[12288,64]{1,0:T(8,128)} %get-tuple-element.23.refs_2_, f32[2048,64]{1,0:T(8,128)} %pad_maximum_fusion.2.refs_3_, ...), custom_call_target="tpu_custom_call" | custom-call | flops 1073741824 | bytes 26214400 | tf_op jit(solution)/shard_map/pallas_call | solution.py:129
  241.3 5.9 %collective-permute-start.6 = (f32[1024,64]{1,0:T(8,128)S(1)}, f32[1024,64]{1,0:T(8,128)S(1)}, u32[]{:S(2)}, u32[]{:S(2)}) collective-permute-start(f32[1024,64]{1,0:T(8,128)S(1)} %get-tuple-element.31), channel_id=1, source_target_pairs={{0,4},{4,8},{8,12},{12,16},{16,20},{20,24},{24,28},{28,32},{32,36}... | collective-permute-start | bytes 786440 | tf_op jit(solution)/shard_map/ppermute | solution.py:253
  249.2 2.8 collective-permute-done.6
  252.0 3.9 %collective-permute-done.7 = f32[1024,64]{1,0:T(8,128)S(1)} collective-permute-done((f32[1024,64]{1,0:T(8,128)S(1)}, f32[1024,64]{1,0:T(8,128)S(1)}, u32[]{:S(2)}, u32[]{:S(2)}) %collective-permute-start.7) | collective-permute-done | bytes 262176 | tf_op jit(solution)/shard_map/ppermute | solution.py:254
  256.9 12.2 %shard_map.78 = bf16[12288,64]{1,0:T(8,128)(2,1)} custom-call(s32[2048]{0:T(1024)} %pad_add_fusion.refs_0_, f32[12288,64]{1,0:T(8,128)} %get-tuple-element.26.refs_1_, f32[2048,64]{1,0:T(8,128)} %pad_maximum_fusion.3.refs_2_, bf16[12288,64]{1,0:T(8,128)(2,1)} %get-tuple-element.28.refs_3_), custom_call_target="tpu_custom_call" | custom-call | bytes 9437184 | tf_op jit(solution)/shard_map/pallas_call | solution.py:129
  269.1 4.3 %copy.11 = bf16[4,3072,64]{1,2,0:T(8,128)(2,1)} copy(bf16[4,3072,64]{2,1,0:T(8,128)(2,1)} %bitcast.56) | data formatting | bytes 3145728 | tf_op jit(solution)/shard_map/all_to_all | solution.py:271
  273.4 5.3 %all-to-all-start = ((bf16[4,3072,64]{1,2,0:T(8,128)(2,1)}), bf16[4,3072,64]{1,2,0:T(8,128)(2,1)S(1)}, u32[]{:S(2)}, u32[]{:S(2)}) async-start(bf16[4,3072,64]{1,2,0:T(8,128)(2,1)} %copy.11), calls=%async_computation | async-start | bytes 3145728 | tf_op jit(solution)/shard_map/all_to_all | solution.py:271
  278.7 8.2 %scatter_custom_fusion = f32[12288]{0:T(1024)S(1)} fusion(s32[2048]{0:T(1024)S(1)} %bitcast.62, f32[2048]{0:T(1024)S(1)} %add_divide_fusion, f32[]{:T(128)} %constant.17.clone.1), kind=kCustom, calls=%fused_computation.27 | custom fusion | bytes 49156 | tf_op jit(solution)/shard_map/scatter | solution.py:238
  287.0 11.1 %all-to-all-done = bf16[4,3072,64]{1,2,0:T(8,128)(2,1)S(1)} async-done(((bf16[4,3072,64]{1,2,0:T(8,128)(2,1)}), bf16[4,3072,64]{1,2,0:T(8,128)(2,1)S(1)}, u32[]{:S(2)}, u32[]{:S(2)}) %all-to-all-start) | async-done | bytes 1572896 | tf_op jit(solution)/shard_map/all_to_all | solution.py:271
  298.7 2.7 collective-permute-start.8
  303.2 8.0 %collective-permute-done.9 = f32[256,256]{1,0:T(8,128)S(1)} collective-permute-done((f32[256,256]{1,0:T(8,128)S(1)}, f32[256,256]{1,0:T(8,128)S(1)}, u32[]{:S(2)}, u32[]{:S(2)}) %collective-permute-start.9) | collective-permute-done | bytes 262176 | tf_op jit(solution)/shard_map/ppermute | solution.py:216
  312.3 8.3 %collective-permute-done.10 = f32[256,256]{1,0:T(8,128)S(1)} collective-permute-done((f32[256,256]{1,0:T(8,128)S(1)}, f32[256,256]{1,0:T(8,128)S(1)}, u32[]{:S(2)}, u32[]{:S(2)}) %collective-permute-start.10) | collective-permute-done | bytes 262176 | tf_op jit(solution)/shard_map/ppermute | solution.py:216
  320.7 7.5 %collective-permute-done.11 = f32[256,256]{1,0:T(8,128)S(1)} collective-permute-done((f32[256,256]{1,0:T(8,128)S(1)}, f32[256,256]{1,0:T(8,128)S(1)}, u32[]{:S(2)}, u32[]{:S(2)}) %collective-permute-start.11) | collective-permute-done | bytes 262176 | tf_op jit(solution)/shard_map/ppermute | solution.py:216
  328.4 7.9 %collective-permute-done.12 = f32[256,256]{1,0:T(8,128)S(1)} collective-permute-done((f32[256,256]{1,0:T(8,128)S(1)}, f32[256,256]{1,0:T(8,128)S(1)}, u32[]{:S(2)}, u32[]{:S(2)}) %collective-permute-start.12) | collective-permute-done | bytes 262176 | tf_op jit(solution)/shard_map/ppermute | solution.py:216
  338.0 6.6 %collective-permute-done.13 = f32[256,256]{1,0:T(8,128)S(1)} collective-permute-done((f32[256,256]{1,0:T(8,128)S(1)}, f32[256,256]{1,0:T(8,128)S(1)}, u32[]{:S(2)}, u32[]{:S(2)}) %collective-permute-start.13) | collective-permute-done | bytes 262176 | tf_op jit(solution)/shard_map/ppermute | solution.py:216
  344.6 2.8 collective-permute-start.14
  347.5 5.1 %collective-permute-done.14 = f32[256,256]{1,0:T(8,128)S(1)} collective-permute-done((f32[256,256]{1,0:T(8,128)S(1)}, f32[256,256]{1,0:T(8,128)S(1)}, u32[]{:S(2)}, u32[]{:S(2)}) %collective-permute-start.14) | collective-permute-done | bytes 262176 | tf_op jit(solution)/shard_map/ppermute | solution.py:216
  359.9 17.3 %all_to_all.38 = bf16[3072,4,64]{0,2,1:T(8,128)(2,1)S(1)} all-to-all(bf16[3072,4,64]{0,2,1:T(8,128)(2,1)S(1)} %bitcast.57), channel_id=1, replica_groups=mesh['dom'=32,'band'=4] {'band'}, dimensions={1} | all-to-all | bytes 3145728 | tf_op jit(solution)/shard_map/all_to_all | solution.py:285
  (58 shorter events, 35.2 us)
Async XLA Ops:
  4.7 4.1 %copy-start = (f32[32]{0:T(128)S(1)}, f32[32]{0:T(128)}, u32[]{:S(2)}) copy-start(f32[32]{0:T(128)} %param.9) | copy-start | bytes 388
  73.4 10.5 %collective-permute-start = (f32[1024,64]{1,0:T(8,128)S(1)}, f32[1024,64]{1,0:T(8,128)S(1)}, u32[]{:S(2)}, u32[]{:S(2)}) collective-permute-start(f32[1024,64]{1,0:T(8,128)S(1)} %get-tuple-element.37), channel_id=1, source_target_pairs={{0,4},{4,8},{8,12},{12,16},{16,20},{20,24},{24,28},{28,32},{32,36}... | collective-permute-start | bytes 786440 | tf_op jit(solution)/shard_map/ppermute | solution.py:253
  75.3 10.3 %collective-permute-start.1 = (f32[1024,64]{1,0:T(8,128)S(1)}, f32[1024,64]{1,0:T(8,128)S(1)}, u32[]{:S(2)}, u32[]{:S(2)}) collective-permute-start(f32[1024,64]{1,0:T(8,128)S(1)} %get-tuple-element.38), channel_id=1, source_target_pairs={{4,0},{8,4},{12,8},{16,12},{20,16},{24,20},{28,24},{32,28},{36,32}... | collective-permute-start | bytes 786440 | tf_op jit(solution)/shard_map/ppermute | solution.py:254
  127.3 10.7 %collective-permute-start.2 = (f32[1024,64]{1,0:T(8,128)S(1)}, f32[1024,64]{1,0:T(8,128)S(1)}, u32[]{:S(2)}, u32[]{:S(2)}) collective-permute-start(f32[1024,64]{1,0:T(8,128)S(1)} %get-tuple-element.35), channel_id=1, source_target_pairs={{0,4},{4,8},{8,12},{12,16},{16,20},{20,24},{24,28},{28,32},{32,36}... | collective-permute-start | bytes 786440 | tf_op jit(solution)/shard_map/ppermute | solution.py:253
  133.1 8.6 %collective-permute-start.3 = (f32[1024,64]{1,0:T(8,128)S(1)}, f32[1024,64]{1,0:T(8,128)S(1)}, u32[]{:S(2)}, u32[]{:S(2)}) collective-permute-start(f32[1024,64]{1,0:T(8,128)S(1)} %get-tuple-element.36), channel_id=1, source_target_pairs={{4,0},{8,4},{12,8},{16,12},{20,16},{24,20},{28,24},{32,28},{36,32}... | collective-permute-start | bytes 786440 | tf_op jit(solution)/shard_map/ppermute | solution.py:254
  184.2 10.7 %collective-permute-start.4 = (f32[1024,64]{1,0:T(8,128)S(1)}, f32[1024,64]{1,0:T(8,128)S(1)}, u32[]{:S(2)}, u32[]{:S(2)}) collective-permute-start(f32[1024,64]{1,0:T(8,128)S(1)} %get-tuple-element.33), channel_id=1, source_target_pairs={{0,4},{4,8},{8,12},{12,16},{16,20},{20,24},{24,28},{28,32},{32,36}... | collective-permute-start | bytes 786440 | tf_op jit(solution)/shard_map/ppermute | solution.py:253
  190.1 8.6 %collective-permute-start.5 = (f32[1024,64]{1,0:T(8,128)S(1)}, f32[1024,64]{1,0:T(8,128)S(1)}, u32[]{:S(2)}, u32[]{:S(2)}) collective-permute-start(f32[1024,64]{1,0:T(8,128)S(1)} %get-tuple-element.34), channel_id=1, source_target_pairs={{4,0},{8,4},{12,8},{16,12},{20,16},{24,20},{28,24},{32,28},{36,32}... | collective-permute-start | bytes 786440 | tf_op jit(solution)/shard_map/ppermute | solution.py:254
  241.3 10.7 %collective-permute-start.6 = (f32[1024,64]{1,0:T(8,128)S(1)}, f32[1024,64]{1,0:T(8,128)S(1)}, u32[]{:S(2)}, u32[]{:S(2)}) collective-permute-start(f32[1024,64]{1,0:T(8,128)S(1)} %get-tuple-element.31), channel_id=1, source_target_pairs={{0,4},{4,8},{8,12},{12,16},{16,20},{20,24},{24,28},{28,32},{32,36}... | collective-permute-start | bytes 786440 | tf_op jit(solution)/shard_map/ppermute | solution.py:253
  247.2 8.6 %collective-permute-start.7 = (f32[1024,64]{1,0:T(8,128)S(1)}, f32[1024,64]{1,0:T(8,128)S(1)}, u32[]{:S(2)}, u32[]{:S(2)}) collective-permute-start(f32[1024,64]{1,0:T(8,128)S(1)} %get-tuple-element.32), channel_id=1, source_target_pairs={{4,0},{8,4},{12,8},{16,12},{20,16},{24,20},{28,24},{32,28},{36,32}... | collective-permute-start | bytes 786440 | tf_op jit(solution)/shard_map/ppermute | solution.py:254
  273.4 24.6 %all-to-all-start = ((bf16[4,3072,64]{1,2,0:T(8,128)(2,1)}), bf16[4,3072,64]{1,2,0:T(8,128)(2,1)S(1)}, u32[]{:S(2)}, u32[]{:S(2)}) async-start(bf16[4,3072,64]{1,2,0:T(8,128)(2,1)} %copy.11), calls=%async_computation | async-start | bytes 3145728 | tf_op jit(solution)/shard_map/all_to_all | solution.py:271
  298.7 3.8 %collective-permute-start.8 = (f32[256,256]{1,0:T(8,128)S(1)}, f32[256,256]{1,0:T(8,128)S(1)}, u32[]{:S(2)}, u32[]{:S(2)}) collective-permute-start(f32[256,256]{1,0:T(8,128)S(1)} %fusion.13), channel_id=1, source_target_pairs={{0,4},{1,5},{2,6},{3,7},{4,0},{5,1},{6,2},{7,3},{8,12},{9,13},{10,... | collective-permute-start | bytes 786440 | tf_op jit(solution)/shard_map/ppermute | solution.py:216
  302.6 8.7 %collective-permute-start.9 = (f32[256,256]{1,0:T(8,128)S(1)}, f32[256,256]{1,0:T(8,128)S(1)}, u32[]{:S(2)}, u32[]{:S(2)}) collective-permute-start(f32[256,256]{1,0:T(8,128)S(1)} %add.53), channel_id=1, source_target_pairs={{0,1},{1,0},{2,3},{3,2},{4,5},{5,4},{6,7},{7,6},{8,9},{9,8},{10,11... | collective-permute-start | bytes 786440 | tf_op jit(solution)/shard_map/ppermute | solution.py:216
  311.3 9.3 %collective-permute-start.10 = (f32[256,256]{1,0:T(8,128)S(1)}, f32[256,256]{1,0:T(8,128)S(1)}, u32[]{:S(2)}, u32[]{:S(2)}) collective-permute-start(f32[256,256]{1,0:T(8,128)S(1)} %add.54), channel_id=1, source_target_pairs={{0,2},{1,3},{2,0},{3,1},{4,6},{5,7},{6,4},{7,5},{8,10},{9,11},{10,... | collective-permute-start | bytes 786440 | tf_op jit(solution)/shard_map/ppermute | solution.py:216
  320.7 7.6 %collective-permute-start.11 = (f32[256,256]{1,0:T(8,128)S(1)}, f32[256,256]{1,0:T(8,128)S(1)}, u32[]{:S(2)}, u32[]{:S(2)}) collective-permute-start(f32[256,256]{1,0:T(8,128)S(1)} %add.55), channel_id=1, source_target_pairs={{0,8},{1,9},{2,10},{3,11},{4,12},{5,13},{6,14},{7,15},{8,0},{9,1},... | collective-permute-start | bytes 786440 | tf_op jit(solution)/shard_map/ppermute | solution.py:216
  328.3 8.0 %collective-permute-start.12 = (f32[256,256]{1,0:T(8,128)S(1)}, f32[256,256]{1,0:T(8,128)S(1)}, u32[]{:S(2)}, u32[]{:S(2)}) collective-permute-start(f32[256,256]{1,0:T(8,128)S(1)} %add.56), channel_id=1, source_target_pairs={{0,16},{1,17},{2,18},{3,19},{4,20},{5,21},{6,22},{7,23},{8,24},{9,... | collective-permute-start | bytes 786440 | tf_op jit(solution)/shard_map/ppermute | solution.py:216
  336.3 8.3 %collective-permute-start.13 = (f32[256,256]{1,0:T(8,128)S(1)}, f32[256,256]{1,0:T(8,128)S(1)}, u32[]{:S(2)}, u32[]{:S(2)}) collective-permute-start(f32[256,256]{1,0:T(8,128)S(1)} %add.57), channel_id=1, source_target_pairs={{0,32},{1,33},{2,34},{3,35},{4,36},{5,37},{6,38},{7,39},{8,40},{9,... | collective-permute-start | bytes 786440 | tf_op jit(solution)/shard_map/ppermute | solution.py:216
  344.6 8.0 %collective-permute-start.14 = (f32[256,256]{1,0:T(8,128)S(1)}, f32[256,256]{1,0:T(8,128)S(1)}, u32[]{:S(2)}, u32[]{:S(2)}) collective-permute-start(f32[256,256]{1,0:T(8,128)S(1)} %add.58), channel_id=1, source_target_pairs={{0,64},{1,65},{2,66},{3,67},{4,68},{5,69},{6,70},{7,71},{8,72},{9,... | collective-permute-start | bytes 786440 | tf_op jit(solution)/shard_map/ppermute | solution.py:216

commit v3 on v2

--- a/solution.py
+++ b/solution.py
@@ -14,7 +14,7 @@
 VMEM_LIMIT = 60 * 1024 * 1024
 
 
-def field_kernel(combine, older, apply, alpha, *refs):
+def field_kernel(combine, older, apply, build, alpha, *refs):
     refs = list(refs)
     faces = refs.pop(0)
     if apply:
@@ -29,11 +29,16 @@
     if apply:
         ops_ref = refs.pop(0)
         pot_ref = refs.pop(0)
+        if build:
+            kinetic_ref = refs.pop(0)
     if combine:
         vector_out = refs.pop(0)
     if apply:
         local_out = refs.pop(0)
         faces_out = refs.pop(0)
+        if build:
+            ops_out = refs.pop(0)
+            pot_out = refs.pop(0)
     if combine:
         work = refs.pop(0)
     vector = vector_out if combine else vector_in
@@ -63,7 +68,7 @@
             prologue()
 
     if apply:
-        width = ops_ref.shape[1]
+        width = ops_ref.shape[-1]
         quarter = width // 4
         body_rows = width - quarter
 
@@ -75,11 +80,17 @@
         tail = pl.multiple_of(lax.rem((cell + 1) * body_rows, node_total), quarter)
         main_rows = vector[pl.ds(start, body_rows), :]
         tail_rows = vector[pl.ds(tail, quarter), :]
-        ops = ops_ref[0]
+        if build:
+            ops, pot_row = build_operator(ops_ref[0], pot_ref[0], kinetic_ref[...])
+            ops_out[0] = ops
+            pot_out[0] = pot_row
+        else:
+            ops = ops_ref[0]
+            pot_row = pot_ref[0]
         product = jnp.dot(ops[:, :body_rows], main_rows, preferred_element_type=jnp.float32)
         product = product + jnp.dot(ops[:, body_rows:], tail_rows, preferred_element_type=jnp.float32)
         scale = scales[cell]
-        pot = jnp.transpose(jnp.broadcast_to(pot_ref[0], (8, width)))[:, 0:1]
+        pot = jnp.transpose(jnp.broadcast_to(pot_row, (8, width)))[:, 0:1]
         top = product[:body_rows] * scale + pot[:body_rows] * main_rows.astype(jnp.float32)
         bottom = product[body_rows:] * scale + pot[body_rows:] * tail_rows.astype(jnp.float32)
         local_out[pl.ds(start, body_rows), :] += top
@@ -96,12 +107,13 @@
 
 
 def field_step(faces, scales, window_ops, window_pot, vector=None, local_in=None,
-               received=None, older=None, alpha=1.0, apply=True):
+               received=None, older=None, alpha=1.0, apply=True, kinetic=None):
     combine = local_in is not None
     has_older = older is not None
+    build = kinetic is not None
     node_total, cols = (local_in if combine else vector).shape
     face_total = faces.shape[0]
-    cells, width, _ = window_ops.shape
+    cells, width = window_pot.shape[0], window_pot.shape[-1]
     smem = pl.BlockSpec(memory_space=pltpu.SMEM)
     whole = pl.BlockSpec(memory_space=pltpu.VMEM)
     args, specs = [faces], [smem]
@@ -113,10 +125,13 @@
             args.append(older); specs.append(whole)
     else:
         args.append(vector); specs.append(whole)
+    cell_block = pl.BlockSpec((1, width, width), lambda c: (c, 0, 0))
+    row_block = pl.BlockSpec((1, 1, width), lambda c: (c, 0, 0))
     if apply:
         args += [window_ops, window_pot]
-        specs += [pl.BlockSpec((1, width, width), lambda c: (c, 0, 0)),
-                  pl.BlockSpec((1, 1, width), lambda c: (c, 0, 0))]
+        specs += [row_block if build else cell_block, row_block]
+        if build:
+            args.append(kinetic); specs.append(whole)
     out_shape, out_specs = [], []
     if combine:
         out_shape.append(jax.ShapeDtypeStruct((node_total, cols), jnp.bfloat16)); out_specs.append(whole)
@@ -124,10 +139,14 @@
         out_shape += [jax.ShapeDtypeStruct((node_total, cols), jnp.float32),
                       jax.ShapeDtypeStruct((face_total, cols), jnp.float32)]
         out_specs += [whole, whole]
+        if build:
+            out_shape += [jax.ShapeDtypeStruct((cells, width, width), jnp.bfloat16),
+                          jax.ShapeDtypeStruct((cells, 1, width), jnp.float32)]
+            out_specs += [cell_block, row_block]
     scratch = [pltpu.VMEM((node_total, cols), jnp.float32)] if combine else []
-    flops = 2 * cells * width * width * cols if apply else 0
+    flops = (2 * cells * width * width * cols if apply else 0) + (4 * cells * width ** 3 if build else 0)
     result = pl.pallas_call(
-        functools.partial(field_kernel, combine, has_older, apply, alpha),
+        functools.partial(field_kernel, combine, has_older, apply, build, alpha),
         grid=(cells if apply else 1,),
         in_specs=specs,
         out_specs=out_specs,
@@ -142,16 +161,13 @@
     return result
 
 
-def operator_kernel(slot_ref, pot_ref, kinetic_ref, ops_ref, pot_out_ref):
-    width = kinetic_ref.shape[0]
-    slot_row = slot_ref[0]
+def build_operator(slot_row, pot_row, kinetic):
+    width = kinetic.shape[0]
     picks = (lax.broadcasted_iota(jnp.int32, (width, width), 0) == slot_row).astype(jnp.bfloat16)
-    kinetic = kinetic_ref[...]
     columns = lax.dot_general(
         kinetic, picks, (((1,), (1,)), ((), ())), preferred_element_type=jnp.float32
     ).astype(jnp.bfloat16)
-    ops_ref[0] = jnp.dot(picks, columns, preferred_element_type=jnp.float32).astype(ops_ref.dtype)
-    pot_row = pot_ref[0]
+    ops = jnp.dot(picks, columns, preferred_element_type=jnp.float32).astype(jnp.bfloat16)
     high = pot_row.astype(jnp.bfloat16)
     rest = pot_row - high.astype(jnp.float32)
     middle = rest.astype(jnp.bfloat16)
@@ -162,32 +178,7 @@
     moved = lax.dot_general(
         parts, picks, (((1,), (1,)), ((), ())), preferred_element_type=jnp.float32
     )
-    pot_out_ref[0] = moved[0:1] + moved[1:2] + moved[2:3]
-
-
-def cell_operators(slots, potential, kinetic, cols):
-    cells, width = slots.shape
-    return pl.pallas_call(
-        operator_kernel,
-        grid=(cells,),
-        in_specs=[
-            pl.BlockSpec((1, 1, width), lambda c: (c, 0, 0)),
-            pl.BlockSpec((1, 1, width), lambda c: (c, 0, 0)),
-            pl.BlockSpec(memory_space=pltpu.VMEM),
-        ],
-        out_specs=[
-            pl.BlockSpec((1, width, width), lambda c: (c, 0, 0)),
-            pl.BlockSpec((1, 1, width), lambda c: (c, 0, 0)),
-        ],
-        out_shape=[
-            jax.ShapeDtypeStruct((cells, width, width), jnp.bfloat16),
-            jax.ShapeDtypeStruct((cells, 1, width), jnp.float32),
-        ],
-        compiler_params=pltpu.CompilerParams(dimension_semantics=("arbitrary",)),
-        cost_estimate=pl.CostEstimate(
-            flops=4 * cells * width * width * width, transcendentals=0,
-            bytes_accessed=cells * width * (width * 2 + 12)),
-    )(slots.reshape(cells, 1, width), potential.reshape(cells, 1, width), kinetic)
+    return ops, moved[0:1] + moved[1:2] + moved[2:3]
 
 
 def newton(gram_matrix):
@@ -243,9 +234,8 @@
     slots = (connectivity - starts[:, None]) % node_total
     alive = (jnp.arange(cells) < live_count).astype(jnp.float32)
     scales = cell_scale * alive
-    window_ops, window_pot = cell_operators(
-        slots, cell_potential * alive[:, None], cell_kinetic, state_cols
-    )
+    slot_rows = slots.reshape(cells, 1, width)
+    potential_rows = (cell_potential * alive[:, None]).reshape(cells, 1, width)
     up = [(i, i + 1) for i in range(domains - 1)]
     down = [(j, i) for i, j in up]
 
@@ -254,9 +244,11 @@
         from_right = lax.ppermute(face_values[:face_width], "dom", down)
         return jnp.concatenate([from_left, from_right], axis=0)
 
+    first = states.T
+    local_sum, face_values, window_ops, window_pot = field_step(
+        faces, scales, slot_rows, potential_rows, vector=first, kinetic=cell_kinetic
+    )
     step = functools.partial(field_step, faces, scales, window_ops, window_pot)
-    first = states.T
-    local_sum, face_values = step(vector=first)
     second, local_sum, face_values = step(local_in=local_sum, received=exchange(face_values))
     history = [first, second]
     for repeat in range(CHEB - 2):

time: 381 us -> 366 us (0.961)
  Pallas kernels: 194 us -> 180 us
    pallas_call x1 -> x0, Pallas kernels: 31.4 us -> none  [cell_operators(): pl.pallas_call(operator_kernel, grid=(cells,), in_specs=[pl.BlockSpec((1,...]
    pallas_call x5, Pallas kernels: 163 us -> 180 us  [field_step(): pl.pallas_call(functools.partial(field_kernel, combine, has_older, apply,...]
where the time goes in v3:
time: 366 us; the launch traced here: 364 us
  Pallas kernels  180 us (49%)
  waiting for transfers between devices  83.2 us (23%)
  starting transfers between devices  42.6 us (12%)
  local copies, waits for them, and re-layouts  25.1 us (7%)
  blocking collectives  16.9 us (5%)
  other arithmetic  8.13 us (2%)
  matrix products  6.39 us (2%)
    pallas_call x5, Pallas kernels, field_step(): pl.pallas_call(functools.partial(field_kernel, combine, has_older, apply,...  180 us
    ppermute x7, waiting for transfers between devices, doubling_sum(): total = total + lax.ppermute(total, ('dom', 'band'), pairs)  45.5 us
    ppermute x4, starting transfers between devices, exchange(): from_left = lax.ppermute(face_values[face_width:], 'dom', up)  19.6 us
    all_to_all x1, blocking collectives, body(): lax.all_to_all(rotated, 'band', split_axis=1, concat_axis=0, tiled=True)  16.9 us
    ppermute x4, waiting for transfers between devices, exchange(): from_left = lax.ppermute(face_values[face_width:], 'dom', up)  13.5 us
    ppermute x4, waiting for transfers between devices, exchange(): from_right = lax.ppermute(face_values[:face_width], 'dom', down)  13.2 us
    all_to_all x1, waiting for transfers between devices, body(): lax.all_to_all(current, 'band', split_axis=0, concat_axis=1, tiled=True)  11.1 us
    ppermute x4, starting transfers between devices, exchange(): from_right = lax.ppermute(face_values[:face_width], 'dom', down)  9.4 us
  transfers between devices with their start and end apart: 16, of which 16 were waited for; matrix products, arithmetic and copies ran while one was open for 2% of the time, Pallas kernels for 0%

profile of v3, /device:TPU:6, one launch (start us, length us, event | category | flops | bytes accessed | tf_op | source)
XLA Modules:
  0.0 364.2 jit_solution(549268406811013114)
XLA Ops:
  4.6 4.1 %copy.10 = bf16[64,12288]{0,1:T(8,128)(2,1)} copy(bf16[64,12288]{1,0:T(8,128)(2,1)} %param.7) | data formatting | bytes 3145728 | tf_op args[0]
  9.9 48.1 %shard_map.73 = (f32[12288,64]{1,0:T(8,128)}, f32[2048,64]{1,0:T(8,128)}, bf16[32,512,512]{2,1,0:T(8,128)(2,1)}, f32[32,1,512]{2,1,0:T(1,128)}) custom-call(s32[2048]{0:T(1024)} %pad_add_fusion.refs_0_, f32[32]{0:T(128)} %compare_select_fusion.1.refs_1_, bf16[12288,64]{1,0:T(8,128)(2,1)} %bitcast.55, s32[32,1,512]{2,1,0:T(1,128)} %reshape.113.refs_3_, ...), custom_call_target="tpu_custom_call" | custom-call | flops 18253611008 | bytes 26214400 | tf_op jit(solution)/shard_map/pallas_call | solution.py:148
  59.3 1.9 collective-permute-start
  61.2 3.6 %collective-permute-start.1 = (f32[1024,64]{1,0:T(8,128)S(1)}, f32[1024,64]{1,0:T(8,128)S(1)}, u32[]{:S(2)}, u32[]{:S(2)}) collective-permute-start(f32[1024,64]{1,0:T(8,128)S(1)} %get-tuple-element.38), channel_id=1, source_target_pairs={{4,0},{8,4},{12,8},{16,12},{20,16},{24,20},{28,24},{32,28},{36,32}... | collective-permute-start | bytes 786440 | tf_op jit(solution)/shard_map/ppermute | solution.py:244
  64.9 4.9 %collective-permute-done = f32[1024,64]{1,0:T(8,128)S(1)} collective-permute-done((f32[1024,64]{1,0:T(8,128)S(1)}, f32[1024,64]{1,0:T(8,128)S(1)}, u32[]{:S(2)}, u32[]{:S(2)}) %collective-permute-start) | collective-permute-done | bytes 262176 | tf_op jit(solution)/shard_map/ppermute | solution.py:243
  72.6 39.4 %shard_map.74 = (bf16[12288,64]{1,0:T(8,128)(2,1)}, f32[12288,64]{1,0:T(8,128)}, f32[2048,64]{1,0:T(8,128)}) custom-call(s32[2048]{0:T(1024)} %pad_add_fusion.refs_0_, f32[32]{0:T(128)} %compare_select_fusion.1.refs_1_, f32[12288,64]{1,0:T(8,128)} %get-tuple-element.17.refs_2_, f32[2048,64]{1,0:T(8,128)} %pad_maximum_fusion.refs_3_, ...), custom_call_target="tpu_custom_call" | custom-call | flops 1073741824 | bytes 26214400 | tf_op jit(solution)/shard_map/pallas_call | solution.py:148
  113.2 5.8 %collective-permute-start.2 = (f32[1024,64]{1,0:T(8,128)S(1)}, f32[1024,64]{1,0:T(8,128)S(1)}, u32[]{:S(2)}, u32[]{:S(2)}) collective-permute-start(f32[1024,64]{1,0:T(8,128)S(1)} %get-tuple-element.35), channel_id=1, source_target_pairs={{0,4},{4,8},{8,12},{12,16},{16,20},{20,24},{24,28},{28,32},{32,36}... | collective-permute-start | bytes 786440 | tf_op jit(solution)/shard_map/ppermute | solution.py:243
  119.0 1.9 collective-permute-start.3
  120.9 3.0 collective-permute-done.2
  123.9 3.7 %collective-permute-done.3 = f32[1024,64]{1,0:T(8,128)S(1)} collective-permute-done((f32[1024,64]{1,0:T(8,128)S(1)}, f32[1024,64]{1,0:T(8,128)S(1)}, u32[]{:S(2)}, u32[]{:S(2)}) %collective-permute-start.3) | collective-permute-done | bytes 262176 | tf_op jit(solution)/shard_map/ppermute | solution.py:244
  128.7 40.2 %shard_map.75 = (bf16[12288,64]{1,0:T(8,128)(2,1)}, f32[12288,64]{1,0:T(8,128)}, f32[2048,64]{1,0:T(8,128)}) custom-call(s32[2048]{0:T(1024)} %pad_add_fusion.refs_0_, f32[32]{0:T(128)} %compare_select_fusion.1.refs_1_, f32[12288,64]{1,0:T(8,128)} %get-tuple-element.21.refs_2_, f32[2048,64]{1,0:T(8,128)} %pad_maximum_fusion.1.refs_3_, ...), custom_call_target="tpu_custom_call" | custom-call | flops 1073741824 | bytes 26214400 | tf_op jit(solution)/shard_map/pallas_call | solution.py:148
  170.1 5.9 %collective-permute-start.4 = (f32[1024,64]{1,0:T(8,128)S(1)}, f32[1024,64]{1,0:T(8,128)S(1)}, u32[]{:S(2)}, u32[]{:S(2)}) collective-permute-start(f32[1024,64]{1,0:T(8,128)S(1)} %get-tuple-element.33), channel_id=1, source_target_pairs={{0,4},{4,8},{8,12},{12,16},{16,20},{20,24},{24,28},{28,32},{32,36}... | collective-permute-start | bytes 786440 | tf_op jit(solution)/shard_map/ppermute | solution.py:243
  178.0 2.8 collective-permute-done.4
  180.8 3.9 %collective-permute-done.5 = f32[1024,64]{1,0:T(8,128)S(1)} collective-permute-done((f32[1024,64]{1,0:T(8,128)S(1)}, f32[1024,64]{1,0:T(8,128)S(1)}, u32[]{:S(2)}, u32[]{:S(2)}) %collective-permute-start.5) | collective-permute-done | bytes 262176 | tf_op jit(solution)/shard_map/ppermute | solution.py:244
  185.7 40.2 %shard_map.76 = (bf16[12288,64]{1,0:T(8,128)(2,1)}, f32[12288,64]{1,0:T(8,128)}, f32[2048,64]{1,0:T(8,128)}) custom-call(s32[2048]{0:T(1024)} %pad_add_fusion.refs_0_, f32[32]{0:T(128)} %compare_select_fusion.1.refs_1_, f32[12288,64]{1,0:T(8,128)} %get-tuple-element.23.refs_2_, f32[2048,64]{1,0:T(8,128)} %pad_maximum_fusion.2.refs_3_, ...), custom_call_target="tpu_custom_call" | custom-call | flops 1073741824 | bytes 26214400 | tf_op jit(solution)/shard_map/pallas_call | solution.py:148
  227.2 5.9 %collective-permute-start.6 = (f32[1024,64]{1,0:T(8,128)S(1)}, f32[1024,64]{1,0:T(8,128)S(1)}, u32[]{:S(2)}, u32[]{:S(2)}) collective-permute-start(f32[1024,64]{1,0:T(8,128)S(1)} %get-tuple-element.31), channel_id=1, source_target_pairs={{0,4},{4,8},{8,12},{12,16},{16,20},{20,24},{24,28},{28,32},{32,36}... | collective-permute-start | bytes 786440 | tf_op jit(solution)/shard_map/ppermute | solution.py:243
  235.1 2.8 collective-permute-done.6
  237.9 3.9 %collective-permute-done.7 = f32[1024,64]{1,0:T(8,128)S(1)} collective-permute-done((f32[1024,64]{1,0:T(8,128)S(1)}, f32[1024,64]{1,0:T(8,128)S(1)}, u32[]{:S(2)}, u32[]{:S(2)}) %collective-permute-start.7) | collective-permute-done | bytes 262176 | tf_op jit(solution)/shard_map/ppermute | solution.py:244
  242.8 12.2 %shard_map.77 = bf16[12288,64]{1,0:T(8,128)(2,1)} custom-call(s32[2048]{0:T(1024)} %pad_add_fusion.refs_0_, f32[12288,64]{1,0:T(8,128)} %get-tuple-element.26.refs_1_, f32[2048,64]{1,0:T(8,128)} %pad_maximum_fusion.3.refs_2_, bf16[12288,64]{1,0:T(8,128)(2,1)} %get-tuple-element.28.refs_3_), custom_call_target="tpu_custom_call" | custom-call | bytes 9437184 | tf_op jit(solution)/shard_map/pallas_call | solution.py:148
  255.0 4.3 %copy.11 = bf16[4,3072,64]{1,2,0:T(8,128)(2,1)} copy(bf16[4,3072,64]{2,1,0:T(8,128)(2,1)} %bitcast.54) | data formatting | bytes 3145728 | tf_op jit(solution)/shard_map/all_to_all | solution.py:263
  259.3 5.3 %all-to-all-start = ((bf16[4,3072,64]{1,2,0:T(8,128)(2,1)}), bf16[4,3072,64]{1,2,0:T(8,128)(2,1)S(1)}, u32[]{:S(2)}, u32[]{:S(2)}) async-start(bf16[4,3072,64]{1,2,0:T(8,128)(2,1)} %copy.11), calls=%async_computation | async-start | bytes 3145728 | tf_op jit(solution)/shard_map/all_to_all | solution.py:263
  264.7 8.2 %scatter_custom_fusion = f32[12288]{0:T(1024)S(1)} fusion(s32[2048]{0:T(1024)S(1)} %bitcast.62, f32[2048]{0:T(1024)S(1)} %add_divide_fusion, f32[]{:T(128)} %constant.17.clone.1), kind=kCustom, calls=%fused_computation.27 | custom fusion | bytes 49156 | tf_op jit(solution)/shard_map/scatter | solution.py:229
  272.9 11.1 %all-to-all-done = bf16[4,3072,64]{1,2,0:T(8,128)(2,1)S(1)} async-done(((bf16[4,3072,64]{1,2,0:T(8,128)(2,1)}), bf16[4,3072,64]{1,2,0:T(8,128)(2,1)S(1)}, u32[]{:S(2)}, u32[]{:S(2)}) %all-to-all-start) | async-done | bytes 1572896 | tf_op jit(solution)/shard_map/all_to_all | solution.py:263
  284.7 2.7 collective-permute-start.8
  289.2 8.0 %collective-permute-done.9 = f32[256,256]{1,0:T(8,128)S(1)} collective-permute-done((f32[256,256]{1,0:T(8,128)S(1)}, f32[256,256]{1,0:T(8,128)S(1)}, u32[]{:S(2)}, u32[]{:S(2)}) %collective-permute-start.9) | collective-permute-done | bytes 262176 | tf_op jit(solution)/shard_map/ppermute | solution.py:207
  298.3 8.3 %collective-permute-done.10 = f32[256,256]{1,0:T(8,128)S(1)} collective-permute-done((f32[256,256]{1,0:T(8,128)S(1)}, f32[256,256]{1,0:T(8,128)S(1)}, u32[]{:S(2)}, u32[]{:S(2)}) %collective-permute-start.10) | collective-permute-done | bytes 262176 | tf_op jit(solution)/shard_map/ppermute | solution.py:207
  306.7 7.5 %collective-permute-done.11 = f32[256,256]{1,0:T(8,128)S(1)} collective-permute-done((f32[256,256]{1,0:T(8,128)S(1)}, f32[256,256]{1,0:T(8,128)S(1)}, u32[]{:S(2)}, u32[]{:S(2)}) %collective-permute-start.11) | collective-permute-done | bytes 262176 | tf_op jit(solution)/shard_map/ppermute | solution.py:207
  314.4 7.9 %collective-permute-done.12 = f32[256,256]{1,0:T(8,128)S(1)} collective-permute-done((f32[256,256]{1,0:T(8,128)S(1)}, f32[256,256]{1,0:T(8,128)S(1)}, u32[]{:S(2)}, u32[]{:S(2)}) %collective-permute-start.12) | collective-permute-done | bytes 262176 | tf_op jit(solution)/shard_map/ppermute | solution.py:207
  323.8 7.0 %collective-permute-done.13 = f32[256,256]{1,0:T(8,128)S(1)} collective-permute-done((f32[256,256]{1,0:T(8,128)S(1)}, f32[256,256]{1,0:T(8,128)S(1)}, u32[]{:S(2)}, u32[]{:S(2)}) %collective-permute-start.13) | collective-permute-done | bytes 262176 | tf_op jit(solution)/shard_map/ppermute | solution.py:207
  330.8 2.4 collective-permute-start.14
  333.2 5.6 %collective-permute-done.14 = f32[256,256]{1,0:T(8,128)S(1)} collective-permute-done((f32[256,256]{1,0:T(8,128)S(1)}, f32[256,256]{1,0:T(8,128)S(1)}, u32[]{:S(2)}, u32[]{:S(2)}) %collective-permute-start.14) | collective-permute-done | bytes 262176 | tf_op jit(solution)/shard_map/ppermute | solution.py:207
  346.0 16.9 %all_to_all.38 = bf16[3072,4,64]{0,2,1:T(8,128)(2,1)S(1)} all-to-all(bf16[3072,4,64]{0,2,1:T(8,128)(2,1)S(1)} %bitcast.57), channel_id=1, replica_groups=mesh['dom'=32,'band'=4] {'band'}, dimensions={1} | all-to-all | bytes 3145728 | tf_op jit(solution)/shard_map/all_to_all | solution.py:277
  (57 shorter events, 33.0 us)
Async XLA Ops:
  4.6 4.1 %copy-start = (f32[32]{0:T(128)S(1)}, f32[32]{0:T(128)}, u32[]{:S(2)}) copy-start(f32[32]{0:T(128)} %param.9) | copy-start | bytes 388
  59.3 10.5 %collective-permute-start = (f32[1024,64]{1,0:T(8,128)S(1)}, f32[1024,64]{1,0:T(8,128)S(1)}, u32[]{:S(2)}, u32[]{:S(2)}) collective-permute-start(f32[1024,64]{1,0:T(8,128)S(1)} %get-tuple-element.37), channel_id=1, source_target_pairs={{0,4},{4,8},{8,12},{12,16},{16,20},{20,24},{24,28},{28,32},{32,36}... | collective-permute-start | bytes 786440 | tf_op jit(solution)/shard_map/ppermute | solution.py:243
  61.2 10.3 %collective-permute-start.1 = (f32[1024,64]{1,0:T(8,128)S(1)}, f32[1024,64]{1,0:T(8,128)S(1)}, u32[]{:S(2)}, u32[]{:S(2)}) collective-permute-start(f32[1024,64]{1,0:T(8,128)S(1)} %get-tuple-element.38), channel_id=1, source_target_pairs={{4,0},{8,4},{12,8},{16,12},{20,16},{24,20},{28,24},{32,28},{36,32}... | collective-permute-start | bytes 786440 | tf_op jit(solution)/shard_map/ppermute | solution.py:244
  113.2 10.7 %collective-permute-start.2 = (f32[1024,64]{1,0:T(8,128)S(1)}, f32[1024,64]{1,0:T(8,128)S(1)}, u32[]{:S(2)}, u32[]{:S(2)}) collective-permute-start(f32[1024,64]{1,0:T(8,128)S(1)} %get-tuple-element.35), channel_id=1, source_target_pairs={{0,4},{4,8},{8,12},{12,16},{16,20},{20,24},{24,28},{28,32},{32,36}... | collective-permute-start | bytes 786440 | tf_op jit(solution)/shard_map/ppermute | solution.py:243
  119.0 8.6 %collective-permute-start.3 = (f32[1024,64]{1,0:T(8,128)S(1)}, f32[1024,64]{1,0:T(8,128)S(1)}, u32[]{:S(2)}, u32[]{:S(2)}) collective-permute-start(f32[1024,64]{1,0:T(8,128)S(1)} %get-tuple-element.36), channel_id=1, source_target_pairs={{4,0},{8,4},{12,8},{16,12},{20,16},{24,20},{28,24},{32,28},{36,32}... | collective-permute-start | bytes 786440 | tf_op jit(solution)/shard_map/ppermute | solution.py:244
  170.1 10.7 %collective-permute-start.4 = (f32[1024,64]{1,0:T(8,128)S(1)}, f32[1024,64]{1,0:T(8,128)S(1)}, u32[]{:S(2)}, u32[]{:S(2)}) collective-permute-start(f32[1024,64]{1,0:T(8,128)S(1)} %get-tuple-element.33), channel_id=1, source_target_pairs={{0,4},{4,8},{8,12},{12,16},{16,20},{20,24},{24,28},{28,32},{32,36}... | collective-permute-start | bytes 786440 | tf_op jit(solution)/shard_map/ppermute | solution.py:243
  176.1 8.6 %collective-permute-start.5 = (f32[1024,64]{1,0:T(8,128)S(1)}, f32[1024,64]{1,0:T(8,128)S(1)}, u32[]{:S(2)}, u32[]{:S(2)}) collective-permute-start(f32[1024,64]{1,0:T(8,128)S(1)} %get-tuple-element.34), channel_id=1, source_target_pairs={{4,0},{8,4},{12,8},{16,12},{20,16},{24,20},{28,24},{32,28},{36,32}... | collective-permute-start | bytes 786440 | tf_op jit(solution)/shard_map/ppermute | solution.py:244
  227.2 10.7 %collective-permute-start.6 = (f32[1024,64]{1,0:T(8,128)S(1)}, f32[1024,64]{1,0:T(8,128)S(1)}, u32[]{:S(2)}, u32[]{:S(2)}) collective-permute-start(f32[1024,64]{1,0:T(8,128)S(1)} %get-tuple-element.31), channel_id=1, source_target_pairs={{0,4},{4,8},{8,12},{12,16},{16,20},{20,24},{24,28},{28,32},{32,36}... | collective-permute-start | bytes 786440 | tf_op jit(solution)/shard_map/ppermute | solution.py:243
  233.2 8.6 %collective-permute-start.7 = (f32[1024,64]{1,0:T(8,128)S(1)}, f32[1024,64]{1,0:T(8,128)S(1)}, u32[]{:S(2)}, u32[]{:S(2)}) collective-permute-start(f32[1024,64]{1,0:T(8,128)S(1)} %get-tuple-element.32), channel_id=1, source_target_pairs={{4,0},{8,4},{12,8},{16,12},{20,16},{24,20},{28,24},{32,28},{36,32}... | collective-permute-start | bytes 786440 | tf_op jit(solution)/shard_map/ppermute | solution.py:244
  259.3 24.7 %all-to-all-start = ((bf16[4,3072,64]{1,2,0:T(8,128)(2,1)}), bf16[4,3072,64]{1,2,0:T(8,128)(2,1)S(1)}, u32[]{:S(2)}, u32[]{:S(2)}) async-start(bf16[4,3072,64]{1,2,0:T(8,128)(2,1)} %copy.11), calls=%async_computation | async-start | bytes 3145728 | tf_op jit(solution)/shard_map/all_to_all | solution.py:263
  284.7 3.8 %collective-permute-start.8 = (f32[256,256]{1,0:T(8,128)S(1)}, f32[256,256]{1,0:T(8,128)S(1)}, u32[]{:S(2)}, u32[]{:S(2)}) collective-permute-start(f32[256,256]{1,0:T(8,128)S(1)} %fusion.13), channel_id=1, source_target_pairs={{0,4},{1,5},{2,6},{3,7},{4,0},{5,1},{6,2},{7,3},{8,12},{9,13},{10,... | collective-permute-start | bytes 786440 | tf_op jit(solution)/shard_map/ppermute | solution.py:207
  288.6 8.7 %collective-permute-start.9 = (f32[256,256]{1,0:T(8,128)S(1)}, f32[256,256]{1,0:T(8,128)S(1)}, u32[]{:S(2)}, u32[]{:S(2)}) collective-permute-start(f32[256,256]{1,0:T(8,128)S(1)} %add.53), channel_id=1, source_target_pairs={{0,1},{1,0},{2,3},{3,2},{4,5},{5,4},{6,7},{7,6},{8,9},{9,8},{10,11... | collective-permute-start | bytes 786440 | tf_op jit(solution)/shard_map/ppermute | solution.py:207
  297.3 9.3 %collective-permute-start.10 = (f32[256,256]{1,0:T(8,128)S(1)}, f32[256,256]{1,0:T(8,128)S(1)}, u32[]{:S(2)}, u32[]{:S(2)}) collective-permute-start(f32[256,256]{1,0:T(8,128)S(1)} %add.54), channel_id=1, source_target_pairs={{0,2},{1,3},{2,0},{3,1},{4,6},{5,7},{6,4},{7,5},{8,10},{9,11},{10,... | collective-permute-start | bytes 786440 | tf_op jit(solution)/shard_map/ppermute | solution.py:207
  306.6 7.6 %collective-permute-start.11 = (f32[256,256]{1,0:T(8,128)S(1)}, f32[256,256]{1,0:T(8,128)S(1)}, u32[]{:S(2)}, u32[]{:S(2)}) collective-permute-start(f32[256,256]{1,0:T(8,128)S(1)} %add.55), channel_id=1, source_target_pairs={{0,8},{1,9},{2,10},{3,11},{4,12},{5,13},{6,14},{7,15},{8,0},{9,1},... | collective-permute-start | bytes 786440 | tf_op jit(solution)/shard_map/ppermute | solution.py:207
  314.3 8.0 %collective-permute-start.12 = (f32[256,256]{1,0:T(8,128)S(1)}, f32[256,256]{1,0:T(8,128)S(1)}, u32[]{:S(2)}, u32[]{:S(2)}) collective-permute-start(f32[256,256]{1,0:T(8,128)S(1)} %add.56), channel_id=1, source_target_pairs={{0,16},{1,17},{2,18},{3,19},{4,20},{5,21},{6,22},{7,23},{8,24},{9,... | collective-permute-start | bytes 786440 | tf_op jit(solution)/shard_map/ppermute | solution.py:207
  322.3 8.5 %collective-permute-start.13 = (f32[256,256]{1,0:T(8,128)S(1)}, f32[256,256]{1,0:T(8,128)S(1)}, u32[]{:S(2)}, u32[]{:S(2)}) collective-permute-start(f32[256,256]{1,0:T(8,128)S(1)} %add.57), channel_id=1, source_target_pairs={{0,32},{1,33},{2,34},{3,35},{4,36},{5,37},{6,38},{7,39},{8,40},{9,... | collective-permute-start | bytes 786440 | tf_op jit(solution)/shard_map/ppermute | solution.py:207
  330.8 8.0 %collective-permute-start.14 = (f32[256,256]{1,0:T(8,128)S(1)}, f32[256,256]{1,0:T(8,128)S(1)}, u32[]{:S(2)}, u32[]{:S(2)}) collective-permute-start(f32[256,256]{1,0:T(8,128)S(1)} %add.58), channel_id=1, source_target_pairs={{0,64},{1,65},{2,66},{3,67},{4,68},{5,69},{6,70},{7,71},{8,72},{9,... | collective-permute-start | bytes 786440 | tf_op jit(solution)/shard_map/ppermute | solution.py:207

commit v4 on v3

--- a/solution.py
+++ b/solution.py
@@ -21,7 +21,7 @@
         scales = refs.pop(0)
     if combine:
         local_in = refs.pop(0)
-        received = refs.pop(0)
+        received = (refs.pop(0), refs.pop(0))
         if older:
             older_ref = refs.pop(0)
     else:
@@ -35,27 +35,28 @@
         vector_out = refs.pop(0)
     if apply:
         local_out = refs.pop(0)
-        faces_out = refs.pop(0)
+        faces_out = (refs.pop(0), refs.pop(0))
         if build:
             ops_out = refs.pop(0)
             pot_out = refs.pop(0)
     if combine:
         work = refs.pop(0)
     vector = vector_out if combine else vector_in
-    face_total = faces.shape[0]
+    face_half = faces.shape[0] // 2
     node_total = vector.shape[0]
     cell = pl.program_id(0) if apply else None
 
     def prologue():
         work[...] = local_in[...] if alpha == 1.0 else alpha * local_in[...]
 
-        def fix(p, carry):
-            n = faces[p]
-            row = received[pl.ds(p, 1), :]
-            work[pl.ds(n, 1), :] += row if alpha == 1.0 else alpha * row
-            return carry
-
-        lax.fori_loop(0, face_total, fix, 0, unroll=8)
+        for side in range(2):
+            def fix(p, carry):
+                n = faces[side * face_half + p]
+                row = received[side][pl.ds(p, 1), :]
+                work[pl.ds(n, 1), :] += row if alpha == 1.0 else alpha * row
+                return carry
+
+            lax.fori_loop(0, face_half, fix, 0, unroll=8)
         value = work[...]
         if older:
             value = value - older_ref[...].astype(jnp.float32)
@@ -98,12 +99,13 @@
 
         @pl.when(cell == pl.num_programs(0) - 1)
         def _():
-            def pick(p, carry):
-                n = faces[p]
-                faces_out[pl.ds(p, 1), :] = local_out[pl.ds(n, 1), :]
-                return carry
-
-            lax.fori_loop(0, face_total, pick, 0, unroll=8)
+            for side in range(2):
+                def pick(p, carry):
+                    n = faces[side * face_half + p]
+                    faces_out[side][pl.ds(p, 1), :] = local_out[pl.ds(n, 1), :]
+                    return carry
+
+                lax.fori_loop(0, face_half, pick, 0, unroll=8)
 
 
 def field_step(faces, scales, window_ops, window_pot, vector=None, local_in=None,
@@ -112,7 +114,7 @@
     has_older = older is not None
     build = kinetic is not None
     node_total, cols = (local_in if combine else vector).shape
-    face_total = faces.shape[0]
+    face_half = faces.shape[0] // 2
     cells, width = window_pot.shape[0], window_pot.shape[-1]
     smem = pl.BlockSpec(memory_space=pltpu.SMEM)
     whole = pl.BlockSpec(memory_space=pltpu.VMEM)
@@ -120,7 +122,7 @@
     if apply:
         args.append(scales); specs.append(smem)
     if combine:
-        args += [local_in, received]; specs += [whole, whole]
+        args += [local_in, *received]; specs += [whole, whole, whole]
         if has_older:
             args.append(older); specs.append(whole)
     else:
@@ -137,8 +139,9 @@
         out_shape.append(jax.ShapeDtypeStruct((node_total, cols), jnp.bfloat16)); out_specs.append(whole)
     if apply:
         out_shape += [jax.ShapeDtypeStruct((node_total, cols), jnp.float32),
-                      jax.ShapeDtypeStruct((face_total, cols), jnp.float32)]
-        out_specs += [whole, whole]
+                      jax.ShapeDtypeStruct((face_half, cols), jnp.float32),
+                      jax.ShapeDtypeStruct((face_half, cols), jnp.float32)]
+        out_specs += [whole, whole, whole]
         if build:
             out_shape += [jax.ShapeDtypeStruct((cells, width, width), jnp.bfloat16),
                           jax.ShapeDtypeStruct((cells, 1, width), jnp.float32)]
@@ -239,25 +242,25 @@
     up = [(i, i + 1) for i in range(domains - 1)]
     down = [(j, i) for i, j in up]
 
-    def exchange(face_values):
-        from_left = lax.ppermute(face_values[face_width:], "dom", up)
-        from_right = lax.ppermute(face_values[:face_width], "dom", down)
-        return jnp.concatenate([from_left, from_right], axis=0)
+    def exchange(left_values, right_values):
+        from_left = lax.ppermute(right_values, "dom", up)
+        from_right = lax.ppermute(left_values, "dom", down)
+        return (from_left, from_right)
 
     first = states.T
-    local_sum, face_values, window_ops, window_pot = field_step(
+    local_sum, *face_values, window_ops, window_pot = field_step(
         faces, scales, slot_rows, potential_rows, vector=first, kinetic=cell_kinetic
     )
     step = functools.partial(field_step, faces, scales, window_ops, window_pot)
-    second, local_sum, face_values = step(local_in=local_sum, received=exchange(face_values))
+    second, local_sum, *face_values = step(local_in=local_sum, received=exchange(*face_values))
     history = [first, second]
     for repeat in range(CHEB - 2):
-        following, local_sum, face_values = step(
-            local_in=local_sum, received=exchange(face_values), older=history[-2], alpha=2.0
+        following, local_sum, *face_values = step(
+            local_in=local_sum, received=exchange(*face_values), older=history[-2], alpha=2.0
         )
         history.append(following)
     (current,) = step(
-        local_in=local_sum, received=exchange(face_values), older=history[-2], alpha=2.0,
+        local_in=local_sum, received=exchange(*face_values), older=history[-2], alpha=2.0,
         apply=False,
     )
     row_shard = lax.all_to_all(current, "band", split_axis=0, concat_axis=1, tiled=True)

time: 366 us -> 365 us (level)
  other arithmetic: 8.13 us -> 3.97 us
  Pallas kernels: 180 us -> 184 us
    slice x4 -> x0, local copies, waits for them, and re-layouts: 5.07 us -> none  [exchange(): from_left = lax.ppermute(face_values[face_width:], 'dom', up)]
    concatenate x4 -> x0, other arithmetic: 4.16 us -> none  [exchange(): return jnp.concatenate([from_left, from_right], axis=0)]
    unnamed x3 -> x19, local copies, waits for them, and re-layouts: 4.14 us -> 7.33 us
where the time goes in v4:
time: 365 us; the launch traced here: 363 us
  Pallas kernels  184 us (50%)
  waiting for transfers between devices  84 us (23%)
  starting transfers between devices  43.1 us (12%)
  local copies, waits for them, and re-layouts  23.1 us (6%)
  blocking collectives  17.3 us (5%)
  matrix products  6.39 us (2%)
  other arithmetic  3.97 us (1%)
    pallas_call x5, Pallas kernels, field_step(): pl.pallas_call(functools.partial(field_kernel, combine, has_older, apply,...  184 us
    ppermute x7, waiting for transfers between devices, doubling_sum(): total = total + lax.ppermute(total, ('dom', 'band'), pairs)  44.7 us
    ppermute x4, starting transfers between devices, exchange(): from_left = lax.ppermute(right_values, 'dom', up)  19.3 us
    all_to_all x1, blocking collectives, body(): lax.all_to_all(rotated, 'band', split_axis=1, concat_axis=0, tiled=True)  17.3 us
    ppermute x4, waiting for transfers between devices, exchange(): from_left = lax.ppermute(right_values, 'dom', up)  14.3 us
    ppermute x4, waiting for transfers between devices, exchange(): from_right = lax.ppermute(left_values, 'dom', down)  13.6 us
    all_to_all x1, waiting for transfers between devices, body(): lax.all_to_all(current, 'band', split_axis=0, concat_axis=1, tiled=True)  11.3 us
    ppermute x4, starting transfers between devices, exchange(): from_right = lax.ppermute(left_values, 'dom', down)  9.32 us
  transfers between devices with their start and end apart: 16, of which 16 were waited for; matrix products, arithmetic and copies ran while one was open for 2% of the time, Pallas kernels for 0%

profile of v4, /device:TPU:6, one launch (start us, length us, event | category | flops | bytes accessed | tf_op | source)
XLA Modules:
  0.0 363.2 jit_solution(2434916777874172682)
XLA Ops:
  4.7 4.2 %copy.10 = bf16[64,12288]{0,1:T(8,128)(2,1)} copy(bf16[64,12288]{1,0:T(8,128)(2,1)} %param.7) | data formatting | bytes 3145728 | tf_op args[0]
  9.9 48.2 %shard_map.73 = (f32[12288,64]{1,0:T(8,128)}, f32[1024,64]{1,0:T(8,128)}, f32[1024,64]{1,0:T(8,128)}, bf16[32,512,512]{2,1,0:T(8,128)(2,1)}, f32[32,1,512]{2,1,0:T(1,128)}) custom-call(s32[2048]{0:T(1024)} %pad_add_fusion.refs_0_, f32[32]{0:T(128)} %compare_select_fusion.1.refs_1_, bf16[12288,64]{1,0:T(8,128)(2,1)} %bitcast.55, ...), custom_call_target="tpu_custom_call" | custom-call | flops 18253611008 | bytes 26214400 | tf_op jit(solution)/shard_map/pallas_call | solution.py:151
  58.1 2.0 collective-permute-start
  60.1 3.6 collective-permute-start.1
  63.7 5.1 %collective-permute-done.refs_3_ = f32[1024,64]{1,0:T(8,128)S(1)} collective-permute-done((f32[1024,64]{1,0:T(8,128)}, f32[1024,64]{1,0:T(8,128)S(1)}, u32[]{:S(2)}, u32[]{:S(2)}) %collective-permute-start) | collective-permute-done | bytes 262176 | tf_op jit(solution)/shard_map/ppermute | solution.py:246
  71.5 40.1 %shard_map.74 = (bf16[12288,64]{1,0:T(8,128)(2,1)}, f32[12288,64]{1,0:T(8,128)}, f32[1024,64]{1,0:T(8,128)}, f32[1024,64]{1,0:T(8,128)}) custom-call(s32[2048]{0:T(1024)} %pad_add_fusion.refs_0_, f32[32]{0:T(128)} %compare_select_fusion.1.refs_1_, f32[12288,64]{1,0:T(8,128)} %get-tuple-element.21.refs_2_, f32[1024,64]{1,0:T(8,128)} %copy-done.2, ...), custom_call_target="tpu_custom_call" | custom-call | flops 1073741824 | bytes 26214400 | tf_op jit(solution)/shard_map/pallas_call | solution.py:151
  111.6 5.7 %collective-permute-start.2 = (f32[1024,64]{1,0:T(8,128)}, f32[1024,64]{1,0:T(8,128)S(1)}, u32[]{:S(2)}, u32[]{:S(2)}) collective-permute-start(f32[1024,64]{1,0:T(8,128)} %get-tuple-element.27), channel_id=1, source_target_pairs={{0,4},{4,8},{8,12},{12,16},{16,20},{20,24},{24,28},{28,32},{32,36}... | collective-permute-start | bytes 786440 | tf_op jit(solution)/shard_map/ppermute | solution.py:246
  117.3 1.9 collective-permute-start.3
  119.2 3.2 collective-permute-done.2.refs_3_
  122.4 3.8 %collective-permute-done.3.refs_4_ = f32[1024,64]{1,0:T(8,128)S(1)} collective-permute-done((f32[1024,64]{1,0:T(8,128)}, f32[1024,64]{1,0:T(8,128)S(1)}, u32[]{:S(2)}, u32[]{:S(2)}) %collective-permute-start.3) | collective-permute-done | bytes 262176 | tf_op jit(solution)/shard_map/ppermute | solution.py:247
  127.0 41.5 %shard_map.75 = (bf16[12288,64]{1,0:T(8,128)(2,1)}, f32[12288,64]{1,0:T(8,128)}, f32[1024,64]{1,0:T(8,128)}, f32[1024,64]{1,0:T(8,128)}) custom-call(s32[2048]{0:T(1024)} %pad_add_fusion.refs_0_, f32[32]{0:T(128)} %compare_select_fusion.1.refs_1_, f32[12288,64]{1,0:T(8,128)} %get-tuple-element.26.refs_2_, f32[1024,64]{1,0:T(8,128)} %copy-done.3, ...), custom_call_target="tpu_custom_call" | custom-call | flops 1073741824 | bytes 26214400 | tf_op jit(solution)/shard_map/pallas_call | solution.py:151
  168.5 5.8 %collective-permute-start.4 = (f32[1024,64]{1,0:T(8,128)}, f32[1024,64]{1,0:T(8,128)S(1)}, u32[]{:S(2)}, u32[]{:S(2)}) collective-permute-start(f32[1024,64]{1,0:T(8,128)} %get-tuple-element.30), channel_id=1, source_target_pairs={{0,4},{4,8},{8,12},{12,16},{16,20},{20,24},{24,28},{28,32},{32,36}... | collective-permute-start | bytes 786440 | tf_op jit(solution)/shard_map/ppermute | solution.py:246
  176.2 3.0 collective-permute-done.4.refs_3_
  179.2 4.0 %collective-permute-done.5.refs_4_ = f32[1024,64]{1,0:T(8,128)S(1)} collective-permute-done((f32[1024,64]{1,0:T(8,128)}, f32[1024,64]{1,0:T(8,128)S(1)}, u32[]{:S(2)}, u32[]{:S(2)}) %collective-permute-start.5) | collective-permute-done | bytes 262176 | tf_op jit(solution)/shard_map/ppermute | solution.py:247
  184.0 41.4 %shard_map.76 = (bf16[12288,64]{1,0:T(8,128)(2,1)}, f32[12288,64]{1,0:T(8,128)}, f32[1024,64]{1,0:T(8,128)}, f32[1024,64]{1,0:T(8,128)}) custom-call(s32[2048]{0:T(1024)} %pad_add_fusion.refs_0_, f32[32]{0:T(128)} %compare_select_fusion.1.refs_1_, f32[12288,64]{1,0:T(8,128)} %get-tuple-element.29.refs_2_, f32[1024,64]{1,0:T(8,128)} %copy-done, ...), custom_call_target="tpu_custom_call" | custom-call | flops 1073741824 | bytes 26214400 | tf_op jit(solution)/shard_map/pallas_call | solution.py:151
  225.4 5.8 %collective-permute-start.6 = (f32[1024,64]{1,0:T(8,128)}, f32[1024,64]{1,0:T(8,128)S(1)}, u32[]{:S(2)}, u32[]{:S(2)}) collective-permute-start(f32[1024,64]{1,0:T(8,128)} %get-tuple-element.34), channel_id=1, source_target_pairs={{0,4},{4,8},{8,12},{12,16},{16,20},{20,24},{24,28},{28,32},{32,36}... | collective-permute-start | bytes 786440 | tf_op jit(solution)/shard_map/ppermute | solution.py:246
  233.1 3.0 collective-permute-done.6.refs_2_
  236.2 4.0 %collective-permute-done.7.refs_3_ = f32[1024,64]{1,0:T(8,128)S(1)} collective-permute-done((f32[1024,64]{1,0:T(8,128)}, f32[1024,64]{1,0:T(8,128)S(1)}, u32[]{:S(2)}, u32[]{:S(2)}) %collective-permute-start.7) | collective-permute-done | bytes 262176 | tf_op jit(solution)/shard_map/ppermute | solution.py:247
  240.9 12.5 %shard_map.77 = bf16[12288,64]{1,0:T(8,128)(2,1)} custom-call(s32[2048]{0:T(1024)} %pad_add_fusion.refs_0_, f32[12288,64]{1,0:T(8,128)} %get-tuple-element.33.refs_1_, f32[1024,64]{1,0:T(8,128)} %copy-done.4, f32[1024,64]{1,0:T(8,128)} %copy-done.7, bf16[12288,64]{1,0:T(8,128)(2,1)} %get-tuple-element.36.refs_4_), custom_call_target="tpu_custom_call" | custom-call | bytes 9437184 | tf_op jit(solution)/shard_map/pallas_call | solution.py:151
  253.4 4.3 %copy.11 = bf16[4,3072,64]{1,2,0:T(8,128)(2,1)} copy(bf16[4,3072,64]{2,1,0:T(8,128)(2,1)} %bitcast.54) | data formatting | bytes 3145728 | tf_op jit(solution)/shard_map/all_to_all | solution.py:266
  257.7 5.6 %all-to-all-start = ((bf16[4,3072,64]{1,2,0:T(8,128)(2,1)}), bf16[4,3072,64]{1,2,0:T(8,128)(2,1)S(1)}, u32[]{:S(2)}, u32[]{:S(2)}) async-start(bf16[4,3072,64]{1,2,0:T(8,128)(2,1)} %copy.11), calls=%async_computation | async-start | bytes 3145728 | tf_op jit(solution)/shard_map/all_to_all | solution.py:266
  263.3 8.1 %scatter_custom_fusion = f32[12288]{0:T(1024)S(1)} fusion(s32[2048]{0:T(1024)S(1)} %bitcast.62, f32[2048]{0:T(1024)S(1)} %add_divide_fusion, f32[]{:T(128)} %constant.17.clone.1), kind=kCustom, calls=%fused_computation.23 | custom fusion | bytes 49156 | tf_op jit(solution)/shard_map/scatter | solution.py:232
  271.4 11.3 %all-to-all-done = bf16[4,3072,64]{1,2,0:T(8,128)(2,1)S(1)} async-done(((bf16[4,3072,64]{1,2,0:T(8,128)(2,1)}), bf16[4,3072,64]{1,2,0:T(8,128)(2,1)S(1)}, u32[]{:S(2)}, u32[]{:S(2)}) %all-to-all-start) | async-done | bytes 1572896 | tf_op jit(solution)/shard_map/all_to_all | solution.py:266
  283.5 2.6 collective-permute-start.8
  288.1 8.0 %collective-permute-done.9 = f32[256,256]{1,0:T(8,128)S(1)} collective-permute-done((f32[256,256]{1,0:T(8,128)S(1)}, f32[256,256]{1,0:T(8,128)S(1)}, u32[]{:S(2)}, u32[]{:S(2)}) %collective-permute-start.9) | collective-permute-done | bytes 262176 | tf_op jit(solution)/shard_map/ppermute | solution.py:210
  297.1 8.3 %collective-permute-done.10 = f32[256,256]{1,0:T(8,128)S(1)} collective-permute-done((f32[256,256]{1,0:T(8,128)S(1)}, f32[256,256]{1,0:T(8,128)S(1)}, u32[]{:S(2)}, u32[]{:S(2)}) %collective-permute-start.10) | collective-permute-done | bytes 262176 | tf_op jit(solution)/shard_map/ppermute | solution.py:210
  305.6 7.5 %collective-permute-done.11 = f32[256,256]{1,0:T(8,128)S(1)} collective-permute-done((f32[256,256]{1,0:T(8,128)S(1)}, f32[256,256]{1,0:T(8,128)S(1)}, u32[]{:S(2)}, u32[]{:S(2)}) %collective-permute-start.11) | collective-permute-done | bytes 262176 | tf_op jit(solution)/shard_map/ppermute | solution.py:210
  313.2 7.9 %collective-permute-done.12 = f32[256,256]{1,0:T(8,128)S(1)} collective-permute-done((f32[256,256]{1,0:T(8,128)S(1)}, f32[256,256]{1,0:T(8,128)S(1)}, u32[]{:S(2)}, u32[]{:S(2)}) %collective-permute-start.12) | collective-permute-done | bytes 262176 | tf_op jit(solution)/shard_map/ppermute | solution.py:210
  322.8 6.7 %collective-permute-done.13 = f32[256,256]{1,0:T(8,128)S(1)} collective-permute-done((f32[256,256]{1,0:T(8,128)S(1)}, f32[256,256]{1,0:T(8,128)S(1)}, u32[]{:S(2)}, u32[]{:S(2)}) %collective-permute-start.13) | collective-permute-done | bytes 262176 | tf_op jit(solution)/shard_map/ppermute | solution.py:210
  329.5 2.8 collective-permute-start.14
  332.2 5.2 %collective-permute-done.14 = f32[256,256]{1,0:T(8,128)S(1)} collective-permute-done((f32[256,256]{1,0:T(8,128)S(1)}, f32[256,256]{1,0:T(8,128)S(1)}, u32[]{:S(2)}, u32[]{:S(2)}) %collective-permute-start.14) | collective-permute-done | bytes 262176 | tf_op jit(solution)/shard_map/ppermute | solution.py:210
  344.7 17.3 %all_to_all.38 = bf16[3072,4,64]{0,2,1:T(8,128)(2,1)S(1)} all-to-all(bf16[3072,4,64]{0,2,1:T(8,128)(2,1)S(1)} %bitcast.57), channel_id=1, replica_groups=mesh['dom'=32,'band'=4] {'band'}, dimensions={1} | all-to-all | bytes 3145728 | tf_op jit(solution)/shard_map/all_to_all | solution.py:280
  (65 shorter events, 27.4 us)
Async XLA Ops:
  4.6 4.2 %copy-start.8 = (f32[32]{0:T(128)S(1)}, f32[32]{0:T(128)}, u32[]{:S(2)}) copy-start(f32[32]{0:T(128)} %param.9) | copy-start | bytes 388
  58.1 10.7 %collective-permute-start = (f32[1024,64]{1,0:T(8,128)}, f32[1024,64]{1,0:T(8,128)S(1)}, u32[]{:S(2)}, u32[]{:S(2)}) collective-permute-start(f32[1024,64]{1,0:T(8,128)} %get-tuple-element.22), channel_id=1, source_target_pairs={{0,4},{4,8},{8,12},{12,16},{16,20},{20,24},{24,28},{28,32},{32,36}... | collective-permute-start | bytes 786440 | tf_op jit(solution)/shard_map/ppermute | solution.py:246
  60.1 10.6 %collective-permute-start.1 = (f32[1024,64]{1,0:T(8,128)}, f32[1024,64]{1,0:T(8,128)S(1)}, u32[]{:S(2)}, u32[]{:S(2)}) collective-permute-start(f32[1024,64]{1,0:T(8,128)} %get-tuple-element.23), channel_id=1, source_target_pairs={{4,0},{8,4},{12,8},{16,12},{20,16},{24,20},{28,24},{32,28},{36,32}... | collective-permute-start | bytes 786440 | tf_op jit(solution)/shard_map/ppermute | solution.py:247
  68.8 1.9 copy-start.2
  70.7 0.8 copy-start.5
  111.6 10.8 %collective-permute-start.2 = (f32[1024,64]{1,0:T(8,128)}, f32[1024,64]{1,0:T(8,128)S(1)}, u32[]{:S(2)}, u32[]{:S(2)}) collective-permute-start(f32[1024,64]{1,0:T(8,128)} %get-tuple-element.27), channel_id=1, source_target_pairs={{0,4},{4,8},{8,12},{12,16},{16,20},{20,24},{24,28},{28,32},{32,36}... | collective-permute-start | bytes 786440 | tf_op jit(solution)/shard_map/ppermute | solution.py:246
  117.3 8.9 %collective-permute-start.3 = (f32[1024,64]{1,0:T(8,128)}, f32[1024,64]{1,0:T(8,128)S(1)}, u32[]{:S(2)}, u32[]{:S(2)}) collective-permute-start(f32[1024,64]{1,0:T(8,128)} %get-tuple-element.28), channel_id=1, source_target_pairs={{4,0},{8,4},{12,8},{16,12},{20,16},{24,20},{28,24},{32,28},{36,32}... | collective-permute-start | bytes 786440 | tf_op jit(solution)/shard_map/ppermute | solution.py:247
  122.4 3.8 %copy-start.3 = (f32[1024,64]{1,0:T(8,128)}, f32[1024,64]{1,0:T(8,128)S(1)}, u32[]{:S(2)}) copy-start(f32[1024,64]{1,0:T(8,128)S(1)} %collective-permute-done.2.refs_3_) | copy-start | bytes 786436
  126.2 0.8 copy-start.6
  168.5 10.8 %collective-permute-start.4 = (f32[1024,64]{1,0:T(8,128)}, f32[1024,64]{1,0:T(8,128)S(1)}, u32[]{:S(2)}, u32[]{:S(2)}) collective-permute-start(f32[1024,64]{1,0:T(8,128)} %get-tuple-element.30), channel_id=1, source_target_pairs={{0,4},{4,8},{8,12},{12,16},{16,20},{20,24},{24,28},{28,32},{32,36}... | collective-permute-start | bytes 786440 | tf_op jit(solution)/shard_map/ppermute | solution.py:246
  174.3 8.9 %collective-permute-start.5 = (f32[1024,64]{1,0:T(8,128)}, f32[1024,64]{1,0:T(8,128)S(1)}, u32[]{:S(2)}, u32[]{:S(2)}) collective-permute-start(f32[1024,64]{1,0:T(8,128)} %get-tuple-element.31), channel_id=1, source_target_pairs={{4,0},{8,4},{12,8},{16,12},{20,16},{24,20},{28,24},{32,28},{36,32}... | collective-permute-start | bytes 786440 | tf_op jit(solution)/shard_map/ppermute | solution.py:247
  179.2 4.0 %copy-start = (f32[1024,64]{1,0:T(8,128)}, f32[1024,64]{1,0:T(8,128)S(1)}, u32[]{:S(2)}) copy-start(f32[1024,64]{1,0:T(8,128)S(1)} %collective-permute-done.4.refs_3_) | copy-start | bytes 786436
  183.2 0.8 copy-start.1
  225.4 10.8 %collective-permute-start.6 = (f32[1024,64]{1,0:T(8,128)}, f32[1024,64]{1,0:T(8,128)S(1)}, u32[]{:S(2)}, u32[]{:S(2)}) collective-permute-start(f32[1024,64]{1,0:T(8,128)} %get-tuple-element.34), channel_id=1, source_target_pairs={{0,4},{4,8},{8,12},{12,16},{16,20},{20,24},{24,28},{28,32},{32,36}... | collective-permute-start | bytes 786440 | tf_op jit(solution)/shard_map/ppermute | solution.py:246
  231.2 8.9 %collective-permute-start.7 = (f32[1024,64]{1,0:T(8,128)}, f32[1024,64]{1,0:T(8,128)S(1)}, u32[]{:S(2)}, u32[]{:S(2)}) collective-permute-start(f32[1024,64]{1,0:T(8,128)} %get-tuple-element.35), channel_id=1, source_target_pairs={{4,0},{8,4},{12,8},{16,12},{20,16},{24,20},{28,24},{32,28},{36,32}... | collective-permute-start | bytes 786440 | tf_op jit(solution)/shard_map/ppermute | solution.py:247
  236.2 4.0 %copy-start.4 = (f32[1024,64]{1,0:T(8,128)}, f32[1024,64]{1,0:T(8,128)S(1)}, u32[]{:S(2)}) copy-start(f32[1024,64]{1,0:T(8,128)S(1)} %collective-permute-done.6.refs_2_) | copy-start | bytes 786436
  240.1 0.8 copy-start.7
  257.7 25.0 %all-to-all-start = ((bf16[4,3072,64]{1,2,0:T(8,128)(2,1)}), bf16[4,3072,64]{1,2,0:T(8,128)(2,1)S(1)}, u32[]{:S(2)}, u32[]{:S(2)}) async-start(bf16[4,3072,64]{1,2,0:T(8,128)(2,1)} %copy.11), calls=%async_computation | async-start | bytes 3145728 | tf_op jit(solution)/shard_map/all_to_all | solution.py:266
  283.5 3.7 %collective-permute-start.8 = (f32[256,256]{1,0:T(8,128)S(1)}, f32[256,256]{1,0:T(8,128)S(1)}, u32[]{:S(2)}, u32[]{:S(2)}) collective-permute-start(f32[256,256]{1,0:T(8,128)S(1)} %fusion.9), channel_id=1, source_target_pairs={{0,4},{1,5},{2,6},{3,7},{4,0},{5,1},{6,2},{7,3},{8,12},{9,13},{10,... | collective-permute-start | bytes 786440 | tf_op jit(solution)/shard_map/ppermute | solution.py:210
  287.2 8.8 %collective-permute-start.9 = (f32[256,256]{1,0:T(8,128)S(1)}, f32[256,256]{1,0:T(8,128)S(1)}, u32[]{:S(2)}, u32[]{:S(2)}) collective-permute-start(f32[256,256]{1,0:T(8,128)S(1)} %add.53), channel_id=1, source_target_pairs={{0,1},{1,0},{2,3},{3,2},{4,5},{5,4},{6,7},{7,6},{8,9},{9,8},{10,11... | collective-permute-start | bytes 786440 | tf_op jit(solution)/shard_map/ppermute | solution.py:210
  296.1 9.3 %collective-permute-start.10 = (f32[256,256]{1,0:T(8,128)S(1)}, f32[256,256]{1,0:T(8,128)S(1)}, u32[]{:S(2)}, u32[]{:S(2)}) collective-permute-start(f32[256,256]{1,0:T(8,128)S(1)} %add.54), channel_id=1, source_target_pairs={{0,2},{1,3},{2,0},{3,1},{4,6},{5,7},{6,4},{7,5},{8,10},{9,11},{10,... | collective-permute-start | bytes 786440 | tf_op jit(solution)/shard_map/ppermute | solution.py:210
  305.5 7.6 %collective-permute-start.11 = (f32[256,256]{1,0:T(8,128)S(1)}, f32[256,256]{1,0:T(8,128)S(1)}, u32[]{:S(2)}, u32[]{:S(2)}) collective-permute-start(f32[256,256]{1,0:T(8,128)S(1)} %add.55), channel_id=1, source_target_pairs={{0,8},{1,9},{2,10},{3,11},{4,12},{5,13},{6,14},{7,15},{8,0},{9,1},... | collective-permute-start | bytes 786440 | tf_op jit(solution)/shard_map/ppermute | solution.py:210
  313.1 8.0 %collective-permute-start.12 = (f32[256,256]{1,0:T(8,128)S(1)}, f32[256,256]{1,0:T(8,128)S(1)}, u32[]{:S(2)}, u32[]{:S(2)}) collective-permute-start(f32[256,256]{1,0:T(8,128)S(1)} %add.56), channel_id=1, source_target_pairs={{0,16},{1,17},{2,18},{3,19},{4,20},{5,21},{6,22},{7,23},{8,24},{9,... | collective-permute-start | bytes 786440 | tf_op jit(solution)/shard_map/ppermute | solution.py:210
  321.1 8.3 %collective-permute-start.13 = (f32[256,256]{1,0:T(8,128)S(1)}, f32[256,256]{1,0:T(8,128)S(1)}, u32[]{:S(2)}, u32[]{:S(2)}) collective-permute-start(f32[256,256]{1,0:T(8,128)S(1)} %add.57), channel_id=1, source_target_pairs={{0,32},{1,33},{2,34},{3,35},{4,36},{5,37},{6,38},{7,39},{8,40},{9,... | collective-permute-start | bytes 786440 | tf_op jit(solution)/shard_map/ppermute | solution.py:210
  329.5 8.0 %collective-permute-start.14 = (f32[256,256]{1,0:T(8,128)S(1)}, f32[256,256]{1,0:T(8,128)S(1)}, u32[]{:S(2)}, u32[]{:S(2)}) collective-permute-start(f32[256,256]{1,0:T(8,128)S(1)} %add.58), channel_id=1, source_target_pairs={{0,64},{1,65},{2,66},{3,67},{4,68},{5,69},{6,70},{7,71},{8,72},{9,... | collective-permute-start | bytes 786440 | tf_op jit(solution)/shard_map/ppermute | solution.py:210

commit v5 on v4

--- a/solution.py
+++ b/solution.py
@@ -43,7 +43,7 @@
         work = refs.pop(0)
     vector = vector_out if combine else vector_in
     face_half = faces.shape[0] // 2
-    node_total = vector.shape[0]
+    node_total = (local_in if combine else vector_in).shape[0]
     cell = pl.program_id(0) if apply else None
 
     def prologue():
@@ -60,7 +60,18 @@
         value = work[...]
         if older:
             value = value - older_ref[...].astype(jnp.float32)
-        vector_out[...] = value.astype(vector_out.dtype)
+        if apply:
+            vector_out[...] = value.astype(vector_out.dtype)
+        else:
+            work[...] = value
+            lanes = 128
+
+            def turn(j, carry):
+                rows = pl.ds(pl.multiple_of(j * lanes, lanes), lanes)
+                vector_out[:, rows] = jnp.transpose(work[rows, :]).astype(vector_out.dtype)
+                return carry
+
+            lax.fori_loop(0, node_total // lanes, turn, 0)
 
     if combine:
         if apply:
@@ -136,7 +147,8 @@
             args.append(kinetic); specs.append(whole)
     out_shape, out_specs = [], []
     if combine:
-        out_shape.append(jax.ShapeDtypeStruct((node_total, cols), jnp.bfloat16)); out_specs.append(whole)
+        shape = (node_total, cols) if apply else (cols, node_total)
+        out_shape.append(jax.ShapeDtypeStruct(shape, jnp.bfloat16)); out_specs.append(whole)
     if apply:
         out_shape += [jax.ShapeDtypeStruct((node_total, cols), jnp.float32),
                       jax.ShapeDtypeStruct((face_half, cols), jnp.float32),
@@ -263,22 +275,21 @@
         local_in=local_sum, received=exchange(*face_values), older=history[-2], alpha=2.0,
         apply=False,
     )
-    row_shard = lax.all_to_all(current, "band", split_axis=0, concat_axis=1, tiled=True)
-    piece_nodes = row_shard.shape[0]
+    row_shard = lax.all_to_all(current, "band", split_axis=1, concat_axis=0, tiled=True)
+    piece_nodes = row_shard.shape[1]
     weight_rows = lax.dynamic_slice_in_dim(
         node_weight, lax.axis_index("band") * piece_nodes, piece_nodes, 0
     )
-    weighted = row_shard * weight_rows[:, None]
+    weighted = row_shard * weight_rows[None]
     partial_gram = lax.dot_general(
-        weighted, row_shard, (((0,), (0,)), ((), ())), preferred_element_type=jnp.float32
+        weighted, row_shard, (((1,), (1,)), ((), ())), preferred_element_type=jnp.float32
     )
     gram_matrix = doubling_sum(partial_gram)
     mixing = newton(gram_matrix)
     rotated = lax.dot_general(
-        row_shard, mixing, (((1,), (0,)), ((), ())), preferred_element_type=jnp.float32
+        mixing, row_shard, (((0,), (0,)), ((), ())), preferred_element_type=jnp.float32
     ).astype(jnp.bfloat16)
-    back = lax.all_to_all(rotated, "band", split_axis=1, concat_axis=0, tiled=True)
-    return back.T
+    return lax.all_to_all(rotated, "band", split_axis=0, concat_axis=1, tiled=True)
 
 
 def solution(mesh):

time: 365 us -> 371 us (1.016)
  Pallas kernels: 184 us -> 191 us
    pallas_call x5, Pallas kernels: 184 us -> 191 us  [field_step(): pl.pallas_call(functools.partial(field_kernel, combine, has_older, apply,...]
where the time goes in v5:
time: 371 us; the launch traced here: 369 us
  Pallas kernels  191 us (51%)
  waiting for transfers between devices  84.1 us (23%)
  starting transfers between devices  43.1 us (12%)
  local copies, waits for them, and re-layouts  21.5 us (6%)
  blocking collectives  17.2 us (5%)
  matrix products  6.37 us (2%)
  other arithmetic  3.97 us (1%)
    pallas_call x5, Pallas kernels, field_step(): pl.pallas_call(functools.partial(field_kernel, combine, has_older, apply,...  191 us
    ppermute x7, waiting for transfers between devices, doubling_sum(): total = total + lax.ppermute(total, ('dom', 'band'), pairs)  44.8 us
    ppermute x4, starting transfers between devices, exchange(): from_left = lax.ppermute(right_values, 'dom', up)  19.3 us
    all_to_all x1, blocking collectives, body(): lax.all_to_all(rotated, 'band', split_axis=0, concat_axis=1, tiled=True)  17.2 us
    ppermute x4, waiting for transfers between devices, exchange(): from_left = lax.ppermute(right_values, 'dom', up)  14.3 us
    ppermute x4, waiting for transfers between devices, exchange(): from_right = lax.ppermute(left_values, 'dom', down)  13.6 us
    all_to_all x1, waiting for transfers between devices, body(): lax.all_to_all(current, 'band', split_axis=1, concat_axis=0, tiled=True)  11.3 us
    ppermute x4, starting transfers between devices, exchange(): from_right = lax.ppermute(left_values, 'dom', down)  9.32 us
  transfers between devices with their start and end apart: 16, of which 16 were waited for; matrix products, arithmetic and copies ran while one was open for 2% of the time, Pallas kernels for 0%

profile of v5, /device:TPU:6, one launch (start us, length us, event | category | flops | bytes accessed | tf_op | source)
XLA Modules:
  0.0 369.2 jit_solution(12560407467711359760)
XLA Ops:
  4.7 4.2 %copy.10 = bf16[64,12288]{0,1:T(8,128)(2,1)} copy(bf16[64,12288]{1,0:T(8,128)(2,1)} %param.7) | data formatting | bytes 3145728 | tf_op args[0]
  9.9 48.2 %shard_map.73 = (f32[12288,64]{1,0:T(8,128)}, f32[1024,64]{1,0:T(8,128)}, f32[1024,64]{1,0:T(8,128)}, bf16[32,512,512]{2,1,0:T(8,128)(2,1)}, f32[32,1,512]{2,1,0:T(1,128)}) custom-call(s32[2048]{0:T(1024)} %pad_add_fusion.refs_0_, f32[32]{0:T(128)} %compare_select_fusion.1.refs_1_, bf16[12288,64]{1,0:T(8,128)(2,1)} %bitcast.55, ...), custom_call_target="tpu_custom_call" | custom-call | flops 18253611008 | bytes 26214400 | tf_op jit(solution)/shard_map/pallas_call | solution.py:163
  58.1 2.0 collective-permute-start
  60.1 3.6 collective-permute-start.1
  63.7 5.1 %collective-permute-done.refs_3_ = f32[1024,64]{1,0:T(8,128)S(1)} collective-permute-done((f32[1024,64]{1,0:T(8,128)}, f32[1024,64]{1,0:T(8,128)S(1)}, u32[]{:S(2)}, u32[]{:S(2)}) %collective-permute-start) | collective-permute-done | bytes 262176 | tf_op jit(solution)/shard_map/ppermute | solution.py:258
  71.5 40.1 %shard_map.74 = (bf16[12288,64]{1,0:T(8,128)(2,1)}, f32[12288,64]{1,0:T(8,128)}, f32[1024,64]{1,0:T(8,128)}, f32[1024,64]{1,0:T(8,128)}) custom-call(s32[2048]{0:T(1024)} %pad_add_fusion.refs_0_, f32[32]{0:T(128)} %compare_select_fusion.1.refs_1_, f32[12288,64]{1,0:T(8,128)} %get-tuple-element.21.refs_2_, f32[1024,64]{1,0:T(8,128)} %copy-done.2, ...), custom_call_target="tpu_custom_call" | custom-call | flops 1073741824 | bytes 26214400 | tf_op jit(solution)/shard_map/pallas_call | solution.py:163
  111.6 5.7 %collective-permute-start.2 = (f32[1024,64]{1,0:T(8,128)}, f32[1024,64]{1,0:T(8,128)S(1)}, u32[]{:S(2)}, u32[]{:S(2)}) collective-permute-start(f32[1024,64]{1,0:T(8,128)} %get-tuple-element.27), channel_id=1, source_target_pairs={{0,4},{4,8},{8,12},{12,16},{16,20},{20,24},{24,28},{28,32},{32,36}... | collective-permute-start | bytes 786440 | tf_op jit(solution)/shard_map/ppermute | solution.py:258
  117.3 1.9 collective-permute-start.3
  119.2 3.2 collective-permute-done.2.refs_3_
  122.4 3.8 %collective-permute-done.3.refs_4_ = f32[1024,64]{1,0:T(8,128)S(1)} collective-permute-done((f32[1024,64]{1,0:T(8,128)}, f32[1024,64]{1,0:T(8,128)S(1)}, u32[]{:S(2)}, u32[]{:S(2)}) %collective-permute-start.3) | collective-permute-done | bytes 262176 | tf_op jit(solution)/shard_map/ppermute | solution.py:259
  127.0 41.5 %shard_map.75 = (bf16[12288,64]{1,0:T(8,128)(2,1)}, f32[12288,64]{1,0:T(8,128)}, f32[1024,64]{1,0:T(8,128)}, f32[1024,64]{1,0:T(8,128)}) custom-call(s32[2048]{0:T(1024)} %pad_add_fusion.refs_0_, f32[32]{0:T(128)} %compare_select_fusion.1.refs_1_, f32[12288,64]{1,0:T(8,128)} %get-tuple-element.26.refs_2_, f32[1024,64]{1,0:T(8,128)} %copy-done.3, ...), custom_call_target="tpu_custom_call" | custom-call | flops 1073741824 | bytes 26214400 | tf_op jit(solution)/shard_map/pallas_call | solution.py:163
  168.5 5.8 %collective-permute-start.4 = (f32[1024,64]{1,0:T(8,128)}, f32[1024,64]{1,0:T(8,128)S(1)}, u32[]{:S(2)}, u32[]{:S(2)}) collective-permute-start(f32[1024,64]{1,0:T(8,128)} %get-tuple-element.30), channel_id=1, source_target_pairs={{0,4},{4,8},{8,12},{12,16},{16,20},{20,24},{24,28},{28,32},{32,36}... | collective-permute-start | bytes 786440 | tf_op jit(solution)/shard_map/ppermute | solution.py:258
  176.2 3.0 collective-permute-done.4.refs_3_
  179.2 4.0 %collective-permute-done.5.refs_4_ = f32[1024,64]{1,0:T(8,128)S(1)} collective-permute-done((f32[1024,64]{1,0:T(8,128)}, f32[1024,64]{1,0:T(8,128)S(1)}, u32[]{:S(2)}, u32[]{:S(2)}) %collective-permute-start.5) | collective-permute-done | bytes 262176 | tf_op jit(solution)/shard_map/ppermute | solution.py:259
  184.0 41.4 %shard_map.76 = (bf16[12288,64]{1,0:T(8,128)(2,1)}, f32[12288,64]{1,0:T(8,128)}, f32[1024,64]{1,0:T(8,128)}, f32[1024,64]{1,0:T(8,128)}) custom-call(s32[2048]{0:T(1024)} %pad_add_fusion.refs_0_, f32[32]{0:T(128)} %compare_select_fusion.1.refs_1_, f32[12288,64]{1,0:T(8,128)} %get-tuple-element.29.refs_2_, f32[1024,64]{1,0:T(8,128)} %copy-done, ...), custom_call_target="tpu_custom_call" | custom-call | flops 1073741824 | bytes 26214400 | tf_op jit(solution)/shard_map/pallas_call | solution.py:163
  225.4 5.8 %collective-permute-start.6 = (f32[1024,64]{1,0:T(8,128)}, f32[1024,64]{1,0:T(8,128)S(1)}, u32[]{:S(2)}, u32[]{:S(2)}) collective-permute-start(f32[1024,64]{1,0:T(8,128)} %get-tuple-element.34), channel_id=1, source_target_pairs={{0,4},{4,8},{8,12},{12,16},{16,20},{20,24},{24,28},{28,32},{32,36}... | collective-permute-start | bytes 786440 | tf_op jit(solution)/shard_map/ppermute | solution.py:258
  233.2 3.0 collective-permute-done.6.refs_2_
  236.2 4.0 %collective-permute-done.7.refs_3_ = f32[1024,64]{1,0:T(8,128)S(1)} collective-permute-done((f32[1024,64]{1,0:T(8,128)}, f32[1024,64]{1,0:T(8,128)S(1)}, u32[]{:S(2)}, u32[]{:S(2)}) %collective-permute-start.7) | collective-permute-done | bytes 262176 | tf_op jit(solution)/shard_map/ppermute | solution.py:259
  241.0 20.0 %shard_map.77 = bf16[64,12288]{1,0:T(8,128)(2,1)} custom-call(s32[2048]{0:T(1024)} %pad_add_fusion.refs_0_, f32[12288,64]{1,0:T(8,128)} %get-tuple-element.33.refs_1_, f32[1024,64]{1,0:T(8,128)} %copy-done.4, f32[1024,64]{1,0:T(8,128)} %copy-done.7, bf16[12288,64]{1,0:T(8,128)(2,1)} %get-tuple-element.36.refs_4_), custom_call_target="tpu_custom_call" | custom-call | bytes 9437184 | tf_op jit(solution)/shard_map/pallas_call | solution.py:163
  261.0 2.7 copy.16
  263.7 5.6 %all-to-all-start = ((bf16[64,4,3072]{2,0,1:T(8,128)(2,1)}), bf16[64,4,3072]{2,0,1:T(8,128)(2,1)S(1)}, u32[]{:S(2)}, u32[]{:S(2)}) async-start(bf16[64,4,3072]{2,0,1:T(8,128)(2,1)} %bitcast.49), calls=%async_computation | async-start | bytes 3145728 | tf_op jit(solution)/shard_map/all_to_all | solution.py:278
  269.3 8.1 %scatter_custom_fusion = f32[12288]{0:T(1024)S(1)} fusion(s32[2048]{0:T(1024)S(1)} %bitcast.63, f32[2048]{0:T(1024)S(1)} %add_divide_fusion, f32[]{:T(128)} %constant.17.clone.1), kind=kCustom, calls=%fused_computation.24 | custom fusion | bytes 49156 | tf_op jit(solution)/shard_map/scatter | solution.py:244
  277.4 11.3 %all-to-all-done = bf16[64,4,3072]{2,0,1:T(8,128)(2,1)S(1)} async-done(((bf16[64,4,3072]{2,0,1:T(8,128)(2,1)}), bf16[64,4,3072]{2,0,1:T(8,128)(2,1)S(1)}, u32[]{:S(2)}, u32[]{:S(2)}) %all-to-all-start) | async-done | bytes 1572896 | tf_op jit(solution)/shard_map/all_to_all | solution.py:278
  289.5 2.6 collective-permute-start.8
  293.9 8.0 %collective-permute-done.9 = f32[256,256]{1,0:T(8,128)S(1)} collective-permute-done((f32[256,256]{1,0:T(8,128)S(1)}, f32[256,256]{1,0:T(8,128)S(1)}, u32[]{:S(2)}, u32[]{:S(2)}) %collective-permute-start.9) | collective-permute-done | bytes 262176 | tf_op jit(solution)/shard_map/ppermute | solution.py:222
  303.1 8.3 %collective-permute-done.10 = f32[256,256]{1,0:T(8,128)S(1)} collective-permute-done((f32[256,256]{1,0:T(8,128)S(1)}, f32[256,256]{1,0:T(8,128)S(1)}, u32[]{:S(2)}, u32[]{:S(2)}) %collective-permute-start.10) | collective-permute-done | bytes 262176 | tf_op jit(solution)/shard_map/ppermute | solution.py:222
  311.6 7.5 %collective-permute-done.11 = f32[256,256]{1,0:T(8,128)S(1)} collective-permute-done((f32[256,256]{1,0:T(8,128)S(1)}, f32[256,256]{1,0:T(8,128)S(1)}, u32[]{:S(2)}, u32[]{:S(2)}) %collective-permute-start.11) | collective-permute-done | bytes 262176 | tf_op jit(solution)/shard_map/ppermute | solution.py:222
  319.2 7.9 %collective-permute-done.12 = f32[256,256]{1,0:T(8,128)S(1)} collective-permute-done((f32[256,256]{1,0:T(8,128)S(1)}, f32[256,256]{1,0:T(8,128)S(1)}, u32[]{:S(2)}, u32[]{:S(2)}) %collective-permute-start.12) | collective-permute-done | bytes 262176 | tf_op jit(solution)/shard_map/ppermute | solution.py:222
  328.8 6.7 %collective-permute-done.13 = f32[256,256]{1,0:T(8,128)S(1)} collective-permute-done((f32[256,256]{1,0:T(8,128)S(1)}, f32[256,256]{1,0:T(8,128)S(1)}, u32[]{:S(2)}, u32[]{:S(2)}) %collective-permute-start.13) | collective-permute-done | bytes 262176 | tf_op jit(solution)/shard_map/ppermute | solution.py:222
  335.5 2.8 collective-permute-start.14
  338.2 5.2 %collective-permute-done.14 = f32[256,256]{1,0:T(8,128)S(1)} collective-permute-done((f32[256,256]{1,0:T(8,128)S(1)}, f32[256,256]{1,0:T(8,128)S(1)}, u32[]{:S(2)}, u32[]{:S(2)}) %collective-permute-start.14) | collective-permute-done | bytes 262176 | tf_op jit(solution)/shard_map/ppermute | solution.py:222
  350.7 17.2 %all_to_all.38 = bf16[4,64,3072]{2,1,0:T(8,128)(2,1)S(1)} all-to-all(bf16[4,64,3072]{2,1,0:T(8,128)(2,1)S(1)} %bitcast.58), channel_id=1, replica_groups=mesh['dom'=32,'band'=4] {'band'}, dimensions={0} | all-to-all | bytes 3145728 | tf_op jit(solution)/shard_map/all_to_all | solution.py:292
  (65 shorter events, 27.4 us)
Async XLA Ops:
  4.6 4.2 %copy-start.8 = (f32[32]{0:T(128)S(1)}, f32[32]{0:T(128)}, u32[]{:S(2)}) copy-start(f32[32]{0:T(128)} %param.9) | copy-start | bytes 388
  58.1 10.7 %collective-permute-start = (f32[1024,64]{1,0:T(8,128)}, f32[1024,64]{1,0:T(8,128)S(1)}, u32[]{:S(2)}, u32[]{:S(2)}) collective-permute-start(f32[1024,64]{1,0:T(8,128)} %get-tuple-element.22), channel_id=1, source_target_pairs={{0,4},{4,8},{8,12},{12,16},{16,20},{20,24},{24,28},{28,32},{32,36}... | collective-permute-start | bytes 786440 | tf_op jit(solution)/shard_map/ppermute | solution.py:258
  60.1 10.6 %collective-permute-start.1 = (f32[1024,64]{1,0:T(8,128)}, f32[1024,64]{1,0:T(8,128)S(1)}, u32[]{:S(2)}, u32[]{:S(2)}) collective-permute-start(f32[1024,64]{1,0:T(8,128)} %get-tuple-element.23), channel_id=1, source_target_pairs={{4,0},{8,4},{12,8},{16,12},{20,16},{24,20},{28,24},{32,28},{36,32}... | collective-permute-start | bytes 786440 | tf_op jit(solution)/shard_map/ppermute | solution.py:259
  68.8 1.9 copy-start.2
  70.7 0.8 copy-start.5
  111.6 10.8 %collective-permute-start.2 = (f32[1024,64]{1,0:T(8,128)}, f32[1024,64]{1,0:T(8,128)S(1)}, u32[]{:S(2)}, u32[]{:S(2)}) collective-permute-start(f32[1024,64]{1,0:T(8,128)} %get-tuple-element.27), channel_id=1, source_target_pairs={{0,4},{4,8},{8,12},{12,16},{16,20},{20,24},{24,28},{28,32},{32,36}... | collective-permute-start | bytes 786440 | tf_op jit(solution)/shard_map/ppermute | solution.py:258
  117.3 8.9 %collective-permute-start.3 = (f32[1024,64]{1,0:T(8,128)}, f32[1024,64]{1,0:T(8,128)S(1)}, u32[]{:S(2)}, u32[]{:S(2)}) collective-permute-start(f32[1024,64]{1,0:T(8,128)} %get-tuple-element.28), channel_id=1, source_target_pairs={{4,0},{8,4},{12,8},{16,12},{20,16},{24,20},{28,24},{32,28},{36,32}... | collective-permute-start | bytes 786440 | tf_op jit(solution)/shard_map/ppermute | solution.py:259
  122.4 3.8 %copy-start.3 = (f32[1024,64]{1,0:T(8,128)}, f32[1024,64]{1,0:T(8,128)S(1)}, u32[]{:S(2)}) copy-start(f32[1024,64]{1,0:T(8,128)S(1)} %collective-permute-done.2.refs_3_) | copy-start | bytes 786436
  126.2 0.8 copy-start.6
  168.5 10.8 %collective-permute-start.4 = (f32[1024,64]{1,0:T(8,128)}, f32[1024,64]{1,0:T(8,128)S(1)}, u32[]{:S(2)}, u32[]{:S(2)}) collective-permute-start(f32[1024,64]{1,0:T(8,128)} %get-tuple-element.30), channel_id=1, source_target_pairs={{0,4},{4,8},{8,12},{12,16},{16,20},{20,24},{24,28},{28,32},{32,36}... | collective-permute-start | bytes 786440 | tf_op jit(solution)/shard_map/ppermute | solution.py:258
  174.3 8.9 %collective-permute-start.5 = (f32[1024,64]{1,0:T(8,128)}, f32[1024,64]{1,0:T(8,128)S(1)}, u32[]{:S(2)}, u32[]{:S(2)}) collective-permute-start(f32[1024,64]{1,0:T(8,128)} %get-tuple-element.31), channel_id=1, source_target_pairs={{4,0},{8,4},{12,8},{16,12},{20,16},{24,20},{28,24},{32,28},{36,32}... | collective-permute-start | bytes 786440 | tf_op jit(solution)/shard_map/ppermute | solution.py:259
  179.2 4.0 %copy-start = (f32[1024,64]{1,0:T(8,128)}, f32[1024,64]{1,0:T(8,128)S(1)}, u32[]{:S(2)}) copy-start(f32[1024,64]{1,0:T(8,128)S(1)} %collective-permute-done.4.refs_3_) | copy-start | bytes 786436
  183.2 0.8 copy-start.1
  225.4 10.8 %collective-permute-start.6 = (f32[1024,64]{1,0:T(8,128)}, f32[1024,64]{1,0:T(8,128)S(1)}, u32[]{:S(2)}, u32[]{:S(2)}) collective-permute-start(f32[1024,64]{1,0:T(8,128)} %get-tuple-element.34), channel_id=1, source_target_pairs={{0,4},{4,8},{8,12},{12,16},{16,20},{20,24},{24,28},{28,32},{32,36}... | collective-permute-start | bytes 786440 | tf_op jit(solution)/shard_map/ppermute | solution.py:258
  231.3 8.9 %collective-permute-start.7 = (f32[1024,64]{1,0:T(8,128)}, f32[1024,64]{1,0:T(8,128)S(1)}, u32[]{:S(2)}, u32[]{:S(2)}) collective-permute-start(f32[1024,64]{1,0:T(8,128)} %get-tuple-element.35), channel_id=1, source_target_pairs={{4,0},{8,4},{12,8},{16,12},{20,16},{24,20},{28,24},{32,28},{36,32}... | collective-permute-start | bytes 786440 | tf_op jit(solution)/shard_map/ppermute | solution.py:259
  236.2 4.0 %copy-start.4 = (f32[1024,64]{1,0:T(8,128)}, f32[1024,64]{1,0:T(8,128)S(1)}, u32[]{:S(2)}) copy-start(f32[1024,64]{1,0:T(8,128)S(1)} %collective-permute-done.6.refs_2_) | copy-start | bytes 786436
  240.2 0.8 copy-start.7
  263.7 25.0 %all-to-all-start = ((bf16[64,4,3072]{2,0,1:T(8,128)(2,1)}), bf16[64,4,3072]{2,0,1:T(8,128)(2,1)S(1)}, u32[]{:S(2)}, u32[]{:S(2)}) async-start(bf16[64,4,3072]{2,0,1:T(8,128)(2,1)} %bitcast.49), calls=%async_computation | async-start | bytes 3145728 | tf_op jit(solution)/shard_map/all_to_all | solution.py:278
  289.5 3.7 %collective-permute-start.8 = (f32[256,256]{1,0:T(8,128)S(1)}, f32[256,256]{1,0:T(8,128)S(1)}, u32[]{:S(2)}, u32[]{:S(2)}) collective-permute-start(f32[256,256]{1,0:T(8,128)S(1)} %fusion.9), channel_id=1, source_target_pairs={{0,4},{1,5},{2,6},{3,7},{4,0},{5,1},{6,2},{7,3},{8,12},{9,13},{10,... | collective-permute-start | bytes 786440 | tf_op jit(solution)/shard_map/ppermute | solution.py:222
  293.2 8.7 %collective-permute-start.9 = (f32[256,256]{1,0:T(8,128)S(1)}, f32[256,256]{1,0:T(8,128)S(1)}, u32[]{:S(2)}, u32[]{:S(2)}) collective-permute-start(f32[256,256]{1,0:T(8,128)S(1)} %add.53), channel_id=1, source_target_pairs={{0,1},{1,0},{2,3},{3,2},{4,5},{5,4},{6,7},{7,6},{8,9},{9,8},{10,11... | collective-permute-start | bytes 786440 | tf_op jit(solution)/shard_map/ppermute | solution.py:222
  301.9 9.5 %collective-permute-start.10 = (f32[256,256]{1,0:T(8,128)S(1)}, f32[256,256]{1,0:T(8,128)S(1)}, u32[]{:S(2)}, u32[]{:S(2)}) collective-permute-start(f32[256,256]{1,0:T(8,128)S(1)} %add.54), channel_id=1, source_target_pairs={{0,2},{1,3},{2,0},{3,1},{4,6},{5,7},{6,4},{7,5},{8,10},{9,11},{10,... | collective-permute-start | bytes 786440 | tf_op jit(solution)/shard_map/ppermute | solution.py:222
  311.5 7.6 %collective-permute-start.11 = (f32[256,256]{1,0:T(8,128)S(1)}, f32[256,256]{1,0:T(8,128)S(1)}, u32[]{:S(2)}, u32[]{:S(2)}) collective-permute-start(f32[256,256]{1,0:T(8,128)S(1)} %add.55), channel_id=1, source_target_pairs={{0,8},{1,9},{2,10},{3,11},{4,12},{5,13},{6,14},{7,15},{8,0},{9,1},... | collective-permute-start | bytes 786440 | tf_op jit(solution)/shard_map/ppermute | solution.py:222
  319.1 8.0 %collective-permute-start.12 = (f32[256,256]{1,0:T(8,128)S(1)}, f32[256,256]{1,0:T(8,128)S(1)}, u32[]{:S(2)}, u32[]{:S(2)}) collective-permute-start(f32[256,256]{1,0:T(8,128)S(1)} %add.56), channel_id=1, source_target_pairs={{0,16},{1,17},{2,18},{3,19},{4,20},{5,21},{6,22},{7,23},{8,24},{9,... | collective-permute-start | bytes 786440 | tf_op jit(solution)/shard_map/ppermute | solution.py:222
  327.1 8.3 %collective-permute-start.13 = (f32[256,256]{1,0:T(8,128)S(1)}, f32[256,256]{1,0:T(8,128)S(1)}, u32[]{:S(2)}, u32[]{:S(2)}) collective-permute-start(f32[256,256]{1,0:T(8,128)S(1)} %add.57), channel_id=1, source_target_pairs={{0,32},{1,33},{2,34},{3,35},{4,36},{5,37},{6,38},{7,39},{8,40},{9,... | collective-permute-start | bytes 786440 | tf_op jit(solution)/shard_map/ppermute | solution.py:222
  335.5 8.0 %collective-permute-start.14 = (f32[256,256]{1,0:T(8,128)S(1)}, f32[256,256]{1,0:T(8,128)S(1)}, u32[]{:S(2)}, u32[]{:S(2)}) collective-permute-start(f32[256,256]{1,0:T(8,128)S(1)} %add.58), channel_id=1, source_target_pairs={{0,64},{1,65},{2,66},{3,67},{4,68},{5,69},{6,70},{7,71},{8,72},{9,... | collective-permute-start | bytes 786440 | tf_op jit(solution)/shard_map/ppermute | solution.py:222

commit v6 on v4

--- a/solution.py
+++ b/solution.py
@@ -12,6 +12,7 @@
 
 
 VMEM_LIMIT = 60 * 1024 * 1024
+GROUP = 2
 
 
 def field_kernel(combine, older, apply, build, alpha, *refs):
@@ -77,25 +78,29 @@
         def _():
             local_out[...] = jnp.zeros_like(local_out)
 
-        start = pl.multiple_of(cell * body_rows, quarter)
-        tail = pl.multiple_of(lax.rem((cell + 1) * body_rows, node_total), quarter)
-        main_rows = vector[pl.ds(start, body_rows), :]
-        tail_rows = vector[pl.ds(tail, quarter), :]
-        if build:
-            ops, pot_row = build_operator(ops_ref[0], pot_ref[0], kinetic_ref[...])
-            ops_out[0] = ops
-            pot_out[0] = pot_row
-        else:
-            ops = ops_ref[0]
-            pot_row = pot_ref[0]
-        product = jnp.dot(ops[:, :body_rows], main_rows, preferred_element_type=jnp.float32)
-        product = product + jnp.dot(ops[:, body_rows:], tail_rows, preferred_element_type=jnp.float32)
-        scale = scales[cell]
-        pot = jnp.transpose(jnp.broadcast_to(pot_row, (8, width)))[:, 0:1]
-        top = product[:body_rows] * scale + pot[:body_rows] * main_rows.astype(jnp.float32)
-        bottom = product[body_rows:] * scale + pot[body_rows:] * tail_rows.astype(jnp.float32)
-        local_out[pl.ds(start, body_rows), :] += top
-        local_out[pl.ds(tail, quarter), :] += bottom
+        for k in range(GROUP):
+            index = cell * GROUP + k
+            start = pl.multiple_of(index * body_rows, quarter)
+            tail = pl.multiple_of(lax.rem((index + 1) * body_rows, node_total), quarter)
+            main_rows = vector[pl.ds(start, body_rows), :]
+            tail_rows = vector[pl.ds(tail, quarter), :]
+            if build:
+                ops, pot_row = build_operator(ops_ref[k], pot_ref[k], kinetic_ref[...])
+                ops_out[k] = ops
+                pot_out[k] = pot_row
+            else:
+                ops = ops_ref[k]
+                pot_row = pot_ref[k]
+            product = jnp.dot(ops[:, :body_rows], main_rows, preferred_element_type=jnp.float32)
+            product = product + jnp.dot(
+                ops[:, body_rows:], tail_rows, preferred_element_type=jnp.float32
+            )
+            scale = scales[index]
+            pot = jnp.transpose(jnp.broadcast_to(pot_row, (8, width)))[:, 0:1]
+            top = product[:body_rows] * scale + pot[:body_rows] * main_rows.astype(jnp.float32)
+            bottom = product[body_rows:] * scale + pot[body_rows:] * tail_rows.astype(jnp.float32)
+            local_out[pl.ds(start, body_rows), :] += top
+            local_out[pl.ds(tail, quarter), :] += bottom
 
         @pl.when(cell == pl.num_programs(0) - 1)
         def _():
@@ -127,8 +132,8 @@
             args.append(older); specs.append(whole)
     else:
         args.append(vector); specs.append(whole)
-    cell_block = pl.BlockSpec((1, width, width), lambda c: (c, 0, 0))
-    row_block = pl.BlockSpec((1, 1, width), lambda c: (c, 0, 0))
+    cell_block = pl.BlockSpec((GROUP, width, width), lambda c: (c, 0, 0))
+    row_block = pl.BlockSpec((GROUP, 1, width), lambda c: (c, 0, 0))
     if apply:
         args += [window_ops, window_pot]
         specs += [row_block if build else cell_block, row_block]
@@ -150,7 +155,7 @@
     flops = (2 * cells * width * width * cols if apply else 0) + (4 * cells * width ** 3 if build else 0)
     result = pl.pallas_call(
         functools.partial(field_kernel, combine, has_older, apply, build, alpha),
-        grid=(cells if apply else 1,),
+        grid=(cells // GROUP if apply else 1,),
         in_specs=specs,
         out_specs=out_specs,
         out_shape=out_shape,

time: 365 us -> 333 us (0.912)
  Pallas kernels: 184 us -> 152 us
    pallas_call x5, Pallas kernels: 184 us -> 152 us  [field_step(): pl.pallas_call(functools.partial(field_kernel, combine, has_older, apply,...]
where the time goes in v6:
time: 333 us; the launch traced here: 331 us
  Pallas kernels  152 us (46%)
  waiting for transfers between devices  84.1 us (25%)
  starting transfers between devices  42.6 us (13%)
  local copies, waits for them, and re-layouts  23.1 us (7%)
  blocking collectives  17.2 us (5%)
  matrix products  6.39 us (2%)
  other arithmetic  3.97 us (1%)
    pallas_call x5, Pallas kernels, field_step(): pl.pallas_call(functools.partial(field_kernel, combine, has_older, apply,...  152 us
    ppermute x7, waiting for transfers between devices, doubling_sum(): total = total + lax.ppermute(total, ('dom', 'band'), pairs)  44.8 us
    ppermute x4, starting transfers between devices, exchange(): from_left = lax.ppermute(right_values, 'dom', up)  19.2 us
    all_to_all x1, blocking collectives, body(): lax.all_to_all(rotated, 'band', split_axis=1, concat_axis=0, tiled=True)  17.2 us
    ppermute x4, waiting for transfers between devices, exchange(): from_left = lax.ppermute(right_values, 'dom', up)  14.3 us
    ppermute x4, waiting for transfers between devices, exchange(): from_right = lax.ppermute(left_values, 'dom', down)  13.6 us
    all_to_all x1, waiting for transfers between devices, body(): lax.all_to_all(current, 'band', split_axis=0, concat_axis=1, tiled=True)  11.3 us
    ppermute x4, starting transfers between devices, exchange(): from_right = lax.ppermute(left_values, 'dom', down)  9.4 us
  transfers between devices with their start and end apart: 16, of which 16 were waited for; matrix products, arithmetic and copies ran while one was open for 2% of the time, Pallas kernels for 0%

profile of v6, /device:TPU:6, one launch (start us, length us, event | category | flops | bytes accessed | tf_op | source)
XLA Modules:
  0.0 331.1 jit_solution(18355525253119640427)
XLA Ops:
  4.7 4.2 %copy.10 = bf16[64,12288]{0,1:T(8,128)(2,1)} copy(bf16[64,12288]{1,0:T(8,128)(2,1)} %param.7) | data formatting | bytes 3145728 | tf_op args[0]
  9.9 42.3 %shard_map.73 = (f32[12288,64]{1,0:T(8,128)}, f32[1024,64]{1,0:T(8,128)}, f32[1024,64]{1,0:T(8,128)}, bf16[32,512,512]{2,1,0:T(8,128)(2,1)}, f32[32,1,512]{2,1,0:T(1,128)}) custom-call(s32[2048]{0:T(1024)} %pad_add_fusion.refs_0_, f32[32]{0:T(128)} %compare_select_fusion.1.refs_1_, bf16[12288,64]{1,0:T(8,128)(2,1)} %bitcast.55, ...), custom_call_target="tpu_custom_call" | custom-call | flops 18253611008 | bytes 26214400 | tf_op jit(solution)/shard_map/pallas_call | solution.py:156
  54.2 3.6 %collective-permute-start.1 = (f32[1024,64]{1,0:T(8,128)}, f32[1024,64]{1,0:T(8,128)S(1)}, u32[]{:S(2)}, u32[]{:S(2)}) collective-permute-start(f32[1024,64]{1,0:T(8,128)} %get-tuple-element.23), channel_id=1, source_target_pairs={{4,0},{8,4},{12,8},{16,12},{20,16},{24,20},{28,24},{32,28},{36,32}... | collective-permute-start | bytes 786440 | tf_op jit(solution)/shard_map/ppermute | solution.py:252
  57.8 5.1 %collective-permute-done.refs_3_ = f32[1024,64]{1,0:T(8,128)S(1)} collective-permute-done((f32[1024,64]{1,0:T(8,128)}, f32[1024,64]{1,0:T(8,128)S(1)}, u32[]{:S(2)}, u32[]{:S(2)}) %collective-permute-start) | collective-permute-done | bytes 262176 | tf_op jit(solution)/shard_map/ppermute | solution.py:251
  65.6 31.3 %shard_map.74 = (bf16[12288,64]{1,0:T(8,128)(2,1)}, f32[12288,64]{1,0:T(8,128)}, f32[1024,64]{1,0:T(8,128)}, f32[1024,64]{1,0:T(8,128)}) custom-call(s32[2048]{0:T(1024)} %pad_add_fusion.refs_0_, f32[32]{0:T(128)} %compare_select_fusion.1.refs_1_, f32[12288,64]{1,0:T(8,128)} %get-tuple-element.21.refs_2_, f32[1024,64]{1,0:T(8,128)} %copy-done.2, ...), custom_call_target="tpu_custom_call" | custom-call | flops 1073741824 | bytes 26214400 | tf_op jit(solution)/shard_map/pallas_call | solution.py:156
  96.9 5.7 %collective-permute-start.2 = (f32[1024,64]{1,0:T(8,128)}, f32[1024,64]{1,0:T(8,128)S(1)}, u32[]{:S(2)}, u32[]{:S(2)}) collective-permute-start(f32[1024,64]{1,0:T(8,128)} %get-tuple-element.27), channel_id=1, source_target_pairs={{0,4},{4,8},{8,12},{12,16},{16,20},{20,24},{24,28},{28,32},{32,36}... | collective-permute-start | bytes 786440 | tf_op jit(solution)/shard_map/ppermute | solution.py:251
  102.6 1.9 collective-permute-start.3
  104.5 3.2 collective-permute-done.2.refs_3_
  107.6 3.8 %collective-permute-done.3.refs_4_ = f32[1024,64]{1,0:T(8,128)S(1)} collective-permute-done((f32[1024,64]{1,0:T(8,128)}, f32[1024,64]{1,0:T(8,128)S(1)}, u32[]{:S(2)}, u32[]{:S(2)}) %collective-permute-start.3) | collective-permute-done | bytes 262176 | tf_op jit(solution)/shard_map/ppermute | solution.py:252
  112.3 33.0 %shard_map.75 = (bf16[12288,64]{1,0:T(8,128)(2,1)}, f32[12288,64]{1,0:T(8,128)}, f32[1024,64]{1,0:T(8,128)}, f32[1024,64]{1,0:T(8,128)}) custom-call(s32[2048]{0:T(1024)} %pad_add_fusion.refs_0_, f32[32]{0:T(128)} %compare_select_fusion.1.refs_1_, f32[12288,64]{1,0:T(8,128)} %get-tuple-element.26.refs_2_, f32[1024,64]{1,0:T(8,128)} %copy-done.3, ...), custom_call_target="tpu_custom_call" | custom-call | flops 1073741824 | bytes 26214400 | tf_op jit(solution)/shard_map/pallas_call | solution.py:156
  145.3 5.8 %collective-permute-start.4 = (f32[1024,64]{1,0:T(8,128)}, f32[1024,64]{1,0:T(8,128)S(1)}, u32[]{:S(2)}, u32[]{:S(2)}) collective-permute-start(f32[1024,64]{1,0:T(8,128)} %get-tuple-element.30), channel_id=1, source_target_pairs={{0,4},{4,8},{8,12},{12,16},{16,20},{20,24},{24,28},{28,32},{32,36}... | collective-permute-start | bytes 786440 | tf_op jit(solution)/shard_map/ppermute | solution.py:251
  151.1 1.9 collective-permute-start.5
  153.0 3.0 collective-permute-done.4.refs_3_
  156.1 4.0 %collective-permute-done.5.refs_4_ = f32[1024,64]{1,0:T(8,128)S(1)} collective-permute-done((f32[1024,64]{1,0:T(8,128)}, f32[1024,64]{1,0:T(8,128)S(1)}, u32[]{:S(2)}, u32[]{:S(2)}) %collective-permute-start.5) | collective-permute-done | bytes 262176 | tf_op jit(solution)/shard_map/ppermute | solution.py:252
  160.8 32.9 %shard_map.76 = (bf16[12288,64]{1,0:T(8,128)(2,1)}, f32[12288,64]{1,0:T(8,128)}, f32[1024,64]{1,0:T(8,128)}, f32[1024,64]{1,0:T(8,128)}) custom-call(s32[2048]{0:T(1024)} %pad_add_fusion.refs_0_, f32[32]{0:T(128)} %compare_select_fusion.1.refs_1_, f32[12288,64]{1,0:T(8,128)} %get-tuple-element.29.refs_2_, f32[1024,64]{1,0:T(8,128)} %copy-done, ...), custom_call_target="tpu_custom_call" | custom-call | flops 1073741824 | bytes 26214400 | tf_op jit(solution)/shard_map/pallas_call | solution.py:156
  193.8 5.8 %collective-permute-start.6 = (f32[1024,64]{1,0:T(8,128)}, f32[1024,64]{1,0:T(8,128)S(1)}, u32[]{:S(2)}, u32[]{:S(2)}) collective-permute-start(f32[1024,64]{1,0:T(8,128)} %get-tuple-element.34), channel_id=1, source_target_pairs={{0,4},{4,8},{8,12},{12,16},{16,20},{20,24},{24,28},{28,32},{32,36}... | collective-permute-start | bytes 786440 | tf_op jit(solution)/shard_map/ppermute | solution.py:251
  201.5 3.0 collective-permute-done.6.refs_2_
  204.5 4.0 %collective-permute-done.7.refs_3_ = f32[1024,64]{1,0:T(8,128)S(1)} collective-permute-done((f32[1024,64]{1,0:T(8,128)}, f32[1024,64]{1,0:T(8,128)S(1)}, u32[]{:S(2)}, u32[]{:S(2)}) %collective-permute-start.7) | collective-permute-done | bytes 262176 | tf_op jit(solution)/shard_map/ppermute | solution.py:252
  209.3 12.5 %shard_map.77 = bf16[12288,64]{1,0:T(8,128)(2,1)} custom-call(s32[2048]{0:T(1024)} %pad_add_fusion.refs_0_, f32[12288,64]{1,0:T(8,128)} %get-tuple-element.33.refs_1_, f32[1024,64]{1,0:T(8,128)} %copy-done.4, f32[1024,64]{1,0:T(8,128)} %copy-done.7, bf16[12288,64]{1,0:T(8,128)(2,1)} %get-tuple-element.36.refs_4_), custom_call_target="tpu_custom_call" | custom-call | bytes 9437184 | tf_op jit(solution)/shard_map/pallas_call | solution.py:156
  221.8 4.3 %copy.11 = bf16[4,3072,64]{1,2,0:T(8,128)(2,1)} copy(bf16[4,3072,64]{2,1,0:T(8,128)(2,1)} %bitcast.54) | data formatting | bytes 3145728 | tf_op jit(solution)/shard_map/all_to_all | solution.py:271
  226.1 5.2 %all-to-all-start = ((bf16[4,3072,64]{1,2,0:T(8,128)(2,1)}), bf16[4,3072,64]{1,2,0:T(8,128)(2,1)S(1)}, u32[]{:S(2)}, u32[]{:S(2)}) async-start(bf16[4,3072,64]{1,2,0:T(8,128)(2,1)} %copy.11), calls=%async_computation | async-start | bytes 3145728 | tf_op jit(solution)/shard_map/all_to_all | solution.py:271
  231.3 8.1 %scatter_custom_fusion = f32[12288]{0:T(1024)S(1)} fusion(s32[2048]{0:T(1024)S(1)} %bitcast.62, f32[2048]{0:T(1024)S(1)} %add_divide_fusion, f32[]{:T(128)} %constant.17.clone.1), kind=kCustom, calls=%fused_computation.23 | custom fusion | bytes 49156 | tf_op jit(solution)/shard_map/scatter | solution.py:237
  239.4 11.3 %all-to-all-done = bf16[4,3072,64]{1,2,0:T(8,128)(2,1)S(1)} async-done(((bf16[4,3072,64]{1,2,0:T(8,128)(2,1)}), bf16[4,3072,64]{1,2,0:T(8,128)(2,1)S(1)}, u32[]{:S(2)}, u32[]{:S(2)}) %all-to-all-start) | async-done | bytes 1572896 | tf_op jit(solution)/shard_map/all_to_all | solution.py:271
  251.5 2.6 collective-permute-start.8
  255.9 8.0 %collective-permute-done.9 = f32[256,256]{1,0:T(8,128)S(1)} collective-permute-done((f32[256,256]{1,0:T(8,128)S(1)}, f32[256,256]{1,0:T(8,128)S(1)}, u32[]{:S(2)}, u32[]{:S(2)}) %collective-permute-start.9) | collective-permute-done | bytes 262176 | tf_op jit(solution)/shard_map/ppermute | solution.py:215
  264.9 8.3 %collective-permute-done.10 = f32[256,256]{1,0:T(8,128)S(1)} collective-permute-done((f32[256,256]{1,0:T(8,128)S(1)}, f32[256,256]{1,0:T(8,128)S(1)}, u32[]{:S(2)}, u32[]{:S(2)}) %collective-permute-start.10) | collective-permute-done | bytes 262176 | tf_op jit(solution)/shard_map/ppermute | solution.py:215
  273.4 7.5 %collective-permute-done.11 = f32[256,256]{1,0:T(8,128)S(1)} collective-permute-done((f32[256,256]{1,0:T(8,128)S(1)}, f32[256,256]{1,0:T(8,128)S(1)}, u32[]{:S(2)}, u32[]{:S(2)}) %collective-permute-start.11) | collective-permute-done | bytes 262176 | tf_op jit(solution)/shard_map/ppermute | solution.py:215
  281.1 7.9 %collective-permute-done.12 = f32[256,256]{1,0:T(8,128)S(1)} collective-permute-done((f32[256,256]{1,0:T(8,128)S(1)}, f32[256,256]{1,0:T(8,128)S(1)}, u32[]{:S(2)}, u32[]{:S(2)}) %collective-permute-start.12) | collective-permute-done | bytes 262176 | tf_op jit(solution)/shard_map/ppermute | solution.py:215
  290.6 6.7 %collective-permute-done.13 = f32[256,256]{1,0:T(8,128)S(1)} collective-permute-done((f32[256,256]{1,0:T(8,128)S(1)}, f32[256,256]{1,0:T(8,128)S(1)}, u32[]{:S(2)}, u32[]{:S(2)}) %collective-permute-start.13) | collective-permute-done | bytes 262176 | tf_op jit(solution)/shard_map/ppermute | solution.py:215
  297.3 2.8 collective-permute-start.14
  300.1 5.2 %collective-permute-done.14 = f32[256,256]{1,0:T(8,128)S(1)} collective-permute-done((f32[256,256]{1,0:T(8,128)S(1)}, f32[256,256]{1,0:T(8,128)S(1)}, u32[]{:S(2)}, u32[]{:S(2)}) %collective-permute-start.14) | collective-permute-done | bytes 262176 | tf_op jit(solution)/shard_map/ppermute | solution.py:215
  312.5 17.2 %all_to_all.38 = bf16[3072,4,64]{0,2,1:T(8,128)(2,1)S(1)} all-to-all(bf16[3072,4,64]{0,2,1:T(8,128)(2,1)S(1)} %bitcast.57), channel_id=1, replica_groups=mesh['dom'=32,'band'=4] {'band'}, dimensions={1} | all-to-all | bytes 3145728 | tf_op jit(solution)/shard_map/all_to_all | solution.py:285
  (65 shorter events, 27.2 us)
Async XLA Ops:
  4.6 4.2 %copy-start.8 = (f32[32]{0:T(128)S(1)}, f32[32]{0:T(128)}, u32[]{:S(2)}) copy-start(f32[32]{0:T(128)} %param.9) | copy-start | bytes 388
  52.2 10.7 %collective-permute-start = (f32[1024,64]{1,0:T(8,128)}, f32[1024,64]{1,0:T(8,128)S(1)}, u32[]{:S(2)}, u32[]{:S(2)}) collective-permute-start(f32[1024,64]{1,0:T(8,128)} %get-tuple-element.22), channel_id=1, source_target_pairs={{0,4},{4,8},{8,12},{12,16},{16,20},{20,24},{24,28},{28,32},{32,36}... | collective-permute-start | bytes 786440 | tf_op jit(solution)/shard_map/ppermute | solution.py:251
  54.2 10.6 %collective-permute-start.1 = (f32[1024,64]{1,0:T(8,128)}, f32[1024,64]{1,0:T(8,128)S(1)}, u32[]{:S(2)}, u32[]{:S(2)}) collective-permute-start(f32[1024,64]{1,0:T(8,128)} %get-tuple-element.23), channel_id=1, source_target_pairs={{4,0},{8,4},{12,8},{16,12},{20,16},{24,20},{28,24},{32,28},{36,32}... | collective-permute-start | bytes 786440 | tf_op jit(solution)/shard_map/ppermute | solution.py:252
  63.0 1.9 copy-start.2
  64.8 0.8 copy-start.5
  96.9 10.8 %collective-permute-start.2 = (f32[1024,64]{1,0:T(8,128)}, f32[1024,64]{1,0:T(8,128)S(1)}, u32[]{:S(2)}, u32[]{:S(2)}) collective-permute-start(f32[1024,64]{1,0:T(8,128)} %get-tuple-element.27), channel_id=1, source_target_pairs={{0,4},{4,8},{8,12},{12,16},{16,20},{20,24},{24,28},{28,32},{32,36}... | collective-permute-start | bytes 786440 | tf_op jit(solution)/shard_map/ppermute | solution.py:251
  102.6 8.9 %collective-permute-start.3 = (f32[1024,64]{1,0:T(8,128)}, f32[1024,64]{1,0:T(8,128)S(1)}, u32[]{:S(2)}, u32[]{:S(2)}) collective-permute-start(f32[1024,64]{1,0:T(8,128)} %get-tuple-element.28), channel_id=1, source_target_pairs={{4,0},{8,4},{12,8},{16,12},{20,16},{24,20},{28,24},{32,28},{36,32}... | collective-permute-start | bytes 786440 | tf_op jit(solution)/shard_map/ppermute | solution.py:252
  107.6 3.8 %copy-start.3 = (f32[1024,64]{1,0:T(8,128)}, f32[1024,64]{1,0:T(8,128)S(1)}, u32[]{:S(2)}) copy-start(f32[1024,64]{1,0:T(8,128)S(1)} %collective-permute-done.2.refs_3_) | copy-start | bytes 786436
  111.5 0.8 copy-start.6
  145.3 10.8 %collective-permute-start.4 = (f32[1024,64]{1,0:T(8,128)}, f32[1024,64]{1,0:T(8,128)S(1)}, u32[]{:S(2)}, u32[]{:S(2)}) collective-permute-start(f32[1024,64]{1,0:T(8,128)} %get-tuple-element.30), channel_id=1, source_target_pairs={{0,4},{4,8},{8,12},{12,16},{16,20},{20,24},{24,28},{28,32},{32,36}... | collective-permute-start | bytes 786440 | tf_op jit(solution)/shard_map/ppermute | solution.py:251
  151.1 8.9 %collective-permute-start.5 = (f32[1024,64]{1,0:T(8,128)}, f32[1024,64]{1,0:T(8,128)S(1)}, u32[]{:S(2)}, u32[]{:S(2)}) collective-permute-start(f32[1024,64]{1,0:T(8,128)} %get-tuple-element.31), channel_id=1, source_target_pairs={{4,0},{8,4},{12,8},{16,12},{20,16},{24,20},{28,24},{32,28},{36,32}... | collective-permute-start | bytes 786440 | tf_op jit(solution)/shard_map/ppermute | solution.py:252
  156.1 4.0 %copy-start = (f32[1024,64]{1,0:T(8,128)}, f32[1024,64]{1,0:T(8,128)S(1)}, u32[]{:S(2)}) copy-start(f32[1024,64]{1,0:T(8,128)S(1)} %collective-permute-done.4.refs_3_) | copy-start | bytes 786436
  160.0 0.8 copy-start.1
  193.8 10.8 %collective-permute-start.6 = (f32[1024,64]{1,0:T(8,128)}, f32[1024,64]{1,0:T(8,128)S(1)}, u32[]{:S(2)}, u32[]{:S(2)}) collective-permute-start(f32[1024,64]{1,0:T(8,128)} %get-tuple-element.34), channel_id=1, source_target_pairs={{0,4},{4,8},{8,12},{12,16},{16,20},{20,24},{24,28},{28,32},{32,36}... | collective-permute-start | bytes 786440 | tf_op jit(solution)/shard_map/ppermute | solution.py:251
  199.6 8.9 %collective-permute-start.7 = (f32[1024,64]{1,0:T(8,128)}, f32[1024,64]{1,0:T(8,128)S(1)}, u32[]{:S(2)}, u32[]{:S(2)}) collective-permute-start(f32[1024,64]{1,0:T(8,128)} %get-tuple-element.35), channel_id=1, source_target_pairs={{4,0},{8,4},{12,8},{16,12},{20,16},{24,20},{28,24},{32,28},{36,32}... | collective-permute-start | bytes 786440 | tf_op jit(solution)/shard_map/ppermute | solution.py:252
  204.5 4.0 %copy-start.4 = (f32[1024,64]{1,0:T(8,128)}, f32[1024,64]{1,0:T(8,128)S(1)}, u32[]{:S(2)}) copy-start(f32[1024,64]{1,0:T(8,128)S(1)} %collective-permute-done.6.refs_2_) | copy-start | bytes 786436
  208.5 0.8 copy-start.7
  226.1 24.7 %all-to-all-start = ((bf16[4,3072,64]{1,2,0:T(8,128)(2,1)}), bf16[4,3072,64]{1,2,0:T(8,128)(2,1)S(1)}, u32[]{:S(2)}, u32[]{:S(2)}) async-start(bf16[4,3072,64]{1,2,0:T(8,128)(2,1)} %copy.11), calls=%async_computation | async-start | bytes 3145728 | tf_op jit(solution)/shard_map/all_to_all | solution.py:271
  251.5 3.7 %collective-permute-start.8 = (f32[256,256]{1,0:T(8,128)S(1)}, f32[256,256]{1,0:T(8,128)S(1)}, u32[]{:S(2)}, u32[]{:S(2)}) collective-permute-start(f32[256,256]{1,0:T(8,128)S(1)} %fusion.9), channel_id=1, source_target_pairs={{0,4},{1,5},{2,6},{3,7},{4,0},{5,1},{6,2},{7,3},{8,12},{9,13},{10,... | collective-permute-start | bytes 786440 | tf_op jit(solution)/shard_map/ppermute | solution.py:215
  255.3 8.7 %collective-permute-start.9 = (f32[256,256]{1,0:T(8,128)S(1)}, f32[256,256]{1,0:T(8,128)S(1)}, u32[]{:S(2)}, u32[]{:S(2)}) collective-permute-start(f32[256,256]{1,0:T(8,128)S(1)} %add.53), channel_id=1, source_target_pairs={{0,1},{1,0},{2,3},{3,2},{4,5},{5,4},{6,7},{7,6},{8,9},{9,8},{10,11... | collective-permute-start | bytes 786440 | tf_op jit(solution)/shard_map/ppermute | solution.py:215
  264.0 9.3 %collective-permute-start.10 = (f32[256,256]{1,0:T(8,128)S(1)}, f32[256,256]{1,0:T(8,128)S(1)}, u32[]{:S(2)}, u32[]{:S(2)}) collective-permute-start(f32[256,256]{1,0:T(8,128)S(1)} %add.54), channel_id=1, source_target_pairs={{0,2},{1,3},{2,0},{3,1},{4,6},{5,7},{6,4},{7,5},{8,10},{9,11},{10,... | collective-permute-start | bytes 786440 | tf_op jit(solution)/shard_map/ppermute | solution.py:215
  273.3 7.6 %collective-permute-start.11 = (f32[256,256]{1,0:T(8,128)S(1)}, f32[256,256]{1,0:T(8,128)S(1)}, u32[]{:S(2)}, u32[]{:S(2)}) collective-permute-start(f32[256,256]{1,0:T(8,128)S(1)} %add.55), channel_id=1, source_target_pairs={{0,8},{1,9},{2,10},{3,11},{4,12},{5,13},{6,14},{7,15},{8,0},{9,1},... | collective-permute-start | bytes 786440 | tf_op jit(solution)/shard_map/ppermute | solution.py:215
  281.0 8.0 %collective-permute-start.12 = (f32[256,256]{1,0:T(8,128)S(1)}, f32[256,256]{1,0:T(8,128)S(1)}, u32[]{:S(2)}, u32[]{:S(2)}) collective-permute-start(f32[256,256]{1,0:T(8,128)S(1)} %add.56), channel_id=1, source_target_pairs={{0,16},{1,17},{2,18},{3,19},{4,20},{5,21},{6,22},{7,23},{8,24},{9,... | collective-permute-start | bytes 786440 | tf_op jit(solution)/shard_map/ppermute | solution.py:215
  289.0 8.3 %collective-permute-start.13 = (f32[256,256]{1,0:T(8,128)S(1)}, f32[256,256]{1,0:T(8,128)S(1)}, u32[]{:S(2)}, u32[]{:S(2)}) collective-permute-start(f32[256,256]{1,0:T(8,128)S(1)} %add.57), channel_id=1, source_target_pairs={{0,32},{1,33},{2,34},{3,35},{4,36},{5,37},{6,38},{7,39},{8,40},{9,... | collective-permute-start | bytes 786440 | tf_op jit(solution)/shard_map/ppermute | solution.py:215
  297.3 8.0 %collective-permute-start.14 = (f32[256,256]{1,0:T(8,128)S(1)}, f32[256,256]{1,0:T(8,128)S(1)}, u32[]{:S(2)}, u32[]{:S(2)}) collective-permute-start(f32[256,256]{1,0:T(8,128)S(1)} %add.58), channel_id=1, source_target_pairs={{0,64},{1,65},{2,66},{3,67},{4,68},{5,69},{6,70},{7,71},{8,72},{9,... | collective-permute-start | bytes 786440 | tf_op jit(solution)/shard_map/ppermute | solution.py:215

commit v7 on v6

--- a/solution.py
+++ b/solution.py
@@ -12,7 +12,7 @@
 
 
 VMEM_LIMIT = 60 * 1024 * 1024
-GROUP = 2
+GROUP = 4
 
 
 def field_kernel(combine, older, apply, build, alpha, *refs):

time: 333 us -> 316 us (0.949)
  Pallas kernels: 152 us -> 136 us
    pallas_call x5, Pallas kernels: 152 us -> 136 us  [field_step(): pl.pallas_call(functools.partial(field_kernel, combine, has_older, apply,...]
  transfers between devices with their start and end apart: 16 -> 16, of which waited for: 16 -> 16; matrix products, arithmetic and copies ran while one was open for 2% -> 3% of each run, Pallas kernels for 0% -> 0%
where the time goes in v7:
time: 316 us; the launch traced here: 315 us
  Pallas kernels  136 us (43%)
  waiting for transfers between devices  84 us (27%)
  starting transfers between devices  42.8 us (14%)
  local copies, waits for them, and re-layouts  23.1 us (7%)
  blocking collectives  17.2 us (5%)
  matrix products  6.39 us (2%)
  other arithmetic  3.97 us (1%)
    pallas_call x5, Pallas kernels, field_step(): pl.pallas_call(functools.partial(field_kernel, combine, has_older, apply,...  136 us
    ppermute x7, waiting for transfers between devices, doubling_sum(): total = total + lax.ppermute(total, ('dom', 'band'), pairs)  44.8 us
    ppermute x4, starting transfers between devices, exchange(): from_left = lax.ppermute(right_values, 'dom', up)  19.2 us
    all_to_all x1, blocking collectives, body(): lax.all_to_all(rotated, 'band', split_axis=1, concat_axis=0, tiled=True)  17.2 us
    ppermute x4, waiting for transfers between devices, exchange(): from_left = lax.ppermute(right_values, 'dom', up)  14.2 us
    ppermute x4, waiting for transfers between devices, exchange(): from_right = lax.ppermute(left_values, 'dom', down)  13.6 us
    all_to_all x1, waiting for transfers between devices, body(): lax.all_to_all(current, 'band', split_axis=0, concat_axis=1, tiled=True)  11.3 us
    ppermute x4, starting transfers between devices, exchange(): from_right = lax.ppermute(left_values, 'dom', down)  9.58 us
  transfers between devices with their start and end apart: 16, of which 16 were waited for; matrix products, arithmetic and copies ran while one was open for 3% of the time, Pallas kernels for 0%

profile of v7, /device:TPU:6, one launch (start us, length us, event | category | flops | bytes accessed | tf_op | source)
XLA Modules:
  0.0 315.3 jit_solution(9272535551515443809)
XLA Ops:
  4.7 4.2 %copy.10 = bf16[64,12288]{0,1:T(8,128)(2,1)} copy(bf16[64,12288]{1,0:T(8,128)(2,1)} %param.7) | data formatting | bytes 3145728 | tf_op args[0]
  9.9 40.0 %shard_map.73 = (f32[12288,64]{1,0:T(8,128)}, f32[1024,64]{1,0:T(8,128)}, f32[1024,64]{1,0:T(8,128)}, bf16[32,512,512]{2,1,0:T(8,128)(2,1)}, f32[32,1,512]{2,1,0:T(1,128)}) custom-call(s32[2048]{0:T(1024)} %pad_add_fusion.refs_0_, f32[32]{0:T(128)} %compare_select_fusion.1.refs_1_, bf16[12288,64]{1,0:T(8,128)(2,1)} %bitcast.55, ...), custom_call_target="tpu_custom_call" | custom-call | flops 18253611008 | bytes 26214400 | tf_op jit(solution)/shard_map/pallas_call | solution.py:156
  51.8 3.6 %collective-permute-start.1 = (f32[1024,64]{1,0:T(8,128)}, f32[1024,64]{1,0:T(8,128)S(1)}, u32[]{:S(2)}, u32[]{:S(2)}) collective-permute-start(f32[1024,64]{1,0:T(8,128)} %get-tuple-element.23), channel_id=1, source_target_pairs={{4,0},{8,4},{12,8},{16,12},{20,16},{24,20},{28,24},{32,28},{36,32}... | collective-permute-start | bytes 786440 | tf_op jit(solution)/shard_map/ppermute | solution.py:252
  55.5 5.1 %collective-permute-done.refs_3_ = f32[1024,64]{1,0:T(8,128)S(1)} collective-permute-done((f32[1024,64]{1,0:T(8,128)}, f32[1024,64]{1,0:T(8,128)S(1)}, u32[]{:S(2)}, u32[]{:S(2)}) %collective-permute-start) | collective-permute-done | bytes 262176 | tf_op jit(solution)/shard_map/ppermute | solution.py:251
  63.3 26.8 %shard_map.74 = (bf16[12288,64]{1,0:T(8,128)(2,1)}, f32[12288,64]{1,0:T(8,128)}, f32[1024,64]{1,0:T(8,128)}, f32[1024,64]{1,0:T(8,128)}) custom-call(s32[2048]{0:T(1024)} %pad_add_fusion.refs_0_, f32[32]{0:T(128)} %compare_select_fusion.1.refs_1_, f32[12288,64]{1,0:T(8,128)} %get-tuple-element.21.refs_2_, f32[1024,64]{1,0:T(8,128)} %copy-done.2, ...), custom_call_target="tpu_custom_call" | custom-call | flops 1073741824 | bytes 26214400 | tf_op jit(solution)/shard_map/pallas_call | solution.py:156
  90.1 5.7 %collective-permute-start.2 = (f32[1024,64]{1,0:T(8,128)}, f32[1024,64]{1,0:T(8,128)S(1)}, u32[]{:S(2)}, u32[]{:S(2)}) collective-permute-start(f32[1024,64]{1,0:T(8,128)} %get-tuple-element.27), channel_id=1, source_target_pairs={{0,4},{4,8},{8,12},{12,16},{16,20},{20,24},{24,28},{28,32},{32,36}... | collective-permute-start | bytes 786440 | tf_op jit(solution)/shard_map/ppermute | solution.py:251
  95.8 1.9 collective-permute-start.3
  97.7 3.2 %collective-permute-done.2.refs_3_ = f32[1024,64]{1,0:T(8,128)S(1)} collective-permute-done((f32[1024,64]{1,0:T(8,128)}, f32[1024,64]{1,0:T(8,128)S(1)}, u32[]{:S(2)}, u32[]{:S(2)}) %collective-permute-start.2) | collective-permute-done | bytes 262176 | tf_op jit(solution)/shard_map/ppermute | solution.py:251
  100.9 3.8 %collective-permute-done.3.refs_4_ = f32[1024,64]{1,0:T(8,128)S(1)} collective-permute-done((f32[1024,64]{1,0:T(8,128)}, f32[1024,64]{1,0:T(8,128)S(1)}, u32[]{:S(2)}, u32[]{:S(2)}) %collective-permute-start.3) | collective-permute-done | bytes 262176 | tf_op jit(solution)/shard_map/ppermute | solution.py:252
  105.5 28.5 %shard_map.75 = (bf16[12288,64]{1,0:T(8,128)(2,1)}, f32[12288,64]{1,0:T(8,128)}, f32[1024,64]{1,0:T(8,128)}, f32[1024,64]{1,0:T(8,128)}) custom-call(s32[2048]{0:T(1024)} %pad_add_fusion.refs_0_, f32[32]{0:T(128)} %compare_select_fusion.1.refs_1_, f32[12288,64]{1,0:T(8,128)} %get-tuple-element.26.refs_2_, f32[1024,64]{1,0:T(8,128)} %copy-done.3, ...), custom_call_target="tpu_custom_call" | custom-call | flops 1073741824 | bytes 26214400 | tf_op jit(solution)/shard_map/pallas_call | solution.py:156
  134.0 5.8 %collective-permute-start.4 = (f32[1024,64]{1,0:T(8,128)}, f32[1024,64]{1,0:T(8,128)S(1)}, u32[]{:S(2)}, u32[]{:S(2)}) collective-permute-start(f32[1024,64]{1,0:T(8,128)} %get-tuple-element.30), channel_id=1, source_target_pairs={{0,4},{4,8},{8,12},{12,16},{16,20},{20,24},{24,28},{28,32},{32,36}... | collective-permute-start | bytes 786440 | tf_op jit(solution)/shard_map/ppermute | solution.py:251
  141.8 3.0 collective-permute-done.4.refs_3_
  144.8 4.0 %collective-permute-done.5.refs_4_ = f32[1024,64]{1,0:T(8,128)S(1)} collective-permute-done((f32[1024,64]{1,0:T(8,128)}, f32[1024,64]{1,0:T(8,128)S(1)}, u32[]{:S(2)}, u32[]{:S(2)}) %collective-permute-start.5) | collective-permute-done | bytes 262176 | tf_op jit(solution)/shard_map/ppermute | solution.py:252
  149.6 28.5 %shard_map.76 = (bf16[12288,64]{1,0:T(8,128)(2,1)}, f32[12288,64]{1,0:T(8,128)}, f32[1024,64]{1,0:T(8,128)}, f32[1024,64]{1,0:T(8,128)}) custom-call(s32[2048]{0:T(1024)} %pad_add_fusion.refs_0_, f32[32]{0:T(128)} %compare_select_fusion.1.refs_1_, f32[12288,64]{1,0:T(8,128)} %get-tuple-element.29.refs_2_, f32[1024,64]{1,0:T(8,128)} %copy-done, ...), custom_call_target="tpu_custom_call" | custom-call | flops 1073741824 | bytes 26214400 | tf_op jit(solution)/shard_map/pallas_call | solution.py:156
  178.0 5.8 %collective-permute-start.6 = (f32[1024,64]{1,0:T(8,128)}, f32[1024,64]{1,0:T(8,128)S(1)}, u32[]{:S(2)}, u32[]{:S(2)}) collective-permute-start(f32[1024,64]{1,0:T(8,128)} %get-tuple-element.34), channel_id=1, source_target_pairs={{0,4},{4,8},{8,12},{12,16},{16,20},{20,24},{24,28},{28,32},{32,36}... | collective-permute-start | bytes 786440 | tf_op jit(solution)/shard_map/ppermute | solution.py:251
  183.8 2.1 collective-permute-start.7
  185.9 2.9 collective-permute-done.6.refs_2_
  188.8 4.0 %collective-permute-done.7.refs_3_ = f32[1024,64]{1,0:T(8,128)S(1)} collective-permute-done((f32[1024,64]{1,0:T(8,128)}, f32[1024,64]{1,0:T(8,128)S(1)}, u32[]{:S(2)}, u32[]{:S(2)}) %collective-permute-start.7) | collective-permute-done | bytes 262176 | tf_op jit(solution)/shard_map/ppermute | solution.py:252
  193.6 12.5 %shard_map.77 = bf16[12288,64]{1,0:T(8,128)(2,1)} custom-call(s32[2048]{0:T(1024)} %pad_add_fusion.refs_0_, f32[12288,64]{1,0:T(8,128)} %get-tuple-element.33.refs_1_, f32[1024,64]{1,0:T(8,128)} %copy-done.4, f32[1024,64]{1,0:T(8,128)} %copy-done.7, bf16[12288,64]{1,0:T(8,128)(2,1)} %get-tuple-element.36.refs_4_), custom_call_target="tpu_custom_call" | custom-call | bytes 9437184 | tf_op jit(solution)/shard_map/pallas_call | solution.py:156
  206.0 4.3 %copy.11 = bf16[4,3072,64]{1,2,0:T(8,128)(2,1)} copy(bf16[4,3072,64]{2,1,0:T(8,128)(2,1)} %bitcast.54) | data formatting | bytes 3145728 | tf_op jit(solution)/shard_map/all_to_all | solution.py:271
  210.3 5.3 %all-to-all-start = ((bf16[4,3072,64]{1,2,0:T(8,128)(2,1)}), bf16[4,3072,64]{1,2,0:T(8,128)(2,1)S(1)}, u32[]{:S(2)}, u32[]{:S(2)}) async-start(bf16[4,3072,64]{1,2,0:T(8,128)(2,1)} %copy.11), calls=%async_computation | async-start | bytes 3145728 | tf_op jit(solution)/shard_map/all_to_all | solution.py:271
  215.7 8.1 %scatter_custom_fusion = f32[12288]{0:T(1024)S(1)} fusion(s32[2048]{0:T(1024)S(1)} %bitcast.62, f32[2048]{0:T(1024)S(1)} %add_divide_fusion, f32[]{:T(128)} %constant.17.clone.1), kind=kCustom, calls=%fused_computation.23 | custom fusion | bytes 49156 | tf_op jit(solution)/shard_map/scatter | solution.py:237
  223.8 11.3 %all-to-all-done = bf16[4,3072,64]{1,2,0:T(8,128)(2,1)S(1)} async-done(((bf16[4,3072,64]{1,2,0:T(8,128)(2,1)}), bf16[4,3072,64]{1,2,0:T(8,128)(2,1)S(1)}, u32[]{:S(2)}, u32[]{:S(2)}) %all-to-all-start) | async-done | bytes 1572896 | tf_op jit(solution)/shard_map/all_to_all | solution.py:271
  235.8 2.6 collective-permute-start.8
  240.2 8.0 %collective-permute-done.9 = f32[256,256]{1,0:T(8,128)S(1)} collective-permute-done((f32[256,256]{1,0:T(8,128)S(1)}, f32[256,256]{1,0:T(8,128)S(1)}, u32[]{:S(2)}, u32[]{:S(2)}) %collective-permute-start.9) | collective-permute-done | bytes 262176 | tf_op jit(solution)/shard_map/ppermute | solution.py:215
  249.3 8.3 %collective-permute-done.10 = f32[256,256]{1,0:T(8,128)S(1)} collective-permute-done((f32[256,256]{1,0:T(8,128)S(1)}, f32[256,256]{1,0:T(8,128)S(1)}, u32[]{:S(2)}, u32[]{:S(2)}) %collective-permute-start.10) | collective-permute-done | bytes 262176 | tf_op jit(solution)/shard_map/ppermute | solution.py:215
  257.7 7.5 %collective-permute-done.11 = f32[256,256]{1,0:T(8,128)S(1)} collective-permute-done((f32[256,256]{1,0:T(8,128)S(1)}, f32[256,256]{1,0:T(8,128)S(1)}, u32[]{:S(2)}, u32[]{:S(2)}) %collective-permute-start.11) | collective-permute-done | bytes 262176 | tf_op jit(solution)/shard_map/ppermute | solution.py:215
  265.4 7.9 %collective-permute-done.12 = f32[256,256]{1,0:T(8,128)S(1)} collective-permute-done((f32[256,256]{1,0:T(8,128)S(1)}, f32[256,256]{1,0:T(8,128)S(1)}, u32[]{:S(2)}, u32[]{:S(2)}) %collective-permute-start.12) | collective-permute-done | bytes 262176 | tf_op jit(solution)/shard_map/ppermute | solution.py:215
  274.9 6.7 %collective-permute-done.13 = f32[256,256]{1,0:T(8,128)S(1)} collective-permute-done((f32[256,256]{1,0:T(8,128)S(1)}, f32[256,256]{1,0:T(8,128)S(1)}, u32[]{:S(2)}, u32[]{:S(2)}) %collective-permute-start.13) | collective-permute-done | bytes 262176 | tf_op jit(solution)/shard_map/ppermute | solution.py:215
  281.7 2.7 collective-permute-start.14
  284.4 5.2 %collective-permute-done.14 = f32[256,256]{1,0:T(8,128)S(1)} collective-permute-done((f32[256,256]{1,0:T(8,128)S(1)}, f32[256,256]{1,0:T(8,128)S(1)}, u32[]{:S(2)}, u32[]{:S(2)}) %collective-permute-start.14) | collective-permute-done | bytes 262176 | tf_op jit(solution)/shard_map/ppermute | solution.py:215
  296.9 17.2 %all_to_all.38 = bf16[3072,4,64]{0,2,1:T(8,128)(2,1)S(1)} all-to-all(bf16[3072,4,64]{0,2,1:T(8,128)(2,1)S(1)} %bitcast.57), channel_id=1, replica_groups=mesh['dom'=32,'band'=4] {'band'}, dimensions={1} | all-to-all | bytes 3145728 | tf_op jit(solution)/shard_map/all_to_all | solution.py:285
  (65 shorter events, 27.2 us)
Async XLA Ops:
  4.6 4.2 %copy-start.8 = (f32[32]{0:T(128)S(1)}, f32[32]{0:T(128)}, u32[]{:S(2)}) copy-start(f32[32]{0:T(128)} %param.9) | copy-start | bytes 388
  49.9 10.7 %collective-permute-start = (f32[1024,64]{1,0:T(8,128)}, f32[1024,64]{1,0:T(8,128)S(1)}, u32[]{:S(2)}, u32[]{:S(2)}) collective-permute-start(f32[1024,64]{1,0:T(8,128)} %get-tuple-element.22), channel_id=1, source_target_pairs={{0,4},{4,8},{8,12},{12,16},{16,20},{20,24},{24,28},{28,32},{32,36}... | collective-permute-start | bytes 786440 | tf_op jit(solution)/shard_map/ppermute | solution.py:251
  51.8 10.6 %collective-permute-start.1 = (f32[1024,64]{1,0:T(8,128)}, f32[1024,64]{1,0:T(8,128)S(1)}, u32[]{:S(2)}, u32[]{:S(2)}) collective-permute-start(f32[1024,64]{1,0:T(8,128)} %get-tuple-element.23), channel_id=1, source_target_pairs={{4,0},{8,4},{12,8},{16,12},{20,16},{24,20},{28,24},{32,28},{36,32}... | collective-permute-start | bytes 786440 | tf_op jit(solution)/shard_map/ppermute | solution.py:252
  60.6 1.9 copy-start.2
  62.5 0.8 copy-start.5
  90.1 10.8 %collective-permute-start.2 = (f32[1024,64]{1,0:T(8,128)}, f32[1024,64]{1,0:T(8,128)S(1)}, u32[]{:S(2)}, u32[]{:S(2)}) collective-permute-start(f32[1024,64]{1,0:T(8,128)} %get-tuple-element.27), channel_id=1, source_target_pairs={{0,4},{4,8},{8,12},{12,16},{16,20},{20,24},{24,28},{28,32},{32,36}... | collective-permute-start | bytes 786440 | tf_op jit(solution)/shard_map/ppermute | solution.py:251
  95.8 8.9 %collective-permute-start.3 = (f32[1024,64]{1,0:T(8,128)}, f32[1024,64]{1,0:T(8,128)S(1)}, u32[]{:S(2)}, u32[]{:S(2)}) collective-permute-start(f32[1024,64]{1,0:T(8,128)} %get-tuple-element.28), channel_id=1, source_target_pairs={{4,0},{8,4},{12,8},{16,12},{20,16},{24,20},{28,24},{32,28},{36,32}... | collective-permute-start | bytes 786440 | tf_op jit(solution)/shard_map/ppermute | solution.py:252
  100.9 3.8 %copy-start.3 = (f32[1024,64]{1,0:T(8,128)}, f32[1024,64]{1,0:T(8,128)S(1)}, u32[]{:S(2)}) copy-start(f32[1024,64]{1,0:T(8,128)S(1)} %collective-permute-done.2.refs_3_) | copy-start | bytes 786436
  104.7 0.8 copy-start.6
  134.0 10.8 %collective-permute-start.4 = (f32[1024,64]{1,0:T(8,128)}, f32[1024,64]{1,0:T(8,128)S(1)}, u32[]{:S(2)}, u32[]{:S(2)}) collective-permute-start(f32[1024,64]{1,0:T(8,128)} %get-tuple-element.30), channel_id=1, source_target_pairs={{0,4},{4,8},{8,12},{12,16},{16,20},{20,24},{24,28},{28,32},{32,36}... | collective-permute-start | bytes 786440 | tf_op jit(solution)/shard_map/ppermute | solution.py:251
  139.9 8.9 %collective-permute-start.5 = (f32[1024,64]{1,0:T(8,128)}, f32[1024,64]{1,0:T(8,128)S(1)}, u32[]{:S(2)}, u32[]{:S(2)}) collective-permute-start(f32[1024,64]{1,0:T(8,128)} %get-tuple-element.31), channel_id=1, source_target_pairs={{4,0},{8,4},{12,8},{16,12},{20,16},{24,20},{28,24},{32,28},{36,32}... | collective-permute-start | bytes 786440 | tf_op jit(solution)/shard_map/ppermute | solution.py:252
  144.8 4.0 %copy-start = (f32[1024,64]{1,0:T(8,128)}, f32[1024,64]{1,0:T(8,128)S(1)}, u32[]{:S(2)}) copy-start(f32[1024,64]{1,0:T(8,128)S(1)} %collective-permute-done.4.refs_3_) | copy-start | bytes 786436
  148.8 0.8 copy-start.1
  178.0 10.8 %collective-permute-start.6 = (f32[1024,64]{1,0:T(8,128)}, f32[1024,64]{1,0:T(8,128)S(1)}, u32[]{:S(2)}, u32[]{:S(2)}) collective-permute-start(f32[1024,64]{1,0:T(8,128)} %get-tuple-element.34), channel_id=1, source_target_pairs={{0,4},{4,8},{8,12},{12,16},{16,20},{20,24},{24,28},{28,32},{32,36}... | collective-permute-start | bytes 786440 | tf_op jit(solution)/shard_map/ppermute | solution.py:251
  183.8 8.9 %collective-permute-start.7 = (f32[1024,64]{1,0:T(8,128)}, f32[1024,64]{1,0:T(8,128)S(1)}, u32[]{:S(2)}, u32[]{:S(2)}) collective-permute-start(f32[1024,64]{1,0:T(8,128)} %get-tuple-element.35), channel_id=1, source_target_pairs={{4,0},{8,4},{12,8},{16,12},{20,16},{24,20},{28,24},{32,28},{36,32}... | collective-permute-start | bytes 786440 | tf_op jit(solution)/shard_map/ppermute | solution.py:252
  188.8 4.0 %copy-start.4 = (f32[1024,64]{1,0:T(8,128)}, f32[1024,64]{1,0:T(8,128)S(1)}, u32[]{:S(2)}) copy-start(f32[1024,64]{1,0:T(8,128)S(1)} %collective-permute-done.6.refs_2_) | copy-start | bytes 786436
  192.7 0.8 copy-start.7
  210.3 24.8 %all-to-all-start = ((bf16[4,3072,64]{1,2,0:T(8,128)(2,1)}), bf16[4,3072,64]{1,2,0:T(8,128)(2,1)S(1)}, u32[]{:S(2)}, u32[]{:S(2)}) async-start(bf16[4,3072,64]{1,2,0:T(8,128)(2,1)} %copy.11), calls=%async_computation | async-start | bytes 3145728 | tf_op jit(solution)/shard_map/all_to_all | solution.py:271
  235.8 3.7 %collective-permute-start.8 = (f32[256,256]{1,0:T(8,128)S(1)}, f32[256,256]{1,0:T(8,128)S(1)}, u32[]{:S(2)}, u32[]{:S(2)}) collective-permute-start(f32[256,256]{1,0:T(8,128)S(1)} %fusion.9), channel_id=1, source_target_pairs={{0,4},{1,5},{2,6},{3,7},{4,0},{5,1},{6,2},{7,3},{8,12},{9,13},{10,... | collective-permute-start | bytes 786440 | tf_op jit(solution)/shard_map/ppermute | solution.py:215
  239.6 8.7 %collective-permute-start.9 = (f32[256,256]{1,0:T(8,128)S(1)}, f32[256,256]{1,0:T(8,128)S(1)}, u32[]{:S(2)}, u32[]{:S(2)}) collective-permute-start(f32[256,256]{1,0:T(8,128)S(1)} %add.53), channel_id=1, source_target_pairs={{0,1},{1,0},{2,3},{3,2},{4,5},{5,4},{6,7},{7,6},{8,9},{9,8},{10,11... | collective-permute-start | bytes 786440 | tf_op jit(solution)/shard_map/ppermute | solution.py:215
  248.3 9.3 %collective-permute-start.10 = (f32[256,256]{1,0:T(8,128)S(1)}, f32[256,256]{1,0:T(8,128)S(1)}, u32[]{:S(2)}, u32[]{:S(2)}) collective-permute-start(f32[256,256]{1,0:T(8,128)S(1)} %add.54), channel_id=1, source_target_pairs={{0,2},{1,3},{2,0},{3,1},{4,6},{5,7},{6,4},{7,5},{8,10},{9,11},{10,... | collective-permute-start | bytes 786440 | tf_op jit(solution)/shard_map/ppermute | solution.py:215
  257.6 7.6 %collective-permute-start.11 = (f32[256,256]{1,0:T(8,128)S(1)}, f32[256,256]{1,0:T(8,128)S(1)}, u32[]{:S(2)}, u32[]{:S(2)}) collective-permute-start(f32[256,256]{1,0:T(8,128)S(1)} %add.55), channel_id=1, source_target_pairs={{0,8},{1,9},{2,10},{3,11},{4,12},{5,13},{6,14},{7,15},{8,0},{9,1},... | collective-permute-start | bytes 786440 | tf_op jit(solution)/shard_map/ppermute | solution.py:215
  265.3 8.0 %collective-permute-start.12 = (f32[256,256]{1,0:T(8,128)S(1)}, f32[256,256]{1,0:T(8,128)S(1)}, u32[]{:S(2)}, u32[]{:S(2)}) collective-permute-start(f32[256,256]{1,0:T(8,128)S(1)} %add.56), channel_id=1, source_target_pairs={{0,16},{1,17},{2,18},{3,19},{4,20},{5,21},{6,22},{7,23},{8,24},{9,... | collective-permute-start | bytes 786440 | tf_op jit(solution)/shard_map/ppermute | solution.py:215
  273.3 8.3 %collective-permute-start.13 = (f32[256,256]{1,0:T(8,128)S(1)}, f32[256,256]{1,0:T(8,128)S(1)}, u32[]{:S(2)}, u32[]{:S(2)}) collective-permute-start(f32[256,256]{1,0:T(8,128)S(1)} %add.57), channel_id=1, source_target_pairs={{0,32},{1,33},{2,34},{3,35},{4,36},{5,37},{6,38},{7,39},{8,40},{9,... | collective-permute-start | bytes 786440 | tf_op jit(solution)/shard_map/ppermute | solution.py:215
  281.7 8.0 %collective-permute-start.14 = (f32[256,256]{1,0:T(8,128)S(1)}, f32[256,256]{1,0:T(8,128)S(1)}, u32[]{:S(2)}, u32[]{:S(2)}) collective-permute-start(f32[256,256]{1,0:T(8,128)S(1)} %add.58), channel_id=1, source_target_pairs={{0,64},{1,65},{2,66},{3,67},{4,68},{5,69},{6,70},{7,71},{8,72},{9,... | collective-permute-start | bytes 786440 | tf_op jit(solution)/shard_map/ppermute | solution.py:215

commit v8 on v7

--- a/solution.py
+++ b/solution.py
@@ -12,7 +12,7 @@
 
 
 VMEM_LIMIT = 60 * 1024 * 1024
-GROUP = 4
+GROUP = 8
 
 
 def field_kernel(combine, older, apply, build, alpha, *refs):

time: 316 us -> 308 us (0.975)
  Pallas kernels: 136 us -> 129 us
    pallas_call x5, Pallas kernels: 136 us -> 129 us  [field_step(): pl.pallas_call(functools.partial(field_kernel, combine, has_older, apply,...]
where the time goes in v8:
time: 308 us
  Pallas kernels  129 us (42%)
  waiting for transfers between devices  83.7 us (27%)
  starting transfers between devices  43 us (14%)
  local copies, waits for them, and re-layouts  23.1 us (8%)
  blocking collectives  17.2 us (6%)
  matrix products  6.39 us (2%)
  other arithmetic  3.97 us (1%)
    pallas_call x5, Pallas kernels, field_step(): pl.pallas_call(functools.partial(field_kernel, combine, has_older, apply,...  129 us
    ppermute x7, waiting for transfers between devices, doubling_sum(): total = total + lax.ppermute(total, ('dom', 'band'), pairs)  44.6 us
    ppermute x4, starting transfers between devices, exchange(): from_left = lax.ppermute(right_values, 'dom', up)  19.2 us
    all_to_all x1, blocking collectives, body(): lax.all_to_all(rotated, 'band', split_axis=1, concat_axis=0, tiled=True)  17.2 us
    ppermute x4, waiting for transfers between devices, exchange(): from_left = lax.ppermute(right_values, 'dom', up)  14.2 us
    ppermute x4, waiting for transfers between devices, exchange(): from_right = lax.ppermute(left_values, 'dom', down)  13.6 us
    all_to_all x1, waiting for transfers between devices, body(): lax.all_to_all(current, 'band', split_axis=0, concat_axis=1, tiled=True)  11.3 us
    ppermute x4, starting transfers between devices, exchange(): from_right = lax.ppermute(left_values, 'dom', down)  9.58 us
  transfers between devices with their start and end apart: 16, of which 16 were waited for; matrix products, arithmetic and copies ran while one was open for 3% of the time, Pallas kernels for 0%

profile of v8, /device:TPU:6, one launch (start us, length us, event | category | flops | bytes accessed | tf_op | source)
XLA Modules:
  0.0 307.6 jit_solution(4804934071818395362)
XLA Ops:
  4.7 4.2 %copy.10 = bf16[64,12288]{0,1:T(8,128)(2,1)} copy(bf16[64,12288]{1,0:T(8,128)(2,1)} %param.7) | data formatting | bytes 3145728 | tf_op args[0]
  9.9 38.7 %shard_map.73 = (f32[12288,64]{1,0:T(8,128)}, f32[1024,64]{1,0:T(8,128)}, f32[1024,64]{1,0:T(8,128)}, bf16[32,512,512]{2,1,0:T(8,128)(2,1)}, f32[32,1,512]{2,1,0:T(1,128)}) custom-call(s32[2048]{0:T(1024)} %pad_add_fusion.refs_0_, f32[32]{0:T(128)} %compare_select_fusion.1.refs_1_, bf16[12288,64]{1,0:T(8,128)(2,1)} %bitcast.55, ...), custom_call_target="tpu_custom_call" | custom-call | flops 18253611008 | bytes 26214400 | tf_op jit(solution)/shard_map/pallas_call | solution.py:156
  50.6 3.6 %collective-permute-start.1 = (f32[1024,64]{1,0:T(8,128)}, f32[1024,64]{1,0:T(8,128)S(1)}, u32[]{:S(2)}, u32[]{:S(2)}) collective-permute-start(f32[1024,64]{1,0:T(8,128)} %get-tuple-element.23), channel_id=1, source_target_pairs={{4,0},{8,4},{12,8},{16,12},{20,16},{24,20},{28,24},{32,28},{36,32}... | collective-permute-start | bytes 786440 | tf_op jit(solution)/shard_map/ppermute | solution.py:252
  54.2 5.1 %collective-permute-done.refs_3_ = f32[1024,64]{1,0:T(8,128)S(1)} collective-permute-done((f32[1024,64]{1,0:T(8,128)}, f32[1024,64]{1,0:T(8,128)S(1)}, u32[]{:S(2)}, u32[]{:S(2)}) %collective-permute-start) | collective-permute-done | bytes 262176 | tf_op jit(solution)/shard_map/ppermute | solution.py:251
  62.0 24.7 %shard_map.74 = (bf16[12288,64]{1,0:T(8,128)(2,1)}, f32[12288,64]{1,0:T(8,128)}, f32[1024,64]{1,0:T(8,128)}, f32[1024,64]{1,0:T(8,128)}) custom-call(s32[2048]{0:T(1024)} %pad_add_fusion.refs_0_, f32[32]{0:T(128)} %compare_select_fusion.1.refs_1_, f32[12288,64]{1,0:T(8,128)} %get-tuple-element.21.refs_2_, f32[1024,64]{1,0:T(8,128)} %copy-done.2, ...), custom_call_target="tpu_custom_call" | custom-call | flops 1073741824 | bytes 26214400 | tf_op jit(solution)/shard_map/pallas_call | solution.py:156
  86.7 5.7 %collective-permute-start.2 = (f32[1024,64]{1,0:T(8,128)}, f32[1024,64]{1,0:T(8,128)S(1)}, u32[]{:S(2)}, u32[]{:S(2)}) collective-permute-start(f32[1024,64]{1,0:T(8,128)} %get-tuple-element.27), channel_id=1, source_target_pairs={{0,4},{4,8},{8,12},{12,16},{16,20},{20,24},{24,28},{28,32},{32,36}... | collective-permute-start | bytes 786440 | tf_op jit(solution)/shard_map/ppermute | solution.py:251
  92.3 2.1 collective-permute-start.3
  94.4 3.0 collective-permute-done.2.refs_3_
  97.4 3.8 %collective-permute-done.3.refs_4_ = f32[1024,64]{1,0:T(8,128)S(1)} collective-permute-done((f32[1024,64]{1,0:T(8,128)}, f32[1024,64]{1,0:T(8,128)S(1)}, u32[]{:S(2)}, u32[]{:S(2)}) %collective-permute-start.3) | collective-permute-done | bytes 262176 | tf_op jit(solution)/shard_map/ppermute | solution.py:252
  102.0 26.4 %shard_map.75 = (bf16[12288,64]{1,0:T(8,128)(2,1)}, f32[12288,64]{1,0:T(8,128)}, f32[1024,64]{1,0:T(8,128)}, f32[1024,64]{1,0:T(8,128)}) custom-call(s32[2048]{0:T(1024)} %pad_add_fusion.refs_0_, f32[32]{0:T(128)} %compare_select_fusion.1.refs_1_, f32[12288,64]{1,0:T(8,128)} %get-tuple-element.26.refs_2_, f32[1024,64]{1,0:T(8,128)} %copy-done.3, ...), custom_call_target="tpu_custom_call" | custom-call | flops 1073741824 | bytes 26214400 | tf_op jit(solution)/shard_map/pallas_call | solution.py:156
  128.4 5.8 %collective-permute-start.4 = (f32[1024,64]{1,0:T(8,128)}, f32[1024,64]{1,0:T(8,128)S(1)}, u32[]{:S(2)}, u32[]{:S(2)}) collective-permute-start(f32[1024,64]{1,0:T(8,128)} %get-tuple-element.30), channel_id=1, source_target_pairs={{0,4},{4,8},{8,12},{12,16},{16,20},{20,24},{24,28},{28,32},{32,36}... | collective-permute-start | bytes 786440 | tf_op jit(solution)/shard_map/ppermute | solution.py:251
  134.2 1.9 collective-permute-start.5
  136.2 3.0 collective-permute-done.4.refs_3_
  139.2 4.0 %collective-permute-done.5.refs_4_ = f32[1024,64]{1,0:T(8,128)S(1)} collective-permute-done((f32[1024,64]{1,0:T(8,128)}, f32[1024,64]{1,0:T(8,128)S(1)}, u32[]{:S(2)}, u32[]{:S(2)}) %collective-permute-start.5) | collective-permute-done | bytes 262176 | tf_op jit(solution)/shard_map/ppermute | solution.py:252
  143.9 26.3 %shard_map.76 = (bf16[12288,64]{1,0:T(8,128)(2,1)}, f32[12288,64]{1,0:T(8,128)}, f32[1024,64]{1,0:T(8,128)}, f32[1024,64]{1,0:T(8,128)}) custom-call(s32[2048]{0:T(1024)} %pad_add_fusion.refs_0_, f32[32]{0:T(128)} %compare_select_fusion.1.refs_1_, f32[12288,64]{1,0:T(8,128)} %get-tuple-element.29.refs_2_, f32[1024,64]{1,0:T(8,128)} %copy-done, ...), custom_call_target="tpu_custom_call" | custom-call | flops 1073741824 | bytes 26214400 | tf_op jit(solution)/shard_map/pallas_call | solution.py:156
  170.2 5.8 %collective-permute-start.6 = (f32[1024,64]{1,0:T(8,128)}, f32[1024,64]{1,0:T(8,128)S(1)}, u32[]{:S(2)}, u32[]{:S(2)}) collective-permute-start(f32[1024,64]{1,0:T(8,128)} %get-tuple-element.34), channel_id=1, source_target_pairs={{0,4},{4,8},{8,12},{12,16},{16,20},{20,24},{24,28},{28,32},{32,36}... | collective-permute-start | bytes 786440 | tf_op jit(solution)/shard_map/ppermute | solution.py:251
  178.0 3.0 collective-permute-done.6.refs_2_
  181.0 4.0 %collective-permute-done.7.refs_3_ = f32[1024,64]{1,0:T(8,128)S(1)} collective-permute-done((f32[1024,64]{1,0:T(8,128)}, f32[1024,64]{1,0:T(8,128)S(1)}, u32[]{:S(2)}, u32[]{:S(2)}) %collective-permute-start.7) | collective-permute-done | bytes 262176 | tf_op jit(solution)/shard_map/ppermute | solution.py:252
  185.8 12.5 %shard_map.77 = bf16[12288,64]{1,0:T(8,128)(2,1)} custom-call(s32[2048]{0:T(1024)} %pad_add_fusion.refs_0_, f32[12288,64]{1,0:T(8,128)} %get-tuple-element.33.refs_1_, f32[1024,64]{1,0:T(8,128)} %copy-done.4, f32[1024,64]{1,0:T(8,128)} %copy-done.7, bf16[12288,64]{1,0:T(8,128)(2,1)} %get-tuple-element.36.refs_4_), custom_call_target="tpu_custom_call" | custom-call | bytes 9437184 | tf_op jit(solution)/shard_map/pallas_call | solution.py:156
  198.3 4.3 %copy.11 = bf16[4,3072,64]{1,2,0:T(8,128)(2,1)} copy(bf16[4,3072,64]{2,1,0:T(8,128)(2,1)} %bitcast.54) | data formatting | bytes 3145728 | tf_op jit(solution)/shard_map/all_to_all | solution.py:271
  202.5 5.3 %all-to-all-start = ((bf16[4,3072,64]{1,2,0:T(8,128)(2,1)}), bf16[4,3072,64]{1,2,0:T(8,128)(2,1)S(1)}, u32[]{:S(2)}, u32[]{:S(2)}) async-start(bf16[4,3072,64]{1,2,0:T(8,128)(2,1)} %copy.11), calls=%async_computation | async-start | bytes 3145728 | tf_op jit(solution)/shard_map/all_to_all | solution.py:271
  207.9 8.1 %scatter_custom_fusion = f32[12288]{0:T(1024)S(1)} fusion(s32[2048]{0:T(1024)S(1)} %bitcast.62, f32[2048]{0:T(1024)S(1)} %add_divide_fusion, f32[]{:T(128)} %constant.17.clone.1), kind=kCustom, calls=%fused_computation.23 | custom fusion | bytes 49156 | tf_op jit(solution)/shard_map/scatter | solution.py:237
  216.0 11.3 %all-to-all-done = bf16[4,3072,64]{1,2,0:T(8,128)(2,1)S(1)} async-done(((bf16[4,3072,64]{1,2,0:T(8,128)(2,1)}), bf16[4,3072,64]{1,2,0:T(8,128)(2,1)S(1)}, u32[]{:S(2)}, u32[]{:S(2)}) %all-to-all-start) | async-done | bytes 1572896 | tf_op jit(solution)/shard_map/all_to_all | solution.py:271
  228.0 2.6 collective-permute-start.8
  232.4 8.0 %collective-permute-done.9 = f32[256,256]{1,0:T(8,128)S(1)} collective-permute-done((f32[256,256]{1,0:T(8,128)S(1)}, f32[256,256]{1,0:T(8,128)S(1)}, u32[]{:S(2)}, u32[]{:S(2)}) %collective-permute-start.9) | collective-permute-done | bytes 262176 | tf_op jit(solution)/shard_map/ppermute | solution.py:215
  241.5 8.3 %collective-permute-done.10 = f32[256,256]{1,0:T(8,128)S(1)} collective-permute-done((f32[256,256]{1,0:T(8,128)S(1)}, f32[256,256]{1,0:T(8,128)S(1)}, u32[]{:S(2)}, u32[]{:S(2)}) %collective-permute-start.10) | collective-permute-done | bytes 262176 | tf_op jit(solution)/shard_map/ppermute | solution.py:215
  249.9 7.5 %collective-permute-done.11 = f32[256,256]{1,0:T(8,128)S(1)} collective-permute-done((f32[256,256]{1,0:T(8,128)S(1)}, f32[256,256]{1,0:T(8,128)S(1)}, u32[]{:S(2)}, u32[]{:S(2)}) %collective-permute-start.11) | collective-permute-done | bytes 262176 | tf_op jit(solution)/shard_map/ppermute | solution.py:215
  257.6 7.9 %collective-permute-done.12 = f32[256,256]{1,0:T(8,128)S(1)} collective-permute-done((f32[256,256]{1,0:T(8,128)S(1)}, f32[256,256]{1,0:T(8,128)S(1)}, u32[]{:S(2)}, u32[]{:S(2)}) %collective-permute-start.12) | collective-permute-done | bytes 262176 | tf_op jit(solution)/shard_map/ppermute | solution.py:215
  267.1 6.5 %collective-permute-done.13 = f32[256,256]{1,0:T(8,128)S(1)} collective-permute-done((f32[256,256]{1,0:T(8,128)S(1)}, f32[256,256]{1,0:T(8,128)S(1)}, u32[]{:S(2)}, u32[]{:S(2)}) %collective-permute-start.13) | collective-permute-done | bytes 262176 | tf_op jit(solution)/shard_map/ppermute | solution.py:215
  273.7 3.0 collective-permute-start.14
  276.6 5.2 %collective-permute-done.14 = f32[256,256]{1,0:T(8,128)S(1)} collective-permute-done((f32[256,256]{1,0:T(8,128)S(1)}, f32[256,256]{1,0:T(8,128)S(1)}, u32[]{:S(2)}, u32[]{:S(2)}) %collective-permute-start.14) | collective-permute-done | bytes 262176 | tf_op jit(solution)/shard_map/ppermute | solution.py:215
  289.1 17.2 %all_to_all.38 = bf16[3072,4,64]{0,2,1:T(8,128)(2,1)S(1)} all-to-all(bf16[3072,4,64]{0,2,1:T(8,128)(2,1)S(1)} %bitcast.57), channel_id=1, replica_groups=mesh['dom'=32,'band'=4] {'band'}, dimensions={1} | all-to-all | bytes 3145728 | tf_op jit(solution)/shard_map/all_to_all | solution.py:285
  (65 shorter events, 27.2 us)
Async XLA Ops:
  4.6 4.2 %copy-start.8 = (f32[32]{0:T(128)S(1)}, f32[32]{0:T(128)}, u32[]{:S(2)}) copy-start(f32[32]{0:T(128)} %param.9) | copy-start | bytes 388
  48.6 10.7 %collective-permute-start = (f32[1024,64]{1,0:T(8,128)}, f32[1024,64]{1,0:T(8,128)S(1)}, u32[]{:S(2)}, u32[]{:S(2)}) collective-permute-start(f32[1024,64]{1,0:T(8,128)} %get-tuple-element.22), channel_id=1, source_target_pairs={{0,4},{4,8},{8,12},{12,16},{16,20},{20,24},{24,28},{28,32},{32,36}... | collective-permute-start | bytes 786440 | tf_op jit(solution)/shard_map/ppermute | solution.py:251
  50.6 10.6 %collective-permute-start.1 = (f32[1024,64]{1,0:T(8,128)}, f32[1024,64]{1,0:T(8,128)S(1)}, u32[]{:S(2)}, u32[]{:S(2)}) collective-permute-start(f32[1024,64]{1,0:T(8,128)} %get-tuple-element.23), channel_id=1, source_target_pairs={{4,0},{8,4},{12,8},{16,12},{20,16},{24,20},{28,24},{32,28},{36,32}... | collective-permute-start | bytes 786440 | tf_op jit(solution)/shard_map/ppermute | solution.py:252
  59.3 1.9 copy-start.2
  61.2 0.8 copy-start.5
  86.7 10.8 %collective-permute-start.2 = (f32[1024,64]{1,0:T(8,128)}, f32[1024,64]{1,0:T(8,128)S(1)}, u32[]{:S(2)}, u32[]{:S(2)}) collective-permute-start(f32[1024,64]{1,0:T(8,128)} %get-tuple-element.27), channel_id=1, source_target_pairs={{0,4},{4,8},{8,12},{12,16},{16,20},{20,24},{24,28},{28,32},{32,36}... | collective-permute-start | bytes 786440 | tf_op jit(solution)/shard_map/ppermute | solution.py:251
  92.3 8.9 %collective-permute-start.3 = (f32[1024,64]{1,0:T(8,128)}, f32[1024,64]{1,0:T(8,128)S(1)}, u32[]{:S(2)}, u32[]{:S(2)}) collective-permute-start(f32[1024,64]{1,0:T(8,128)} %get-tuple-element.28), channel_id=1, source_target_pairs={{4,0},{8,4},{12,8},{16,12},{20,16},{24,20},{28,24},{32,28},{36,32}... | collective-permute-start | bytes 786440 | tf_op jit(solution)/shard_map/ppermute | solution.py:252
  97.4 3.8 %copy-start.3 = (f32[1024,64]{1,0:T(8,128)}, f32[1024,64]{1,0:T(8,128)S(1)}, u32[]{:S(2)}) copy-start(f32[1024,64]{1,0:T(8,128)S(1)} %collective-permute-done.2.refs_3_) | copy-start | bytes 786436
  101.3 0.8 copy-start.6
  128.4 10.8 %collective-permute-start.4 = (f32[1024,64]{1,0:T(8,128)}, f32[1024,64]{1,0:T(8,128)S(1)}, u32[]{:S(2)}, u32[]{:S(2)}) collective-permute-start(f32[1024,64]{1,0:T(8,128)} %get-tuple-element.30), channel_id=1, source_target_pairs={{0,4},{4,8},{8,12},{12,16},{16,20},{20,24},{24,28},{28,32},{32,36}... | collective-permute-start | bytes 786440 | tf_op jit(solution)/shard_map/ppermute | solution.py:251
  134.2 8.9 %collective-permute-start.5 = (f32[1024,64]{1,0:T(8,128)}, f32[1024,64]{1,0:T(8,128)S(1)}, u32[]{:S(2)}, u32[]{:S(2)}) collective-permute-start(f32[1024,64]{1,0:T(8,128)} %get-tuple-element.31), channel_id=1, source_target_pairs={{4,0},{8,4},{12,8},{16,12},{20,16},{24,20},{28,24},{32,28},{36,32}... | collective-permute-start | bytes 786440 | tf_op jit(solution)/shard_map/ppermute | solution.py:252
  139.2 4.0 %copy-start = (f32[1024,64]{1,0:T(8,128)}, f32[1024,64]{1,0:T(8,128)S(1)}, u32[]{:S(2)}) copy-start(f32[1024,64]{1,0:T(8,128)S(1)} %collective-permute-done.4.refs_3_) | copy-start | bytes 786436
  143.2 0.8 copy-start.1
  170.2 10.8 %collective-permute-start.6 = (f32[1024,64]{1,0:T(8,128)}, f32[1024,64]{1,0:T(8,128)S(1)}, u32[]{:S(2)}, u32[]{:S(2)}) collective-permute-start(f32[1024,64]{1,0:T(8,128)} %get-tuple-element.34), channel_id=1, source_target_pairs={{0,4},{4,8},{8,12},{12,16},{16,20},{20,24},{24,28},{28,32},{32,36}... | collective-permute-start | bytes 786440 | tf_op jit(solution)/shard_map/ppermute | solution.py:251
  176.0 8.9 %collective-permute-start.7 = (f32[1024,64]{1,0:T(8,128)}, f32[1024,64]{1,0:T(8,128)S(1)}, u32[]{:S(2)}, u32[]{:S(2)}) collective-permute-start(f32[1024,64]{1,0:T(8,128)} %get-tuple-element.35), channel_id=1, source_target_pairs={{4,0},{8,4},{12,8},{16,12},{20,16},{24,20},{28,24},{32,28},{36,32}... | collective-permute-start | bytes 786440 | tf_op jit(solution)/shard_map/ppermute | solution.py:252
  181.0 4.0 %copy-start.4 = (f32[1024,64]{1,0:T(8,128)}, f32[1024,64]{1,0:T(8,128)S(1)}, u32[]{:S(2)}) copy-start(f32[1024,64]{1,0:T(8,128)S(1)} %collective-permute-done.6.refs_2_) | copy-start | bytes 786436
  185.0 0.8 copy-start.7
  202.5 24.8 %all-to-all-start = ((bf16[4,3072,64]{1,2,0:T(8,128)(2,1)}), bf16[4,3072,64]{1,2,0:T(8,128)(2,1)S(1)}, u32[]{:S(2)}, u32[]{:S(2)}) async-start(bf16[4,3072,64]{1,2,0:T(8,128)(2,1)} %copy.11), calls=%async_computation | async-start | bytes 3145728 | tf_op jit(solution)/shard_map/all_to_all | solution.py:271
  228.0 3.7 %collective-permute-start.8 = (f32[256,256]{1,0:T(8,128)S(1)}, f32[256,256]{1,0:T(8,128)S(1)}, u32[]{:S(2)}, u32[]{:S(2)}) collective-permute-start(f32[256,256]{1,0:T(8,128)S(1)} %fusion.9), channel_id=1, source_target_pairs={{0,4},{1,5},{2,6},{3,7},{4,0},{5,1},{6,2},{7,3},{8,12},{9,13},{10,... | collective-permute-start | bytes 786440 | tf_op jit(solution)/shard_map/ppermute | solution.py:215
  231.8 8.7 %collective-permute-start.9 = (f32[256,256]{1,0:T(8,128)S(1)}, f32[256,256]{1,0:T(8,128)S(1)}, u32[]{:S(2)}, u32[]{:S(2)}) collective-permute-start(f32[256,256]{1,0:T(8,128)S(1)} %add.53), channel_id=1, source_target_pairs={{0,1},{1,0},{2,3},{3,2},{4,5},{5,4},{6,7},{7,6},{8,9},{9,8},{10,11... | collective-permute-start | bytes 786440 | tf_op jit(solution)/shard_map/ppermute | solution.py:215
  240.5 9.3 %collective-permute-start.10 = (f32[256,256]{1,0:T(8,128)S(1)}, f32[256,256]{1,0:T(8,128)S(1)}, u32[]{:S(2)}, u32[]{:S(2)}) collective-permute-start(f32[256,256]{1,0:T(8,128)S(1)} %add.54), channel_id=1, source_target_pairs={{0,2},{1,3},{2,0},{3,1},{4,6},{5,7},{6,4},{7,5},{8,10},{9,11},{10,... | collective-permute-start | bytes 786440 | tf_op jit(solution)/shard_map/ppermute | solution.py:215
  249.9 7.6 %collective-permute-start.11 = (f32[256,256]{1,0:T(8,128)S(1)}, f32[256,256]{1,0:T(8,128)S(1)}, u32[]{:S(2)}, u32[]{:S(2)}) collective-permute-start(f32[256,256]{1,0:T(8,128)S(1)} %add.55), channel_id=1, source_target_pairs={{0,8},{1,9},{2,10},{3,11},{4,12},{5,13},{6,14},{7,15},{8,0},{9,1},... | collective-permute-start | bytes 786440 | tf_op jit(solution)/shard_map/ppermute | solution.py:215
  257.5 8.0 %collective-permute-start.12 = (f32[256,256]{1,0:T(8,128)S(1)}, f32[256,256]{1,0:T(8,128)S(1)}, u32[]{:S(2)}, u32[]{:S(2)}) collective-permute-start(f32[256,256]{1,0:T(8,128)S(1)} %add.56), channel_id=1, source_target_pairs={{0,16},{1,17},{2,18},{3,19},{4,20},{5,21},{6,22},{7,23},{8,24},{9,... | collective-permute-start | bytes 786440 | tf_op jit(solution)/shard_map/ppermute | solution.py:215
  265.5 8.1 %collective-permute-start.13 = (f32[256,256]{1,0:T(8,128)S(1)}, f32[256,256]{1,0:T(8,128)S(1)}, u32[]{:S(2)}, u32[]{:S(2)}) collective-permute-start(f32[256,256]{1,0:T(8,128)S(1)} %add.57), channel_id=1, source_target_pairs={{0,32},{1,33},{2,34},{3,35},{4,36},{5,37},{6,38},{7,39},{8,40},{9,... | collective-permute-start | bytes 786440 | tf_op jit(solution)/shard_map/ppermute | solution.py:215
  273.7 8.2 %collective-permute-start.14 = (f32[256,256]{1,0:T(8,128)S(1)}, f32[256,256]{1,0:T(8,128)S(1)}, u32[]{:S(2)}, u32[]{:S(2)}) collective-permute-start(f32[256,256]{1,0:T(8,128)S(1)} %add.58), channel_id=1, source_target_pairs={{0,64},{1,65},{2,66},{3,67},{4,68},{5,69},{6,70},{7,71},{8,72},{9,... | collective-permute-start | bytes 786440 | tf_op jit(solution)/shard_map/ppermute | solution.py:215

commit v9 on v8

--- a/solution.py
+++ b/solution.py
@@ -12,10 +12,11 @@
 
 
 VMEM_LIMIT = 60 * 1024 * 1024
-GROUP = 8
-
-
-def field_kernel(combine, older, apply, build, alpha, *refs):
+BUILD_GROUP = 8
+GROUP = 16
+
+
+def field_kernel(combine, older, apply, build, alpha, group, *refs):
     refs = list(refs)
     faces = refs.pop(0)
     if apply:
@@ -78,8 +79,8 @@
         def _():
             local_out[...] = jnp.zeros_like(local_out)
 
-        for k in range(GROUP):
-            index = cell * GROUP + k
+        for k in range(group):
+            index = cell * group + k
             start = pl.multiple_of(index * body_rows, quarter)
             tail = pl.multiple_of(lax.rem((index + 1) * body_rows, node_total), quarter)
             main_rows = vector[pl.ds(start, body_rows), :]
@@ -132,8 +133,9 @@
             args.append(older); specs.append(whole)
     else:
         args.append(vector); specs.append(whole)
-    cell_block = pl.BlockSpec((GROUP, width, width), lambda c: (c, 0, 0))
-    row_block = pl.BlockSpec((GROUP, 1, width), lambda c: (c, 0, 0))
+    group = BUILD_GROUP if build else GROUP
+    cell_block = pl.BlockSpec((group, width, width), lambda c: (c, 0, 0))
+    row_block = pl.BlockSpec((group, 1, width), lambda c: (c, 0, 0))
     if apply:
         args += [window_ops, window_pot]
         specs += [row_block if build else cell_block, row_block]
@@ -154,8 +156,8 @@
     scratch = [pltpu.VMEM((node_total, cols), jnp.float32)] if combine else []
     flops = (2 * cells * width * width * cols if apply else 0) + (4 * cells * width ** 3 if build else 0)
     result = pl.pallas_call(
-        functools.partial(field_kernel, combine, has_older, apply, build, alpha),
-        grid=(cells // GROUP if apply else 1,),
+        functools.partial(field_kernel, combine, has_older, apply, build, alpha, group),
+        grid=(cells // group if apply else 1,),
         in_specs=specs,
         out_specs=out_specs,
         out_shape=out_shape,

time: 308 us -> 307 us (level)
  no operation moved by 1% of the time
where the time goes in v9:
time: 307 us
  Pallas kernels  127 us (41%)
  waiting for transfers between devices  83.9 us (27%)
  starting transfers between devices  43.1 us (14%)
  local copies, waits for them, and re-layouts  23.1 us (8%)
  blocking collectives  17.2 us (6%)
  matrix products  6.39 us (2%)
  other arithmetic  3.97 us (1%)
    pallas_call x5, Pallas kernels, field_step(): pl.pallas_call(functools.partial(field_kernel, combine, has_older, apply,...  127 us
    ppermute x7, waiting for transfers between devices, doubling_sum(): total = total + lax.ppermute(total, ('dom', 'band'), pairs)  44.8 us
    ppermute x4, starting transfers between devices, exchange(): from_left = lax.ppermute(right_values, 'dom', up)  19.2 us
    all_to_all x1, blocking collectives, body(): lax.all_to_all(rotated, 'band', split_axis=1, concat_axis=0, tiled=True)  17.2 us
    ppermute x4, waiting for transfers between devices, exchange(): from_left = lax.ppermute(right_values, 'dom', up)  14.2 us
    ppermute x4, waiting for transfers between devices, exchange(): from_right = lax.ppermute(left_values, 'dom', down)  13.6 us
    all_to_all x1, waiting for transfers between devices, body(): lax.all_to_all(current, 'band', split_axis=0, concat_axis=1, tiled=True)  11.3 us
    ppermute x4, starting transfers between devices, exchange(): from_right = lax.ppermute(left_values, 'dom', down)  9.58 us
  transfers between devices with their start and end apart: 16, of which 16 were waited for; matrix products, arithmetic and copies ran while one was open for 3% of the time, Pallas kernels for 0%

profile of v9, /device:TPU:6, one launch (start us, length us, event | category | flops | bytes accessed | tf_op | source)
XLA Modules:
  0.0 306.5 jit_solution(15929809655596453101)
XLA Ops:
  4.7 4.2 %copy.10 = bf16[64,12288]{0,1:T(8,128)(2,1)} copy(bf16[64,12288]{1,0:T(8,128)(2,1)} %param.7) | data formatting | bytes 3145728 | tf_op args[0]
  9.9 38.7 %shard_map.73 = (f32[12288,64]{1,0:T(8,128)}, f32[1024,64]{1,0:T(8,128)}, f32[1024,64]{1,0:T(8,128)}, bf16[32,512,512]{2,1,0:T(8,128)(2,1)}, f32[32,1,512]{2,1,0:T(1,128)}) custom-call(s32[2048]{0:T(1024)} %pad_add_fusion.refs_0_, f32[32]{0:T(128)} %compare_select_fusion.1.refs_1_, bf16[12288,64]{1,0:T(8,128)(2,1)} %bitcast.55, ...), custom_call_target="tpu_custom_call" | custom-call | flops 18253611008 | bytes 26214400 | tf_op jit(solution)/shard_map/pallas_call | solution.py:158
  50.6 3.6 %collective-permute-start.1 = (f32[1024,64]{1,0:T(8,128)}, f32[1024,64]{1,0:T(8,128)S(1)}, u32[]{:S(2)}, u32[]{:S(2)}) collective-permute-start(f32[1024,64]{1,0:T(8,128)} %get-tuple-element.23), channel_id=1, source_target_pairs={{4,0},{8,4},{12,8},{16,12},{20,16},{24,20},{28,24},{32,28},{36,32}... | collective-permute-start | bytes 786440 | tf_op jit(solution)/shard_map/ppermute | solution.py:254
  54.2 5.1 %collective-permute-done.refs_3_ = f32[1024,64]{1,0:T(8,128)S(1)} collective-permute-done((f32[1024,64]{1,0:T(8,128)}, f32[1024,64]{1,0:T(8,128)S(1)}, u32[]{:S(2)}, u32[]{:S(2)}) %collective-permute-start) | collective-permute-done | bytes 262176 | tf_op jit(solution)/shard_map/ppermute | solution.py:253
  62.0 24.2 %shard_map.74 = (bf16[12288,64]{1,0:T(8,128)(2,1)}, f32[12288,64]{1,0:T(8,128)}, f32[1024,64]{1,0:T(8,128)}, f32[1024,64]{1,0:T(8,128)}) custom-call(s32[2048]{0:T(1024)} %pad_add_fusion.refs_0_, f32[32]{0:T(128)} %compare_select_fusion.1.refs_1_, f32[12288,64]{1,0:T(8,128)} %get-tuple-element.21.refs_2_, f32[1024,64]{1,0:T(8,128)} %copy-done.2, ...), custom_call_target="tpu_custom_call" | custom-call | flops 1073741824 | bytes 26214400 | tf_op jit(solution)/shard_map/pallas_call | solution.py:158
  86.2 5.7 %collective-permute-start.2 = (f32[1024,64]{1,0:T(8,128)}, f32[1024,64]{1,0:T(8,128)S(1)}, u32[]{:S(2)}, u32[]{:S(2)}) collective-permute-start(f32[1024,64]{1,0:T(8,128)} %get-tuple-element.27), channel_id=1, source_target_pairs={{0,4},{4,8},{8,12},{12,16},{16,20},{20,24},{24,28},{28,32},{32,36}... | collective-permute-start | bytes 786440 | tf_op jit(solution)/shard_map/ppermute | solution.py:253
  91.9 2.1 collective-permute-start.3
  94.0 3.0 collective-permute-done.2.refs_3_
  97.0 3.8 %collective-permute-done.3.refs_4_ = f32[1024,64]{1,0:T(8,128)S(1)} collective-permute-done((f32[1024,64]{1,0:T(8,128)}, f32[1024,64]{1,0:T(8,128)S(1)}, u32[]{:S(2)}, u32[]{:S(2)}) %collective-permute-start.3) | collective-permute-done | bytes 262176 | tf_op jit(solution)/shard_map/ppermute | solution.py:254
  101.6 25.9 %shard_map.75 = (bf16[12288,64]{1,0:T(8,128)(2,1)}, f32[12288,64]{1,0:T(8,128)}, f32[1024,64]{1,0:T(8,128)}, f32[1024,64]{1,0:T(8,128)}) custom-call(s32[2048]{0:T(1024)} %pad_add_fusion.refs_0_, f32[32]{0:T(128)} %compare_select_fusion.1.refs_1_, f32[12288,64]{1,0:T(8,128)} %get-tuple-element.26.refs_2_, f32[1024,64]{1,0:T(8,128)} %copy-done.3, ...), custom_call_target="tpu_custom_call" | custom-call | flops 1073741824 | bytes 26214400 | tf_op jit(solution)/shard_map/pallas_call | solution.py:158
  127.6 5.8 %collective-permute-start.4 = (f32[1024,64]{1,0:T(8,128)}, f32[1024,64]{1,0:T(8,128)S(1)}, u32[]{:S(2)}, u32[]{:S(2)}) collective-permute-start(f32[1024,64]{1,0:T(8,128)} %get-tuple-element.30), channel_id=1, source_target_pairs={{0,4},{4,8},{8,12},{12,16},{16,20},{20,24},{24,28},{28,32},{32,36}... | collective-permute-start | bytes 786440 | tf_op jit(solution)/shard_map/ppermute | solution.py:253
  133.4 1.9 collective-permute-start.5
  135.3 3.0 collective-permute-done.4.refs_3_
  138.3 4.0 %collective-permute-done.5.refs_4_ = f32[1024,64]{1,0:T(8,128)S(1)} collective-permute-done((f32[1024,64]{1,0:T(8,128)}, f32[1024,64]{1,0:T(8,128)S(1)}, u32[]{:S(2)}, u32[]{:S(2)}) %collective-permute-start.5) | collective-permute-done | bytes 262176 | tf_op jit(solution)/shard_map/ppermute | solution.py:254
  143.1 25.9 %shard_map.76 = (bf16[12288,64]{1,0:T(8,128)(2,1)}, f32[12288,64]{1,0:T(8,128)}, f32[1024,64]{1,0:T(8,128)}, f32[1024,64]{1,0:T(8,128)}) custom-call(s32[2048]{0:T(1024)} %pad_add_fusion.refs_0_, f32[32]{0:T(128)} %compare_select_fusion.1.refs_1_, f32[12288,64]{1,0:T(8,128)} %get-tuple-element.29.refs_2_, f32[1024,64]{1,0:T(8,128)} %copy-done, ...), custom_call_target="tpu_custom_call" | custom-call | flops 1073741824 | bytes 26214400 | tf_op jit(solution)/shard_map/pallas_call | solution.py:158
  168.9 5.8 %collective-permute-start.6 = (f32[1024,64]{1,0:T(8,128)}, f32[1024,64]{1,0:T(8,128)S(1)}, u32[]{:S(2)}, u32[]{:S(2)}) collective-permute-start(f32[1024,64]{1,0:T(8,128)} %get-tuple-element.34), channel_id=1, source_target_pairs={{0,4},{4,8},{8,12},{12,16},{16,20},{20,24},{24,28},{28,32},{32,36}... | collective-permute-start | bytes 786440 | tf_op jit(solution)/shard_map/ppermute | solution.py:253
  176.7 3.0 collective-permute-done.6.refs_2_
  179.7 4.0 %collective-permute-done.7.refs_3_ = f32[1024,64]{1,0:T(8,128)S(1)} collective-permute-done((f32[1024,64]{1,0:T(8,128)}, f32[1024,64]{1,0:T(8,128)S(1)}, u32[]{:S(2)}, u32[]{:S(2)}) %collective-permute-start.7) | collective-permute-done | bytes 262176 | tf_op jit(solution)/shard_map/ppermute | solution.py:254
  184.5 12.5 %shard_map.77 = bf16[12288,64]{1,0:T(8,128)(2,1)} custom-call(s32[2048]{0:T(1024)} %pad_add_fusion.refs_0_, f32[12288,64]{1,0:T(8,128)} %get-tuple-element.33.refs_1_, f32[1024,64]{1,0:T(8,128)} %copy-done.4, f32[1024,64]{1,0:T(8,128)} %copy-done.7, bf16[12288,64]{1,0:T(8,128)(2,1)} %get-tuple-element.36.refs_4_), custom_call_target="tpu_custom_call" | custom-call | bytes 9437184 | tf_op jit(solution)/shard_map/pallas_call | solution.py:158
  197.0 4.3 %copy.11 = bf16[4,3072,64]{1,2,0:T(8,128)(2,1)} copy(bf16[4,3072,64]{2,1,0:T(8,128)(2,1)} %bitcast.54) | data formatting | bytes 3145728 | tf_op jit(solution)/shard_map/all_to_all | solution.py:273
  201.3 5.3 %all-to-all-start = ((bf16[4,3072,64]{1,2,0:T(8,128)(2,1)}), bf16[4,3072,64]{1,2,0:T(8,128)(2,1)S(1)}, u32[]{:S(2)}, u32[]{:S(2)}) async-start(bf16[4,3072,64]{1,2,0:T(8,128)(2,1)} %copy.11), calls=%async_computation | async-start | bytes 3145728 | tf_op jit(solution)/shard_map/all_to_all | solution.py:273
  206.6 8.1 %scatter_custom_fusion = f32[12288]{0:T(1024)S(1)} fusion(s32[2048]{0:T(1024)S(1)} %bitcast.62, f32[2048]{0:T(1024)S(1)} %add_divide_fusion, f32[]{:T(128)} %constant.17.clone.1), kind=kCustom, calls=%fused_computation.23 | custom fusion | bytes 49156 | tf_op jit(solution)/shard_map/scatter | solution.py:239
  214.7 11.3 %all-to-all-done = bf16[4,3072,64]{1,2,0:T(8,128)(2,1)S(1)} async-done(((bf16[4,3072,64]{1,2,0:T(8,128)(2,1)}), bf16[4,3072,64]{1,2,0:T(8,128)(2,1)S(1)}, u32[]{:S(2)}, u32[]{:S(2)}) %all-to-all-start) | async-done | bytes 1572896 | tf_op jit(solution)/shard_map/all_to_all | solution.py:273
  226.7 2.8 collective-permute-start.8
  231.4 8.0 %collective-permute-done.9 = f32[256,256]{1,0:T(8,128)S(1)} collective-permute-done((f32[256,256]{1,0:T(8,128)S(1)}, f32[256,256]{1,0:T(8,128)S(1)}, u32[]{:S(2)}, u32[]{:S(2)}) %collective-permute-start.9) | collective-permute-done | bytes 262176 | tf_op jit(solution)/shard_map/ppermute | solution.py:217
  240.4 8.3 %collective-permute-done.10 = f32[256,256]{1,0:T(8,128)S(1)} collective-permute-done((f32[256,256]{1,0:T(8,128)S(1)}, f32[256,256]{1,0:T(8,128)S(1)}, u32[]{:S(2)}, u32[]{:S(2)}) %collective-permute-start.10) | collective-permute-done | bytes 262176 | tf_op jit(solution)/shard_map/ppermute | solution.py:217
  248.9 7.5 %collective-permute-done.11 = f32[256,256]{1,0:T(8,128)S(1)} collective-permute-done((f32[256,256]{1,0:T(8,128)S(1)}, f32[256,256]{1,0:T(8,128)S(1)}, u32[]{:S(2)}, u32[]{:S(2)}) %collective-permute-start.11) | collective-permute-done | bytes 262176 | tf_op jit(solution)/shard_map/ppermute | solution.py:217
  256.5 7.9 %collective-permute-done.12 = f32[256,256]{1,0:T(8,128)S(1)} collective-permute-done((f32[256,256]{1,0:T(8,128)S(1)}, f32[256,256]{1,0:T(8,128)S(1)}, u32[]{:S(2)}, u32[]{:S(2)}) %collective-permute-start.12) | collective-permute-done | bytes 262176 | tf_op jit(solution)/shard_map/ppermute | solution.py:217
  266.1 6.7 %collective-permute-done.13 = f32[256,256]{1,0:T(8,128)S(1)} collective-permute-done((f32[256,256]{1,0:T(8,128)S(1)}, f32[256,256]{1,0:T(8,128)S(1)}, u32[]{:S(2)}, u32[]{:S(2)}) %collective-permute-start.13) | collective-permute-done | bytes 262176 | tf_op jit(solution)/shard_map/ppermute | solution.py:217
  272.8 2.8 collective-permute-start.14
  275.5 5.2 %collective-permute-done.14 = f32[256,256]{1,0:T(8,128)S(1)} collective-permute-done((f32[256,256]{1,0:T(8,128)S(1)}, f32[256,256]{1,0:T(8,128)S(1)}, u32[]{:S(2)}, u32[]{:S(2)}) %collective-permute-start.14) | collective-permute-done | bytes 262176 | tf_op jit(solution)/shard_map/ppermute | solution.py:217
  288.0 17.2 %all_to_all.38 = bf16[3072,4,64]{0,2,1:T(8,128)(2,1)S(1)} all-to-all(bf16[3072,4,64]{0,2,1:T(8,128)(2,1)S(1)} %bitcast.57), channel_id=1, replica_groups=mesh['dom'=32,'band'=4] {'band'}, dimensions={1} | all-to-all | bytes 3145728 | tf_op jit(solution)/shard_map/all_to_all | solution.py:287
  (65 shorter events, 27.2 us)
Async XLA Ops:
  4.6 4.2 %copy-start.8 = (f32[32]{0:T(128)S(1)}, f32[32]{0:T(128)}, u32[]{:S(2)}) copy-start(f32[32]{0:T(128)} %param.9) | copy-start | bytes 388
  48.6 10.7 %collective-permute-start = (f32[1024,64]{1,0:T(8,128)}, f32[1024,64]{1,0:T(8,128)S(1)}, u32[]{:S(2)}, u32[]{:S(2)}) collective-permute-start(f32[1024,64]{1,0:T(8,128)} %get-tuple-element.22), channel_id=1, source_target_pairs={{0,4},{4,8},{8,12},{12,16},{16,20},{20,24},{24,28},{28,32},{32,36}... | collective-permute-start | bytes 786440 | tf_op jit(solution)/shard_map/ppermute | solution.py:253
  50.6 10.6 %collective-permute-start.1 = (f32[1024,64]{1,0:T(8,128)}, f32[1024,64]{1,0:T(8,128)S(1)}, u32[]{:S(2)}, u32[]{:S(2)}) collective-permute-start(f32[1024,64]{1,0:T(8,128)} %get-tuple-element.23), channel_id=1, source_target_pairs={{4,0},{8,4},{12,8},{16,12},{20,16},{24,20},{28,24},{32,28},{36,32}... | collective-permute-start | bytes 786440 | tf_op jit(solution)/shard_map/ppermute | solution.py:254
  59.3 1.9 copy-start.2
  61.2 0.8 copy-start.5
  86.2 10.8 %collective-permute-start.2 = (f32[1024,64]{1,0:T(8,128)}, f32[1024,64]{1,0:T(8,128)S(1)}, u32[]{:S(2)}, u32[]{:S(2)}) collective-permute-start(f32[1024,64]{1,0:T(8,128)} %get-tuple-element.27), channel_id=1, source_target_pairs={{0,4},{4,8},{8,12},{12,16},{16,20},{20,24},{24,28},{28,32},{32,36}... | collective-permute-start | bytes 786440 | tf_op jit(solution)/shard_map/ppermute | solution.py:253
  91.9 8.9 %collective-permute-start.3 = (f32[1024,64]{1,0:T(8,128)}, f32[1024,64]{1,0:T(8,128)S(1)}, u32[]{:S(2)}, u32[]{:S(2)}) collective-permute-start(f32[1024,64]{1,0:T(8,128)} %get-tuple-element.28), channel_id=1, source_target_pairs={{4,0},{8,4},{12,8},{16,12},{20,16},{24,20},{28,24},{32,28},{36,32}... | collective-permute-start | bytes 786440 | tf_op jit(solution)/shard_map/ppermute | solution.py:254
  97.0 3.8 %copy-start.3 = (f32[1024,64]{1,0:T(8,128)}, f32[1024,64]{1,0:T(8,128)S(1)}, u32[]{:S(2)}) copy-start(f32[1024,64]{1,0:T(8,128)S(1)} %collective-permute-done.2.refs_3_) | copy-start | bytes 786436
  100.8 0.8 copy-start.6
  127.6 10.8 %collective-permute-start.4 = (f32[1024,64]{1,0:T(8,128)}, f32[1024,64]{1,0:T(8,128)S(1)}, u32[]{:S(2)}, u32[]{:S(2)}) collective-permute-start(f32[1024,64]{1,0:T(8,128)} %get-tuple-element.30), channel_id=1, source_target_pairs={{0,4},{4,8},{8,12},{12,16},{16,20},{20,24},{24,28},{28,32},{32,36}... | collective-permute-start | bytes 786440 | tf_op jit(solution)/shard_map/ppermute | solution.py:253
  133.4 8.9 %collective-permute-start.5 = (f32[1024,64]{1,0:T(8,128)}, f32[1024,64]{1,0:T(8,128)S(1)}, u32[]{:S(2)}, u32[]{:S(2)}) collective-permute-start(f32[1024,64]{1,0:T(8,128)} %get-tuple-element.31), channel_id=1, source_target_pairs={{4,0},{8,4},{12,8},{16,12},{20,16},{24,20},{28,24},{32,28},{36,32}... | collective-permute-start | bytes 786440 | tf_op jit(solution)/shard_map/ppermute | solution.py:254
  138.3 4.0 %copy-start = (f32[1024,64]{1,0:T(8,128)}, f32[1024,64]{1,0:T(8,128)S(1)}, u32[]{:S(2)}) copy-start(f32[1024,64]{1,0:T(8,128)S(1)} %collective-permute-done.4.refs_3_) | copy-start | bytes 786436
  142.3 0.8 copy-start.1
  168.9 10.8 %collective-permute-start.6 = (f32[1024,64]{1,0:T(8,128)}, f32[1024,64]{1,0:T(8,128)S(1)}, u32[]{:S(2)}, u32[]{:S(2)}) collective-permute-start(f32[1024,64]{1,0:T(8,128)} %get-tuple-element.34), channel_id=1, source_target_pairs={{0,4},{4,8},{8,12},{12,16},{16,20},{20,24},{24,28},{28,32},{32,36}... | collective-permute-start | bytes 786440 | tf_op jit(solution)/shard_map/ppermute | solution.py:253
  174.8 8.9 %collective-permute-start.7 = (f32[1024,64]{1,0:T(8,128)}, f32[1024,64]{1,0:T(8,128)S(1)}, u32[]{:S(2)}, u32[]{:S(2)}) collective-permute-start(f32[1024,64]{1,0:T(8,128)} %get-tuple-element.35), channel_id=1, source_target_pairs={{4,0},{8,4},{12,8},{16,12},{20,16},{24,20},{28,24},{32,28},{36,32}... | collective-permute-start | bytes 786440 | tf_op jit(solution)/shard_map/ppermute | solution.py:254
  179.7 4.0 %copy-start.4 = (f32[1024,64]{1,0:T(8,128)}, f32[1024,64]{1,0:T(8,128)S(1)}, u32[]{:S(2)}) copy-start(f32[1024,64]{1,0:T(8,128)S(1)} %collective-permute-done.6.refs_2_) | copy-start | bytes 786436
  183.7 0.8 copy-start.7
  201.3 24.8 %all-to-all-start = ((bf16[4,3072,64]{1,2,0:T(8,128)(2,1)}), bf16[4,3072,64]{1,2,0:T(8,128)(2,1)S(1)}, u32[]{:S(2)}, u32[]{:S(2)}) async-start(bf16[4,3072,64]{1,2,0:T(8,128)(2,1)} %copy.11), calls=%async_computation | async-start | bytes 3145728 | tf_op jit(solution)/shard_map/all_to_all | solution.py:273
  226.7 3.9 %collective-permute-start.8 = (f32[256,256]{1,0:T(8,128)S(1)}, f32[256,256]{1,0:T(8,128)S(1)}, u32[]{:S(2)}, u32[]{:S(2)}) collective-permute-start(f32[256,256]{1,0:T(8,128)S(1)} %fusion.9), channel_id=1, source_target_pairs={{0,4},{1,5},{2,6},{3,7},{4,0},{5,1},{6,2},{7,3},{8,12},{9,13},{10,... | collective-permute-start | bytes 786440 | tf_op jit(solution)/shard_map/ppermute | solution.py:217
  230.7 8.7 %collective-permute-start.9 = (f32[256,256]{1,0:T(8,128)S(1)}, f32[256,256]{1,0:T(8,128)S(1)}, u32[]{:S(2)}, u32[]{:S(2)}) collective-permute-start(f32[256,256]{1,0:T(8,128)S(1)} %add.53), channel_id=1, source_target_pairs={{0,1},{1,0},{2,3},{3,2},{4,5},{5,4},{6,7},{7,6},{8,9},{9,8},{10,11... | collective-permute-start | bytes 786440 | tf_op jit(solution)/shard_map/ppermute | solution.py:217
  239.4 9.3 %collective-permute-start.10 = (f32[256,256]{1,0:T(8,128)S(1)}, f32[256,256]{1,0:T(8,128)S(1)}, u32[]{:S(2)}, u32[]{:S(2)}) collective-permute-start(f32[256,256]{1,0:T(8,128)S(1)} %add.54), channel_id=1, source_target_pairs={{0,2},{1,3},{2,0},{3,1},{4,6},{5,7},{6,4},{7,5},{8,10},{9,11},{10,... | collective-permute-start | bytes 786440 | tf_op jit(solution)/shard_map/ppermute | solution.py:217
  248.8 7.6 %collective-permute-start.11 = (f32[256,256]{1,0:T(8,128)S(1)}, f32[256,256]{1,0:T(8,128)S(1)}, u32[]{:S(2)}, u32[]{:S(2)}) collective-permute-start(f32[256,256]{1,0:T(8,128)S(1)} %add.55), channel_id=1, source_target_pairs={{0,8},{1,9},{2,10},{3,11},{4,12},{5,13},{6,14},{7,15},{8,0},{9,1},... | collective-permute-start | bytes 786440 | tf_op jit(solution)/shard_map/ppermute | solution.py:217
  256.4 8.0 %collective-permute-start.12 = (f32[256,256]{1,0:T(8,128)S(1)}, f32[256,256]{1,0:T(8,128)S(1)}, u32[]{:S(2)}, u32[]{:S(2)}) collective-permute-start(f32[256,256]{1,0:T(8,128)S(1)} %add.56), channel_id=1, source_target_pairs={{0,16},{1,17},{2,18},{3,19},{4,20},{5,21},{6,22},{7,23},{8,24},{9,... | collective-permute-start | bytes 786440 | tf_op jit(solution)/shard_map/ppermute | solution.py:217
  264.4 8.3 %collective-permute-start.13 = (f32[256,256]{1,0:T(8,128)S(1)}, f32[256,256]{1,0:T(8,128)S(1)}, u32[]{:S(2)}, u32[]{:S(2)}) collective-permute-start(f32[256,256]{1,0:T(8,128)S(1)} %add.57), channel_id=1, source_target_pairs={{0,32},{1,33},{2,34},{3,35},{4,36},{5,37},{6,38},{7,39},{8,40},{9,... | collective-permute-start | bytes 786440 | tf_op jit(solution)/shard_map/ppermute | solution.py:217
  272.8 8.0 %collective-permute-start.14 = (f32[256,256]{1,0:T(8,128)S(1)}, f32[256,256]{1,0:T(8,128)S(1)}, u32[]{:S(2)}, u32[]{:S(2)}) collective-permute-start(f32[256,256]{1,0:T(8,128)S(1)} %add.58), channel_id=1, source_target_pairs={{0,64},{1,65},{2,66},{3,67},{4,68},{5,69},{6,70},{7,71},{8,72},{9,... | collective-permute-start | bytes 786440 | tf_op jit(solution)/shard_map/ppermute | solution.py:217

commit v10 on v9

--- a/solution.py
+++ b/solution.py
@@ -58,7 +58,7 @@
                 work[pl.ds(n, 1), :] += row if alpha == 1.0 else alpha * row
                 return carry
 
-            lax.fori_loop(0, face_half, fix, 0, unroll=8)
+            lax.fori_loop(0, face_half, fix, 0, unroll=16)
         value = work[...]
         if older:
             value = value - older_ref[...].astype(jnp.float32)
@@ -111,7 +111,7 @@
                     faces_out[side][pl.ds(p, 1), :] = local_out[pl.ds(n, 1), :]
                     return carry
 
-                lax.fori_loop(0, face_half, pick, 0, unroll=8)
+                lax.fori_loop(0, face_half, pick, 0, unroll=16)
 
 
 def field_step(faces, scales, window_ops, window_pot, vector=None, local_in=None,

time: 307 us -> 308 us (level)
  no operation moved by 1% of the time
where the time goes in v10:
time: 308 us; the launch traced here: 307 us
  Pallas kernels  128 us (42%)
  waiting for transfers between devices  83.9 us (27%)
  starting transfers between devices  42.6 us (14%)
  local copies, waits for them, and re-layouts  23.3 us (8%)
  blocking collectives  17.2 us (6%)
  matrix products  6.38 us (2%)
  other arithmetic  3.97 us (1%)
    pallas_call x5, Pallas kernels, field_step(): pl.pallas_call(functools.partial(field_kernel, combine, has_older, apply,...  128 us
    ppermute x7, waiting for transfers between devices, doubling_sum(): total = total + lax.ppermute(total, ('dom', 'band'), pairs)  44.8 us
    ppermute x4, starting transfers between devices, exchange(): from_left = lax.ppermute(right_values, 'dom', up)  19 us
    all_to_all x1, blocking collectives, body(): lax.all_to_all(rotated, 'band', split_axis=1, concat_axis=0, tiled=True)  17.2 us
    ppermute x4, waiting for transfers between devices, exchange(): from_left = lax.ppermute(right_values, 'dom', up)  14.3 us
    ppermute x4, waiting for transfers between devices, exchange(): from_right = lax.ppermute(left_values, 'dom', down)  13.6 us
    all_to_all x1, waiting for transfers between devices, body(): lax.all_to_all(current, 'band', split_axis=0, concat_axis=1, tiled=True)  11.1 us
    ppermute x4, starting transfers between devices, exchange(): from_right = lax.ppermute(left_values, 'dom', down)  9.58 us
  transfers between devices with their start and end apart: 16, of which 16 were waited for; matrix products, arithmetic and copies ran while one was open for 3% of the time, Pallas kernels for 0%

profile of v10, /device:TPU:6, one launch (start us, length us, event | category | flops | bytes accessed | tf_op | source)
XLA Modules:
  0.0 307.1 jit_solution(3253800498922447711)
XLA Ops:
  4.7 4.2 %copy.10 = bf16[64,12288]{0,1:T(8,128)(2,1)} copy(bf16[64,12288]{1,0:T(8,128)(2,1)} %param.7) | data formatting | bytes 3145728 | tf_op args[0]
  9.9 38.2 %shard_map.73 = (f32[12288,64]{1,0:T(8,128)}, f32[1024,64]{1,0:T(8,128)}, f32[1024,64]{1,0:T(8,128)}, bf16[32,512,512]{2,1,0:T(8,128)(2,1)}, f32[32,1,512]{2,1,0:T(1,128)}) custom-call(s32[2048]{0:T(1024)} %pad_add_fusion.refs_0_, f32[32]{0:T(128)} %compare_select_fusion.1.refs_1_, bf16[12288,64]{1,0:T(8,128)(2,1)} %bitcast.55, ...), custom_call_target="tpu_custom_call" | custom-call | flops 18253611008 | bytes 26214400 | tf_op jit(solution)/shard_map/pallas_call | solution.py:158
  50.0 3.6 %collective-permute-start.1 = (f32[1024,64]{1,0:T(8,128)}, f32[1024,64]{1,0:T(8,128)S(1)}, u32[]{:S(2)}, u32[]{:S(2)}) collective-permute-start(f32[1024,64]{1,0:T(8,128)} %get-tuple-element.23), channel_id=1, source_target_pairs={{4,0},{8,4},{12,8},{16,12},{20,16},{24,20},{28,24},{32,28},{36,32}... | collective-permute-start | bytes 786440 | tf_op jit(solution)/shard_map/ppermute | solution.py:254
  53.6 5.1 %collective-permute-done.refs_3_ = f32[1024,64]{1,0:T(8,128)S(1)} collective-permute-done((f32[1024,64]{1,0:T(8,128)}, f32[1024,64]{1,0:T(8,128)S(1)}, u32[]{:S(2)}, u32[]{:S(2)}) %collective-permute-start) | collective-permute-done | bytes 262176 | tf_op jit(solution)/shard_map/ppermute | solution.py:253
  61.4 24.4 %shard_map.74 = (bf16[12288,64]{1,0:T(8,128)(2,1)}, f32[12288,64]{1,0:T(8,128)}, f32[1024,64]{1,0:T(8,128)}, f32[1024,64]{1,0:T(8,128)}) custom-call(s32[2048]{0:T(1024)} %pad_add_fusion.refs_0_, f32[32]{0:T(128)} %compare_select_fusion.1.refs_1_, f32[12288,64]{1,0:T(8,128)} %get-tuple-element.21.refs_2_, f32[1024,64]{1,0:T(8,128)} %copy-done.2, ...), custom_call_target="tpu_custom_call" | custom-call | flops 1073741824 | bytes 26214400 | tf_op jit(solution)/shard_map/pallas_call | solution.py:158
  85.9 5.7 %collective-permute-start.2 = (f32[1024,64]{1,0:T(8,128)}, f32[1024,64]{1,0:T(8,128)S(1)}, u32[]{:S(2)}, u32[]{:S(2)}) collective-permute-start(f32[1024,64]{1,0:T(8,128)} %get-tuple-element.27), channel_id=1, source_target_pairs={{0,4},{4,8},{8,12},{12,16},{16,20},{20,24},{24,28},{28,32},{32,36}... | collective-permute-start | bytes 786440 | tf_op jit(solution)/shard_map/ppermute | solution.py:253
  91.5 2.1 collective-permute-start.3
  93.6 3.0 collective-permute-done.2.refs_3_
  96.6 4.0 %collective-permute-done.3.refs_4_ = f32[1024,64]{1,0:T(8,128)S(1)} collective-permute-done((f32[1024,64]{1,0:T(8,128)}, f32[1024,64]{1,0:T(8,128)S(1)}, u32[]{:S(2)}, u32[]{:S(2)}) %collective-permute-start.3) | collective-permute-done | bytes 262176 | tf_op jit(solution)/shard_map/ppermute | solution.py:254
  101.4 25.9 %shard_map.75 = (bf16[12288,64]{1,0:T(8,128)(2,1)}, f32[12288,64]{1,0:T(8,128)}, f32[1024,64]{1,0:T(8,128)}, f32[1024,64]{1,0:T(8,128)}) custom-call(s32[2048]{0:T(1024)} %pad_add_fusion.refs_0_, f32[32]{0:T(128)} %compare_select_fusion.1.refs_1_, f32[12288,64]{1,0:T(8,128)} %get-tuple-element.26.refs_2_, f32[1024,64]{1,0:T(8,128)} %copy-done.3, ...), custom_call_target="tpu_custom_call" | custom-call | flops 1073741824 | bytes 26214400 | tf_op jit(solution)/shard_map/pallas_call | solution.py:158
  127.4 5.6 %collective-permute-start.4 = (f32[1024,64]{1,0:T(8,128)}, f32[1024,64]{1,0:T(8,128)S(1)}, u32[]{:S(2)}, u32[]{:S(2)}) collective-permute-start(f32[1024,64]{1,0:T(8,128)} %get-tuple-element.30), channel_id=1, source_target_pairs={{0,4},{4,8},{8,12},{12,16},{16,20},{20,24},{24,28},{28,32},{32,36}... | collective-permute-start | bytes 786440 | tf_op jit(solution)/shard_map/ppermute | solution.py:253
  133.0 1.9 collective-permute-start.5
  134.9 3.2 %collective-permute-done.4.refs_3_ = f32[1024,64]{1,0:T(8,128)S(1)} collective-permute-done((f32[1024,64]{1,0:T(8,128)}, f32[1024,64]{1,0:T(8,128)S(1)}, u32[]{:S(2)}, u32[]{:S(2)}) %collective-permute-start.4) | collective-permute-done | bytes 262176 | tf_op jit(solution)/shard_map/ppermute | solution.py:253
  138.1 3.8 %collective-permute-done.5.refs_4_ = f32[1024,64]{1,0:T(8,128)S(1)} collective-permute-done((f32[1024,64]{1,0:T(8,128)}, f32[1024,64]{1,0:T(8,128)S(1)}, u32[]{:S(2)}, u32[]{:S(2)}) %collective-permute-start.5) | collective-permute-done | bytes 262176 | tf_op jit(solution)/shard_map/ppermute | solution.py:254
  142.7 25.8 %shard_map.76 = (bf16[12288,64]{1,0:T(8,128)(2,1)}, f32[12288,64]{1,0:T(8,128)}, f32[1024,64]{1,0:T(8,128)}, f32[1024,64]{1,0:T(8,128)}) custom-call(s32[2048]{0:T(1024)} %pad_add_fusion.refs_0_, f32[32]{0:T(128)} %compare_select_fusion.1.refs_1_, f32[12288,64]{1,0:T(8,128)} %get-tuple-element.29.refs_2_, f32[1024,64]{1,0:T(8,128)} %copy-done, ...), custom_call_target="tpu_custom_call" | custom-call | flops 1073741824 | bytes 26214400 | tf_op jit(solution)/shard_map/pallas_call | solution.py:158
  168.5 5.8 %collective-permute-start.6 = (f32[1024,64]{1,0:T(8,128)}, f32[1024,64]{1,0:T(8,128)S(1)}, u32[]{:S(2)}, u32[]{:S(2)}) collective-permute-start(f32[1024,64]{1,0:T(8,128)} %get-tuple-element.34), channel_id=1, source_target_pairs={{0,4},{4,8},{8,12},{12,16},{16,20},{20,24},{24,28},{28,32},{32,36}... | collective-permute-start | bytes 786440 | tf_op jit(solution)/shard_map/ppermute | solution.py:253
  176.3 3.0 collective-permute-done.6.refs_2_
  179.3 4.0 %collective-permute-done.7.refs_3_ = f32[1024,64]{1,0:T(8,128)S(1)} collective-permute-done((f32[1024,64]{1,0:T(8,128)}, f32[1024,64]{1,0:T(8,128)S(1)}, u32[]{:S(2)}, u32[]{:S(2)}) %collective-permute-start.7) | collective-permute-done | bytes 262176 | tf_op jit(solution)/shard_map/ppermute | solution.py:254
  184.1 13.7 %shard_map.77 = bf16[12288,64]{1,0:T(8,128)(2,1)} custom-call(s32[2048]{0:T(1024)} %pad_add_fusion.refs_0_, f32[12288,64]{1,0:T(8,128)} %get-tuple-element.33.refs_1_, f32[1024,64]{1,0:T(8,128)} %copy-done.4, f32[1024,64]{1,0:T(8,128)} %copy-done.7, bf16[12288,64]{1,0:T(8,128)(2,1)} %get-tuple-element.36.refs_4_), custom_call_target="tpu_custom_call" | custom-call | bytes 9437184 | tf_op jit(solution)/shard_map/pallas_call | solution.py:158
  197.8 4.3 %copy.11 = bf16[4,3072,64]{1,2,0:T(8,128)(2,1)} copy(bf16[4,3072,64]{2,1,0:T(8,128)(2,1)} %bitcast.54) | data formatting | bytes 3145728 | tf_op jit(solution)/shard_map/all_to_all | solution.py:273
  202.1 5.3 %all-to-all-start = ((bf16[4,3072,64]{1,2,0:T(8,128)(2,1)}), bf16[4,3072,64]{1,2,0:T(8,128)(2,1)S(1)}, u32[]{:S(2)}, u32[]{:S(2)}) async-start(bf16[4,3072,64]{1,2,0:T(8,128)(2,1)} %copy.11), calls=%async_computation | async-start | bytes 3145728 | tf_op jit(solution)/shard_map/all_to_all | solution.py:273
  207.4 8.3 %scatter_custom_fusion = f32[12288]{0:T(1024)S(1)} fusion(s32[2048]{0:T(1024)S(1)} %bitcast.62, f32[2048]{0:T(1024)S(1)} %add_divide_fusion, f32[]{:T(128)} %constant.17.clone.1), kind=kCustom, calls=%fused_computation.23 | custom fusion | bytes 49156 | tf_op jit(solution)/shard_map/scatter | solution.py:239
  215.7 11.1 %all-to-all-done = bf16[4,3072,64]{1,2,0:T(8,128)(2,1)S(1)} async-done(((bf16[4,3072,64]{1,2,0:T(8,128)(2,1)}), bf16[4,3072,64]{1,2,0:T(8,128)(2,1)S(1)}, u32[]{:S(2)}, u32[]{:S(2)}) %all-to-all-start) | async-done | bytes 1572896 | tf_op jit(solution)/shard_map/all_to_all | solution.py:273
  227.6 2.6 collective-permute-start.8
  232.0 8.0 %collective-permute-done.9 = f32[256,256]{1,0:T(8,128)S(1)} collective-permute-done((f32[256,256]{1,0:T(8,128)S(1)}, f32[256,256]{1,0:T(8,128)S(1)}, u32[]{:S(2)}, u32[]{:S(2)}) %collective-permute-start.9) | collective-permute-done | bytes 262176 | tf_op jit(solution)/shard_map/ppermute | solution.py:217
  241.0 8.3 %collective-permute-done.10 = f32[256,256]{1,0:T(8,128)S(1)} collective-permute-done((f32[256,256]{1,0:T(8,128)S(1)}, f32[256,256]{1,0:T(8,128)S(1)}, u32[]{:S(2)}, u32[]{:S(2)}) %collective-permute-start.10) | collective-permute-done | bytes 262176 | tf_op jit(solution)/shard_map/ppermute | solution.py:217
  249.5 7.5 %collective-permute-done.11 = f32[256,256]{1,0:T(8,128)S(1)} collective-permute-done((f32[256,256]{1,0:T(8,128)S(1)}, f32[256,256]{1,0:T(8,128)S(1)}, u32[]{:S(2)}, u32[]{:S(2)}) %collective-permute-start.11) | collective-permute-done | bytes 262176 | tf_op jit(solution)/shard_map/ppermute | solution.py:217
  257.1 7.9 %collective-permute-done.12 = f32[256,256]{1,0:T(8,128)S(1)} collective-permute-done((f32[256,256]{1,0:T(8,128)S(1)}, f32[256,256]{1,0:T(8,128)S(1)}, u32[]{:S(2)}, u32[]{:S(2)}) %collective-permute-start.12) | collective-permute-done | bytes 262176 | tf_op jit(solution)/shard_map/ppermute | solution.py:217
  266.7 6.7 %collective-permute-done.13 = f32[256,256]{1,0:T(8,128)S(1)} collective-permute-done((f32[256,256]{1,0:T(8,128)S(1)}, f32[256,256]{1,0:T(8,128)S(1)}, u32[]{:S(2)}, u32[]{:S(2)}) %collective-permute-start.13) | collective-permute-done | bytes 262176 | tf_op jit(solution)/shard_map/ppermute | solution.py:217
  273.4 2.7 collective-permute-start.14
  276.1 5.2 %collective-permute-done.14 = f32[256,256]{1,0:T(8,128)S(1)} collective-permute-done((f32[256,256]{1,0:T(8,128)S(1)}, f32[256,256]{1,0:T(8,128)S(1)}, u32[]{:S(2)}, u32[]{:S(2)}) %collective-permute-start.14) | collective-permute-done | bytes 262176 | tf_op jit(solution)/shard_map/ppermute | solution.py:217
  288.6 17.2 %all_to_all.38 = bf16[3072,4,64]{0,2,1:T(8,128)(2,1)S(1)} all-to-all(bf16[3072,4,64]{0,2,1:T(8,128)(2,1)S(1)} %bitcast.57), channel_id=1, replica_groups=mesh['dom'=32,'band'=4] {'band'}, dimensions={1} | all-to-all | bytes 3145728 | tf_op jit(solution)/shard_map/all_to_all | solution.py:287
  (65 shorter events, 27.2 us)
Async XLA Ops:
  4.6 4.2 %copy-start.8 = (f32[32]{0:T(128)S(1)}, f32[32]{0:T(128)}, u32[]{:S(2)}) copy-start(f32[32]{0:T(128)} %param.9) | copy-start | bytes 388
  48.1 10.7 %collective-permute-start = (f32[1024,64]{1,0:T(8,128)}, f32[1024,64]{1,0:T(8,128)S(1)}, u32[]{:S(2)}, u32[]{:S(2)}) collective-permute-start(f32[1024,64]{1,0:T(8,128)} %get-tuple-element.22), channel_id=1, source_target_pairs={{0,4},{4,8},{8,12},{12,16},{16,20},{20,24},{24,28},{28,32},{32,36}... | collective-permute-start | bytes 786440 | tf_op jit(solution)/shard_map/ppermute | solution.py:253
  50.0 10.6 %collective-permute-start.1 = (f32[1024,64]{1,0:T(8,128)}, f32[1024,64]{1,0:T(8,128)S(1)}, u32[]{:S(2)}, u32[]{:S(2)}) collective-permute-start(f32[1024,64]{1,0:T(8,128)} %get-tuple-element.23), channel_id=1, source_target_pairs={{4,0},{8,4},{12,8},{16,12},{20,16},{24,20},{28,24},{32,28},{36,32}... | collective-permute-start | bytes 786440 | tf_op jit(solution)/shard_map/ppermute | solution.py:254
  58.8 1.9 copy-start.2
  60.6 0.8 copy-start.5
  85.9 10.8 %collective-permute-start.2 = (f32[1024,64]{1,0:T(8,128)}, f32[1024,64]{1,0:T(8,128)S(1)}, u32[]{:S(2)}, u32[]{:S(2)}) collective-permute-start(f32[1024,64]{1,0:T(8,128)} %get-tuple-element.27), channel_id=1, source_target_pairs={{0,4},{4,8},{8,12},{12,16},{16,20},{20,24},{24,28},{28,32},{32,36}... | collective-permute-start | bytes 786440 | tf_op jit(solution)/shard_map/ppermute | solution.py:253
  91.5 9.1 %collective-permute-start.3 = (f32[1024,64]{1,0:T(8,128)}, f32[1024,64]{1,0:T(8,128)S(1)}, u32[]{:S(2)}, u32[]{:S(2)}) collective-permute-start(f32[1024,64]{1,0:T(8,128)} %get-tuple-element.28), channel_id=1, source_target_pairs={{4,0},{8,4},{12,8},{16,12},{20,16},{24,20},{28,24},{32,28},{36,32}... | collective-permute-start | bytes 786440 | tf_op jit(solution)/shard_map/ppermute | solution.py:254
  96.6 4.0 %copy-start.3 = (f32[1024,64]{1,0:T(8,128)}, f32[1024,64]{1,0:T(8,128)S(1)}, u32[]{:S(2)}) copy-start(f32[1024,64]{1,0:T(8,128)S(1)} %collective-permute-done.2.refs_3_) | copy-start | bytes 786436
  100.6 0.8 copy-start.6
  127.4 10.8 %collective-permute-start.4 = (f32[1024,64]{1,0:T(8,128)}, f32[1024,64]{1,0:T(8,128)S(1)}, u32[]{:S(2)}, u32[]{:S(2)}) collective-permute-start(f32[1024,64]{1,0:T(8,128)} %get-tuple-element.30), channel_id=1, source_target_pairs={{0,4},{4,8},{8,12},{12,16},{16,20},{20,24},{24,28},{28,32},{32,36}... | collective-permute-start | bytes 786440 | tf_op jit(solution)/shard_map/ppermute | solution.py:253
  133.0 8.9 %collective-permute-start.5 = (f32[1024,64]{1,0:T(8,128)}, f32[1024,64]{1,0:T(8,128)S(1)}, u32[]{:S(2)}, u32[]{:S(2)}) collective-permute-start(f32[1024,64]{1,0:T(8,128)} %get-tuple-element.31), channel_id=1, source_target_pairs={{4,0},{8,4},{12,8},{16,12},{20,16},{24,20},{28,24},{32,28},{36,32}... | collective-permute-start | bytes 786440 | tf_op jit(solution)/shard_map/ppermute | solution.py:254
  138.1 3.8 %copy-start = (f32[1024,64]{1,0:T(8,128)}, f32[1024,64]{1,0:T(8,128)S(1)}, u32[]{:S(2)}) copy-start(f32[1024,64]{1,0:T(8,128)S(1)} %collective-permute-done.4.refs_3_) | copy-start | bytes 786436
  141.9 0.8 copy-start.1
  168.5 10.8 %collective-permute-start.6 = (f32[1024,64]{1,0:T(8,128)}, f32[1024,64]{1,0:T(8,128)S(1)}, u32[]{:S(2)}, u32[]{:S(2)}) collective-permute-start(f32[1024,64]{1,0:T(8,128)} %get-tuple-element.34), channel_id=1, source_target_pairs={{0,4},{4,8},{8,12},{12,16},{16,20},{20,24},{24,28},{28,32},{32,36}... | collective-permute-start | bytes 786440 | tf_op jit(solution)/shard_map/ppermute | solution.py:253
  174.4 8.9 %collective-permute-start.7 = (f32[1024,64]{1,0:T(8,128)}, f32[1024,64]{1,0:T(8,128)S(1)}, u32[]{:S(2)}, u32[]{:S(2)}) collective-permute-start(f32[1024,64]{1,0:T(8,128)} %get-tuple-element.35), channel_id=1, source_target_pairs={{4,0},{8,4},{12,8},{16,12},{20,16},{24,20},{28,24},{32,28},{36,32}... | collective-permute-start | bytes 786440 | tf_op jit(solution)/shard_map/ppermute | solution.py:254
  179.3 4.0 %copy-start.4 = (f32[1024,64]{1,0:T(8,128)}, f32[1024,64]{1,0:T(8,128)S(1)}, u32[]{:S(2)}) copy-start(f32[1024,64]{1,0:T(8,128)S(1)} %collective-permute-done.6.refs_2_) | copy-start | bytes 786436
  183.3 0.8 copy-start.7
  202.1 24.8 %all-to-all-start = ((bf16[4,3072,64]{1,2,0:T(8,128)(2,1)}), bf16[4,3072,64]{1,2,0:T(8,128)(2,1)S(1)}, u32[]{:S(2)}, u32[]{:S(2)}) async-start(bf16[4,3072,64]{1,2,0:T(8,128)(2,1)} %copy.11), calls=%async_computation | async-start | bytes 3145728 | tf_op jit(solution)/shard_map/all_to_all | solution.py:273
  227.6 3.7 %collective-permute-start.8 = (f32[256,256]{1,0:T(8,128)S(1)}, f32[256,256]{1,0:T(8,128)S(1)}, u32[]{:S(2)}, u32[]{:S(2)}) collective-permute-start(f32[256,256]{1,0:T(8,128)S(1)} %fusion.9), channel_id=1, source_target_pairs={{0,4},{1,5},{2,6},{3,7},{4,0},{5,1},{6,2},{7,3},{8,12},{9,13},{10,... | collective-permute-start | bytes 786440 | tf_op jit(solution)/shard_map/ppermute | solution.py:217
  231.3 8.7 %collective-permute-start.9 = (f32[256,256]{1,0:T(8,128)S(1)}, f32[256,256]{1,0:T(8,128)S(1)}, u32[]{:S(2)}, u32[]{:S(2)}) collective-permute-start(f32[256,256]{1,0:T(8,128)S(1)} %add.53), channel_id=1, source_target_pairs={{0,1},{1,0},{2,3},{3,2},{4,5},{5,4},{6,7},{7,6},{8,9},{9,8},{10,11... | collective-permute-start | bytes 786440 | tf_op jit(solution)/shard_map/ppermute | solution.py:217
  240.0 9.3 %collective-permute-start.10 = (f32[256,256]{1,0:T(8,128)S(1)}, f32[256,256]{1,0:T(8,128)S(1)}, u32[]{:S(2)}, u32[]{:S(2)}) collective-permute-start(f32[256,256]{1,0:T(8,128)S(1)} %add.54), channel_id=1, source_target_pairs={{0,2},{1,3},{2,0},{3,1},{4,6},{5,7},{6,4},{7,5},{8,10},{9,11},{10,... | collective-permute-start | bytes 786440 | tf_op jit(solution)/shard_map/ppermute | solution.py:217
  249.4 7.6 %collective-permute-start.11 = (f32[256,256]{1,0:T(8,128)S(1)}, f32[256,256]{1,0:T(8,128)S(1)}, u32[]{:S(2)}, u32[]{:S(2)}) collective-permute-start(f32[256,256]{1,0:T(8,128)S(1)} %add.55), channel_id=1, source_target_pairs={{0,8},{1,9},{2,10},{3,11},{4,12},{5,13},{6,14},{7,15},{8,0},{9,1},... | collective-permute-start | bytes 786440 | tf_op jit(solution)/shard_map/ppermute | solution.py:217
  257.0 8.0 %collective-permute-start.12 = (f32[256,256]{1,0:T(8,128)S(1)}, f32[256,256]{1,0:T(8,128)S(1)}, u32[]{:S(2)}, u32[]{:S(2)}) collective-permute-start(f32[256,256]{1,0:T(8,128)S(1)} %add.56), channel_id=1, source_target_pairs={{0,16},{1,17},{2,18},{3,19},{4,20},{5,21},{6,22},{7,23},{8,24},{9,... | collective-permute-start | bytes 786440 | tf_op jit(solution)/shard_map/ppermute | solution.py:217
  265.0 8.3 %collective-permute-start.13 = (f32[256,256]{1,0:T(8,128)S(1)}, f32[256,256]{1,0:T(8,128)S(1)}, u32[]{:S(2)}, u32[]{:S(2)}) collective-permute-start(f32[256,256]{1,0:T(8,128)S(1)} %add.57), channel_id=1, source_target_pairs={{0,32},{1,33},{2,34},{3,35},{4,36},{5,37},{6,38},{7,39},{8,40},{9,... | collective-permute-start | bytes 786440 | tf_op jit(solution)/shard_map/ppermute | solution.py:217
  273.4 8.0 %collective-permute-start.14 = (f32[256,256]{1,0:T(8,128)S(1)}, f32[256,256]{1,0:T(8,128)S(1)}, u32[]{:S(2)}, u32[]{:S(2)}) collective-permute-start(f32[256,256]{1,0:T(8,128)S(1)} %add.58), channel_id=1, source_target_pairs={{0,64},{1,65},{2,66},{3,67},{4,68},{5,69},{6,70},{7,71},{8,72},{9,... | collective-permute-start | bytes 786440 | tf_op jit(solution)/shard_map/ppermute | solution.py:217

commit v11 on v9

--- a/solution.py
+++ b/solution.py
@@ -195,12 +195,15 @@
     identity = jnp.eye(gram_matrix.shape[0], dtype=jnp.float32)
     frobenius = jnp.sqrt(jnp.sum(gram_matrix * gram_matrix))
     scaled = gram_matrix / frobenius
-    inverse_root = identity
-    for repeat in range(NS_ITERS):
+    factor = 1.5 * identity - 0.5 * scaled
+    scaled = jnp.dot(scaled, factor, precision=lax.Precision.HIGHEST)
+    inverse_root = factor
+    for repeat in range(1, NS_ITERS):
         factor = 1.5 * identity - 0.5 * jnp.dot(
             inverse_root, scaled, precision=lax.Precision.HIGHEST
         )
-        scaled = jnp.dot(scaled, factor, precision=lax.Precision.HIGHEST)
+        if repeat < NS_ITERS - 1:
+            scaled = jnp.dot(scaled, factor, precision=lax.Precision.HIGHEST)
         inverse_root = jnp.dot(factor, inverse_root, precision=lax.Precision.HIGHEST)
     return inverse_root.astype(jnp.bfloat16)
 

time: 307 us -> 307 us (level)
  no operation moved by 1% of the time
where the time goes in v11:
time: 307 us; the launch traced here: 306 us
  Pallas kernels  127 us (41%)
  waiting for transfers between devices  83.8 us (27%)
  starting transfers between devices  43.1 us (14%)
  local copies, waits for them, and re-layouts  23.1 us (8%)
  blocking collectives  17.3 us (6%)
  matrix products  5.9 us (2%)
  other arithmetic  3.97 us (1%)
    pallas_call x5, Pallas kernels, field_step(): pl.pallas_call(functools.partial(field_kernel, combine, has_older, apply,...  127 us
    ppermute x7, waiting for transfers between devices, doubling_sum(): total = total + lax.ppermute(total, ('dom', 'band'), pairs)  44.7 us
    ppermute x4, starting transfers between devices, exchange(): from_left = lax.ppermute(right_values, 'dom', up)  19.2 us
    all_to_all x1, blocking collectives, body(): lax.all_to_all(rotated, 'band', split_axis=1, concat_axis=0, tiled=True)  17.3 us
    ppermute x4, waiting for transfers between devices, exchange(): from_left = lax.ppermute(right_values, 'dom', up)  14.2 us
    ppermute x4, waiting for transfers between devices, exchange(): from_right = lax.ppermute(left_values, 'dom', down)  13.6 us
    all_to_all x1, waiting for transfers between devices, body(): lax.all_to_all(current, 'band', split_axis=0, concat_axis=1, tiled=True)  11.3 us
    ppermute x4, starting transfers between devices, exchange(): from_right = lax.ppermute(left_values, 'dom', down)  9.58 us
  transfers between devices with their start and end apart: 16, of which 16 were waited for; matrix products, arithmetic and copies ran while one was open for 3% of the time, Pallas kernels for 0%

profile of v11, /device:TPU:6, one launch (start us, length us, event | category | flops | bytes accessed | tf_op | source)
XLA Modules:
  0.0 306.0 jit_solution(13999947929212851587)
XLA Ops:
  4.7 4.2 %copy.10 = bf16[64,12288]{0,1:T(8,128)(2,1)} copy(bf16[64,12288]{1,0:T(8,128)(2,1)} %param.7) | data formatting | bytes 3145728 | tf_op args[0]
  9.9 38.7 %shard_map.73 = (f32[12288,64]{1,0:T(8,128)}, f32[1024,64]{1,0:T(8,128)}, f32[1024,64]{1,0:T(8,128)}, bf16[32,512,512]{2,1,0:T(8,128)(2,1)}, f32[32,1,512]{2,1,0:T(1,128)}) custom-call(s32[2048]{0:T(1024)} %pad_add_fusion.refs_0_, f32[32]{0:T(128)} %compare_select_fusion.1.refs_1_, bf16[12288,64]{1,0:T(8,128)(2,1)} %bitcast.51, ...), custom_call_target="tpu_custom_call" | custom-call | flops 18253611008 | bytes 26214400 | tf_op jit(solution)/shard_map/pallas_call | solution.py:158
  50.6 3.6 %collective-permute-start.1 = (f32[1024,64]{1,0:T(8,128)}, f32[1024,64]{1,0:T(8,128)S(1)}, u32[]{:S(2)}, u32[]{:S(2)}) collective-permute-start(f32[1024,64]{1,0:T(8,128)} %get-tuple-element.23), channel_id=1, source_target_pairs={{4,0},{8,4},{12,8},{16,12},{20,16},{24,20},{28,24},{32,28},{36,32}... | collective-permute-start | bytes 786440 | tf_op jit(solution)/shard_map/ppermute | solution.py:257
  54.2 5.1 %collective-permute-done.refs_3_ = f32[1024,64]{1,0:T(8,128)S(1)} collective-permute-done((f32[1024,64]{1,0:T(8,128)}, f32[1024,64]{1,0:T(8,128)S(1)}, u32[]{:S(2)}, u32[]{:S(2)}) %collective-permute-start) | collective-permute-done | bytes 262176 | tf_op jit(solution)/shard_map/ppermute | solution.py:256
  62.0 24.2 %shard_map.74 = (bf16[12288,64]{1,0:T(8,128)(2,1)}, f32[12288,64]{1,0:T(8,128)}, f32[1024,64]{1,0:T(8,128)}, f32[1024,64]{1,0:T(8,128)}) custom-call(s32[2048]{0:T(1024)} %pad_add_fusion.refs_0_, f32[32]{0:T(128)} %compare_select_fusion.1.refs_1_, f32[12288,64]{1,0:T(8,128)} %get-tuple-element.21.refs_2_, f32[1024,64]{1,0:T(8,128)} %copy-done.2, ...), custom_call_target="tpu_custom_call" | custom-call | flops 1073741824 | bytes 26214400 | tf_op jit(solution)/shard_map/pallas_call | solution.py:158
  86.2 5.7 %collective-permute-start.2 = (f32[1024,64]{1,0:T(8,128)}, f32[1024,64]{1,0:T(8,128)S(1)}, u32[]{:S(2)}, u32[]{:S(2)}) collective-permute-start(f32[1024,64]{1,0:T(8,128)} %get-tuple-element.27), channel_id=1, source_target_pairs={{0,4},{4,8},{8,12},{12,16},{16,20},{20,24},{24,28},{28,32},{32,36}... | collective-permute-start | bytes 786440 | tf_op jit(solution)/shard_map/ppermute | solution.py:256
  91.9 2.1 collective-permute-start.3
  94.0 3.0 collective-permute-done.2.refs_3_
  97.0 3.8 %collective-permute-done.3.refs_4_ = f32[1024,64]{1,0:T(8,128)S(1)} collective-permute-done((f32[1024,64]{1,0:T(8,128)}, f32[1024,64]{1,0:T(8,128)S(1)}, u32[]{:S(2)}, u32[]{:S(2)}) %collective-permute-start.3) | collective-permute-done | bytes 262176 | tf_op jit(solution)/shard_map/ppermute | solution.py:257
  101.6 25.9 %shard_map.75 = (bf16[12288,64]{1,0:T(8,128)(2,1)}, f32[12288,64]{1,0:T(8,128)}, f32[1024,64]{1,0:T(8,128)}, f32[1024,64]{1,0:T(8,128)}) custom-call(s32[2048]{0:T(1024)} %pad_add_fusion.refs_0_, f32[32]{0:T(128)} %compare_select_fusion.1.refs_1_, f32[12288,64]{1,0:T(8,128)} %get-tuple-element.26.refs_2_, f32[1024,64]{1,0:T(8,128)} %copy-done.3, ...), custom_call_target="tpu_custom_call" | custom-call | flops 1073741824 | bytes 26214400 | tf_op jit(solution)/shard_map/pallas_call | solution.py:158
  127.6 5.8 %collective-permute-start.4 = (f32[1024,64]{1,0:T(8,128)}, f32[1024,64]{1,0:T(8,128)S(1)}, u32[]{:S(2)}, u32[]{:S(2)}) collective-permute-start(f32[1024,64]{1,0:T(8,128)} %get-tuple-element.30), channel_id=1, source_target_pairs={{0,4},{4,8},{8,12},{12,16},{16,20},{20,24},{24,28},{28,32},{32,36}... | collective-permute-start | bytes 786440 | tf_op jit(solution)/shard_map/ppermute | solution.py:256
  133.4 1.9 collective-permute-start.5
  135.3 3.0 collective-permute-done.4.refs_3_
  138.3 4.0 %collective-permute-done.5.refs_4_ = f32[1024,64]{1,0:T(8,128)S(1)} collective-permute-done((f32[1024,64]{1,0:T(8,128)}, f32[1024,64]{1,0:T(8,128)S(1)}, u32[]{:S(2)}, u32[]{:S(2)}) %collective-permute-start.5) | collective-permute-done | bytes 262176 | tf_op jit(solution)/shard_map/ppermute | solution.py:257
  143.1 25.9 %shard_map.76 = (bf16[12288,64]{1,0:T(8,128)(2,1)}, f32[12288,64]{1,0:T(8,128)}, f32[1024,64]{1,0:T(8,128)}, f32[1024,64]{1,0:T(8,128)}) custom-call(s32[2048]{0:T(1024)} %pad_add_fusion.refs_0_, f32[32]{0:T(128)} %compare_select_fusion.1.refs_1_, f32[12288,64]{1,0:T(8,128)} %get-tuple-element.29.refs_2_, f32[1024,64]{1,0:T(8,128)} %copy-done, ...), custom_call_target="tpu_custom_call" | custom-call | flops 1073741824 | bytes 26214400 | tf_op jit(solution)/shard_map/pallas_call | solution.py:158
  168.9 5.8 %collective-permute-start.6 = (f32[1024,64]{1,0:T(8,128)}, f32[1024,64]{1,0:T(8,128)S(1)}, u32[]{:S(2)}, u32[]{:S(2)}) collective-permute-start(f32[1024,64]{1,0:T(8,128)} %get-tuple-element.34), channel_id=1, source_target_pairs={{0,4},{4,8},{8,12},{12,16},{16,20},{20,24},{24,28},{28,32},{32,36}... | collective-permute-start | bytes 786440 | tf_op jit(solution)/shard_map/ppermute | solution.py:256
  176.7 3.0 collective-permute-done.6.refs_2_
  179.7 4.0 %collective-permute-done.7.refs_3_ = f32[1024,64]{1,0:T(8,128)S(1)} collective-permute-done((f32[1024,64]{1,0:T(8,128)}, f32[1024,64]{1,0:T(8,128)S(1)}, u32[]{:S(2)}, u32[]{:S(2)}) %collective-permute-start.7) | collective-permute-done | bytes 262176 | tf_op jit(solution)/shard_map/ppermute | solution.py:257
  184.5 12.5 %shard_map.77 = bf16[12288,64]{1,0:T(8,128)(2,1)} custom-call(s32[2048]{0:T(1024)} %pad_add_fusion.refs_0_, f32[12288,64]{1,0:T(8,128)} %get-tuple-element.33.refs_1_, f32[1024,64]{1,0:T(8,128)} %copy-done.4, f32[1024,64]{1,0:T(8,128)} %copy-done.7, bf16[12288,64]{1,0:T(8,128)(2,1)} %get-tuple-element.36.refs_4_), custom_call_target="tpu_custom_call" | custom-call | bytes 9437184 | tf_op jit(solution)/shard_map/pallas_call | solution.py:158
  197.0 4.3 %copy.11 = bf16[4,3072,64]{1,2,0:T(8,128)(2,1)} copy(bf16[4,3072,64]{2,1,0:T(8,128)(2,1)} %bitcast.50) | data formatting | bytes 3145728 | tf_op jit(solution)/shard_map/all_to_all | solution.py:276
  201.3 5.3 %all-to-all-start = ((bf16[4,3072,64]{1,2,0:T(8,128)(2,1)}), bf16[4,3072,64]{1,2,0:T(8,128)(2,1)S(1)}, u32[]{:S(2)}, u32[]{:S(2)}) async-start(bf16[4,3072,64]{1,2,0:T(8,128)(2,1)} %copy.11), calls=%async_computation | async-start | bytes 3145728 | tf_op jit(solution)/shard_map/all_to_all | solution.py:276
  206.6 8.1 %scatter_custom_fusion = f32[12288]{0:T(1024)S(1)} fusion(s32[2048]{0:T(1024)S(1)} %bitcast.58, f32[2048]{0:T(1024)S(1)} %add_divide_fusion, f32[]{:T(128)} %constant.17.clone.1), kind=kCustom, calls=%fused_computation.31 | custom fusion | bytes 49156 | tf_op jit(solution)/shard_map/scatter | solution.py:242
  214.7 11.3 %all-to-all-done = bf16[4,3072,64]{1,2,0:T(8,128)(2,1)S(1)} async-done(((bf16[4,3072,64]{1,2,0:T(8,128)(2,1)}), bf16[4,3072,64]{1,2,0:T(8,128)(2,1)S(1)}, u32[]{:S(2)}, u32[]{:S(2)}) %all-to-all-start) | async-done | bytes 1572896 | tf_op jit(solution)/shard_map/all_to_all | solution.py:276
  226.8 2.8 collective-permute-start.8
  231.4 8.0 %collective-permute-done.9 = f32[256,256]{1,0:T(8,128)S(1)} collective-permute-done((f32[256,256]{1,0:T(8,128)S(1)}, f32[256,256]{1,0:T(8,128)S(1)}, u32[]{:S(2)}, u32[]{:S(2)}) %collective-permute-start.9) | collective-permute-done | bytes 262176 | tf_op jit(solution)/shard_map/ppermute | solution.py:220
  240.4 8.3 %collective-permute-done.10 = f32[256,256]{1,0:T(8,128)S(1)} collective-permute-done((f32[256,256]{1,0:T(8,128)S(1)}, f32[256,256]{1,0:T(8,128)S(1)}, u32[]{:S(2)}, u32[]{:S(2)}) %collective-permute-start.10) | collective-permute-done | bytes 262176 | tf_op jit(solution)/shard_map/ppermute | solution.py:220
  248.9 7.5 %collective-permute-done.11 = f32[256,256]{1,0:T(8,128)S(1)} collective-permute-done((f32[256,256]{1,0:T(8,128)S(1)}, f32[256,256]{1,0:T(8,128)S(1)}, u32[]{:S(2)}, u32[]{:S(2)}) %collective-permute-start.11) | collective-permute-done | bytes 262176 | tf_op jit(solution)/shard_map/ppermute | solution.py:220
  256.5 7.9 %collective-permute-done.12 = f32[256,256]{1,0:T(8,128)S(1)} collective-permute-done((f32[256,256]{1,0:T(8,128)S(1)}, f32[256,256]{1,0:T(8,128)S(1)}, u32[]{:S(2)}, u32[]{:S(2)}) %collective-permute-start.12) | collective-permute-done | bytes 262176 | tf_op jit(solution)/shard_map/ppermute | solution.py:220
  266.1 6.7 %collective-permute-done.13 = f32[256,256]{1,0:T(8,128)S(1)} collective-permute-done((f32[256,256]{1,0:T(8,128)S(1)}, f32[256,256]{1,0:T(8,128)S(1)}, u32[]{:S(2)}, u32[]{:S(2)}) %collective-permute-start.13) | collective-permute-done | bytes 262176 | tf_op jit(solution)/shard_map/ppermute | solution.py:220
  272.8 2.8 collective-permute-start.14
  275.6 5.2 %collective-permute-done.14 = f32[256,256]{1,0:T(8,128)S(1)} collective-permute-done((f32[256,256]{1,0:T(8,128)S(1)}, f32[256,256]{1,0:T(8,128)S(1)}, u32[]{:S(2)}, u32[]{:S(2)}) %collective-permute-start.14) | collective-permute-done | bytes 262176 | tf_op jit(solution)/shard_map/ppermute | solution.py:220
  287.5 17.3 %all_to_all.38 = bf16[3072,4,64]{0,2,1:T(8,128)(2,1)S(1)} all-to-all(bf16[3072,4,64]{0,2,1:T(8,128)(2,1)S(1)} %bitcast.53), channel_id=1, replica_groups=mesh['dom'=32,'band'=4] {'band'}, dimensions={1} | all-to-all | bytes 3145728 | tf_op jit(solution)/shard_map/all_to_all | solution.py:290
  (63 shorter events, 26.8 us)
Async XLA Ops:
  4.6 4.2 %copy-start.8 = (f32[32]{0:T(128)S(1)}, f32[32]{0:T(128)}, u32[]{:S(2)}) copy-start(f32[32]{0:T(128)} %param.9) | copy-start | bytes 388
  48.6 10.7 %collective-permute-start = (f32[1024,64]{1,0:T(8,128)}, f32[1024,64]{1,0:T(8,128)S(1)}, u32[]{:S(2)}, u32[]{:S(2)}) collective-permute-start(f32[1024,64]{1,0:T(8,128)} %get-tuple-element.22), channel_id=1, source_target_pairs={{0,4},{4,8},{8,12},{12,16},{16,20},{20,24},{24,28},{28,32},{32,36}... | collective-permute-start | bytes 786440 | tf_op jit(solution)/shard_map/ppermute | solution.py:256
  50.6 10.6 %collective-permute-start.1 = (f32[1024,64]{1,0:T(8,128)}, f32[1024,64]{1,0:T(8,128)S(1)}, u32[]{:S(2)}, u32[]{:S(2)}) collective-permute-start(f32[1024,64]{1,0:T(8,128)} %get-tuple-element.23), channel_id=1, source_target_pairs={{4,0},{8,4},{12,8},{16,12},{20,16},{24,20},{28,24},{32,28},{36,32}... | collective-permute-start | bytes 786440 | tf_op jit(solution)/shard_map/ppermute | solution.py:257
  59.3 1.9 copy-start.2
  61.2 0.8 copy-start.5
  86.2 10.8 %collective-permute-start.2 = (f32[1024,64]{1,0:T(8,128)}, f32[1024,64]{1,0:T(8,128)S(1)}, u32[]{:S(2)}, u32[]{:S(2)}) collective-permute-start(f32[1024,64]{1,0:T(8,128)} %get-tuple-element.27), channel_id=1, source_target_pairs={{0,4},{4,8},{8,12},{12,16},{16,20},{20,24},{24,28},{28,32},{32,36}... | collective-permute-start | bytes 786440 | tf_op jit(solution)/shard_map/ppermute | solution.py:256
  91.9 8.9 %collective-permute-start.3 = (f32[1024,64]{1,0:T(8,128)}, f32[1024,64]{1,0:T(8,128)S(1)}, u32[]{:S(2)}, u32[]{:S(2)}) collective-permute-start(f32[1024,64]{1,0:T(8,128)} %get-tuple-element.28), channel_id=1, source_target_pairs={{4,0},{8,4},{12,8},{16,12},{20,16},{24,20},{28,24},{32,28},{36,32}... | collective-permute-start | bytes 786440 | tf_op jit(solution)/shard_map/ppermute | solution.py:257
  97.0 3.8 %copy-start.3 = (f32[1024,64]{1,0:T(8,128)}, f32[1024,64]{1,0:T(8,128)S(1)}, u32[]{:S(2)}) copy-start(f32[1024,64]{1,0:T(8,128)S(1)} %collective-permute-done.2.refs_3_) | copy-start | bytes 786436
  100.8 0.8 copy-start.6
  127.6 10.8 %collective-permute-start.4 = (f32[1024,64]{1,0:T(8,128)}, f32[1024,64]{1,0:T(8,128)S(1)}, u32[]{:S(2)}, u32[]{:S(2)}) collective-permute-start(f32[1024,64]{1,0:T(8,128)} %get-tuple-element.30), channel_id=1, source_target_pairs={{0,4},{4,8},{8,12},{12,16},{16,20},{20,24},{24,28},{28,32},{32,36}... | collective-permute-start | bytes 786440 | tf_op jit(solution)/shard_map/ppermute | solution.py:256
  133.4 8.9 %collective-permute-start.5 = (f32[1024,64]{1,0:T(8,128)}, f32[1024,64]{1,0:T(8,128)S(1)}, u32[]{:S(2)}, u32[]{:S(2)}) collective-permute-start(f32[1024,64]{1,0:T(8,128)} %get-tuple-element.31), channel_id=1, source_target_pairs={{4,0},{8,4},{12,8},{16,12},{20,16},{24,20},{28,24},{32,28},{36,32}... | collective-permute-start | bytes 786440 | tf_op jit(solution)/shard_map/ppermute | solution.py:257
  138.3 4.0 %copy-start = (f32[1024,64]{1,0:T(8,128)}, f32[1024,64]{1,0:T(8,128)S(1)}, u32[]{:S(2)}) copy-start(f32[1024,64]{1,0:T(8,128)S(1)} %collective-permute-done.4.refs_3_) | copy-start | bytes 786436
  142.3 0.8 copy-start.1
  168.9 10.8 %collective-permute-start.6 = (f32[1024,64]{1,0:T(8,128)}, f32[1024,64]{1,0:T(8,128)S(1)}, u32[]{:S(2)}, u32[]{:S(2)}) collective-permute-start(f32[1024,64]{1,0:T(8,128)} %get-tuple-element.34), channel_id=1, source_target_pairs={{0,4},{4,8},{8,12},{12,16},{16,20},{20,24},{24,28},{28,32},{32,36}... | collective-permute-start | bytes 786440 | tf_op jit(solution)/shard_map/ppermute | solution.py:256
  174.8 8.9 %collective-permute-start.7 = (f32[1024,64]{1,0:T(8,128)}, f32[1024,64]{1,0:T(8,128)S(1)}, u32[]{:S(2)}, u32[]{:S(2)}) collective-permute-start(f32[1024,64]{1,0:T(8,128)} %get-tuple-element.35), channel_id=1, source_target_pairs={{4,0},{8,4},{12,8},{16,12},{20,16},{24,20},{28,24},{32,28},{36,32}... | collective-permute-start | bytes 786440 | tf_op jit(solution)/shard_map/ppermute | solution.py:257
  179.7 4.0 %copy-start.4 = (f32[1024,64]{1,0:T(8,128)}, f32[1024,64]{1,0:T(8,128)S(1)}, u32[]{:S(2)}) copy-start(f32[1024,64]{1,0:T(8,128)S(1)} %collective-permute-done.6.refs_2_) | copy-start | bytes 786436
  183.7 0.8 copy-start.7
  201.3 24.8 %all-to-all-start = ((bf16[4,3072,64]{1,2,0:T(8,128)(2,1)}), bf16[4,3072,64]{1,2,0:T(8,128)(2,1)S(1)}, u32[]{:S(2)}, u32[]{:S(2)}) async-start(bf16[4,3072,64]{1,2,0:T(8,128)(2,1)} %copy.11), calls=%async_computation | async-start | bytes 3145728 | tf_op jit(solution)/shard_map/all_to_all | solution.py:276
  226.8 3.9 %collective-permute-start.8 = (f32[256,256]{1,0:T(8,128)S(1)}, f32[256,256]{1,0:T(8,128)S(1)}, u32[]{:S(2)}, u32[]{:S(2)}) collective-permute-start(f32[256,256]{1,0:T(8,128)S(1)} %fusion.26), channel_id=1, source_target_pairs={{0,4},{1,5},{2,6},{3,7},{4,0},{5,1},{6,2},{7,3},{8,12},{9,13},{10,... | collective-permute-start | bytes 786440 | tf_op jit(solution)/shard_map/ppermute | solution.py:220
  230.7 8.7 %collective-permute-start.9 = (f32[256,256]{1,0:T(8,128)S(1)}, f32[256,256]{1,0:T(8,128)S(1)}, u32[]{:S(2)}, u32[]{:S(2)}) collective-permute-start(f32[256,256]{1,0:T(8,128)S(1)} %add.53), channel_id=1, source_target_pairs={{0,1},{1,0},{2,3},{3,2},{4,5},{5,4},{6,7},{7,6},{8,9},{9,8},{10,11... | collective-permute-start | bytes 786440 | tf_op jit(solution)/shard_map/ppermute | solution.py:220
  239.4 9.3 %collective-permute-start.10 = (f32[256,256]{1,0:T(8,128)S(1)}, f32[256,256]{1,0:T(8,128)S(1)}, u32[]{:S(2)}, u32[]{:S(2)}) collective-permute-start(f32[256,256]{1,0:T(8,128)S(1)} %add.54), channel_id=1, source_target_pairs={{0,2},{1,3},{2,0},{3,1},{4,6},{5,7},{6,4},{7,5},{8,10},{9,11},{10,... | collective-permute-start | bytes 786440 | tf_op jit(solution)/shard_map/ppermute | solution.py:220
  248.8 7.6 %collective-permute-start.11 = (f32[256,256]{1,0:T(8,128)S(1)}, f32[256,256]{1,0:T(8,128)S(1)}, u32[]{:S(2)}, u32[]{:S(2)}) collective-permute-start(f32[256,256]{1,0:T(8,128)S(1)} %add.55), channel_id=1, source_target_pairs={{0,8},{1,9},{2,10},{3,11},{4,12},{5,13},{6,14},{7,15},{8,0},{9,1},... | collective-permute-start | bytes 786440 | tf_op jit(solution)/shard_map/ppermute | solution.py:220
  256.4 8.0 %collective-permute-start.12 = (f32[256,256]{1,0:T(8,128)S(1)}, f32[256,256]{1,0:T(8,128)S(1)}, u32[]{:S(2)}, u32[]{:S(2)}) collective-permute-start(f32[256,256]{1,0:T(8,128)S(1)} %add.56), channel_id=1, source_target_pairs={{0,16},{1,17},{2,18},{3,19},{4,20},{5,21},{6,22},{7,23},{8,24},{9,... | collective-permute-start | bytes 786440 | tf_op jit(solution)/shard_map/ppermute | solution.py:220
  264.4 8.3 %collective-permute-start.13 = (f32[256,256]{1,0:T(8,128)S(1)}, f32[256,256]{1,0:T(8,128)S(1)}, u32[]{:S(2)}, u32[]{:S(2)}) collective-permute-start(f32[256,256]{1,0:T(8,128)S(1)} %add.57), channel_id=1, source_target_pairs={{0,32},{1,33},{2,34},{3,35},{4,36},{5,37},{6,38},{7,39},{8,40},{9,... | collective-permute-start | bytes 786440 | tf_op jit(solution)/shard_map/ppermute | solution.py:220
  272.8 8.0 %collective-permute-start.14 = (f32[256,256]{1,0:T(8,128)S(1)}, f32[256,256]{1,0:T(8,128)S(1)}, u32[]{:S(2)}, u32[]{:S(2)}) collective-permute-start(f32[256,256]{1,0:T(8,128)S(1)} %add.58), channel_id=1, source_target_pairs={{0,64},{1,65},{2,66},{3,67},{4,68},{5,69},{6,70},{7,71},{8,72},{9,... | collective-permute-start | bytes 786440 | tf_op jit(solution)/shard_map/ppermute | solution.py:220
